TPU v7x, 256 devices: a whole 4x4x8 slice. The times are simulated.
256 devices in a mesh: dp: 32 (over x, z_hi, core), expert: 8 (over z_lo, y).
Axes of the slice: x: 4, y: 4, z: 8 (z_hi: 4, z_lo: 2; z = z_hi * 2 + z_lo), core: 2. Of those that a mesh axis runs over, the one named last changes fastest.
Arguments:
- tokens: bfloat16 [65536, 2560], P(('dp', 'expert')), may hold values from -24 to 24
- routes: int32 [65536, 1], P(('dp', 'expert')), may hold values from 0 to 7; in each aligned block of 256 rows (0 to 255, 256 to 511, ...) at most 40 rows name the same one
- gate_levels: int32 [65536, 1], P(('dp', 'expert')), may hold values from 1 to 64
- w_gate: bfloat16 [8, 2560, 768], P('expert', 'dp'), may hold values from -0.125 to 0.125
- w_up: bfloat16 [8, 2560, 768], P('expert', 'dp'), may hold values from -0.125 to 0.125
- w_down: bfloat16 [8, 2560, 768], P('expert', 'dp'), may hold values from -0.21875 to 0.21875
- grad_out: bfloat16 [65536, 2560], P(('dp', 'expert')), may hold values from -24 to 24
Outputs:
- moe_out: bfloat16 [65536, 2560], P(('dp', 'expert'))
- grad_tokens: bfloat16 [65536, 2560], P(('dp', 'expert'))
- grad_gate: float32 [8, 2560, 768], P('expert', 'dp')
- grad_up: float32 [8, 2560, 768], P('expert', 'dp')
- grad_down: float32 [8, 2560, 768], P('expert', 'dp')
Inputs may be any that keep to these rules, and one draw needn't show every extreme that they name: `routes`: among the rows of one device, no expert is named by more than 40 tokens, a bound that some block reaches.
All inputs are finite; a program needn't handle non-finite values.
Results may differ from a plain program's by a relative error of at most 0.019.
Values may be sent and summed in bfloat16 or wider, within the bound.
No kernel may reach another device: no remote copies, remote signals or barrier semaphores. Data moves between devices by JAX's collectives and lax.ppermute only.
A program may use at most 128 MiB of HBM per device.

v0:
```python
import jax
import jax.numpy as jnp
from jax import lax
from jax.sharding import PartitionSpec as P

TOP = 1


def contract_last(matrix_a, matrix_b):
    return lax.dot_general(
        matrix_a, matrix_b, (((1,), (1,)), ((), ())), preferred_element_type=jnp.float32
    )


def contract_first(matrix_a, matrix_b):
    return lax.dot_general(
        matrix_a, matrix_b, (((0,), (0,)), ((), ())), preferred_element_type=jnp.float32
    )


def shards(tokens, routes, gate_levels, w_gate, w_up, w_down, grad_out):
    experts = lax.axis_size("expert")
    tok_rows = tokens.shape[0]
    model_width = tokens.shape[1]
    capacity = min(tok_rows, tok_rows * TOP * 5 // (4 * experts))
    slot_count = experts * capacity
    expert_of = routes[:, 0]
    onehot = (expert_of[:, None] == jnp.arange(experts, dtype=jnp.int32)[None, :]).astype(jnp.int32)
    earlier = jnp.cumsum(onehot, axis=0) - onehot
    slot_rank = jnp.sum(earlier * onehot, axis=1)
    slot_index = expert_of * capacity + slot_rank
    source_row = (
        jnp.zeros((slot_count,), jnp.int32)
        .at[slot_index]
        .set(jnp.arange(tok_rows, dtype=jnp.int32))
    )
    filled = (
        jnp.zeros((slot_count, 1), jnp.bfloat16)
        .at[slot_index, 0]
        .set(jnp.ones((tok_rows,), jnp.bfloat16))
    )
    gate_weight = gate_levels.astype(jnp.float32) / 64.0

    def pack_rows(values):
        return (jnp.take(values, source_row, axis=0) * filled).reshape(
            experts, capacity, model_width
        )

    trio_full = (
        lax.all_gather(w_gate, "dp", axis=1, tiled=True),
        lax.all_gather(w_up, "dp", axis=1, tiled=True),
        lax.all_gather(w_down, "dp", axis=1, tiled=True),
    )
    gate_full = trio_full[0][0]
    up_full = trio_full[1][0]
    down_full = trio_full[2][0]
    received = lax.all_to_all(
        pack_rows(tokens), "expert", split_axis=0, concat_axis=0, tiled=True
    ).reshape(slot_count, model_width)
    act_gate = jnp.dot(received, gate_full, preferred_element_type=jnp.float32)
    act_up = jnp.dot(received, up_full, preferred_element_type=jnp.float32)
    sigmoid_gate = jax.nn.sigmoid(act_gate)
    silu_gate = act_gate * sigmoid_gate
    hidden = (silu_gate * act_up).astype(jnp.bfloat16)
    expert_out = (
        contract_last(hidden, down_full)
        .astype(jnp.bfloat16)
        .reshape(experts, capacity, model_width)
    )
    returned = lax.all_to_all(
        expert_out, "expert", split_axis=0, concat_axis=0, tiled=True
    ).reshape(slot_count, model_width)
    moe_out = (gate_weight * jnp.take(returned, slot_index, axis=0).astype(jnp.float32)).astype(
        jnp.bfloat16
    )
    out_grad = (gate_weight * grad_out.astype(jnp.float32)).astype(jnp.bfloat16)
    grad_rows = lax.all_to_all(
        pack_rows(out_grad), "expert", split_axis=0, concat_axis=0, tiled=True
    ).reshape(slot_count, model_width)
    hidden_grad = jnp.dot(grad_rows, down_full, preferred_element_type=jnp.float32)
    gate_delta = (
        hidden_grad * act_up * sigmoid_gate * (1.0 + act_gate * (1.0 - sigmoid_gate))
    ).astype(jnp.bfloat16)
    up_delta = (hidden_grad * silu_gate).astype(jnp.bfloat16)
    token_grad = (contract_last(gate_delta, gate_full) + contract_last(up_delta, up_full)).astype(
        jnp.bfloat16
    )
    arrived = lax.all_to_all(
        token_grad.reshape(experts, capacity, model_width),
        "expert",
        split_axis=0,
        concat_axis=0,
        tiled=True,
    )
    grad_tokens = jnp.take(arrived.reshape(slot_count, model_width), slot_index, axis=0)
    part_gate = contract_first(received, gate_delta).astype(jnp.bfloat16)
    part_up = contract_first(received, up_delta).astype(jnp.bfloat16)
    part_down = contract_first(grad_rows, hidden).astype(jnp.bfloat16)
    shares = (
        lax.psum_scatter(part_gate, "dp", scatter_dimension=0, tiled=True).astype(jnp.float32),
        lax.psum_scatter(part_up, "dp", scatter_dimension=0, tiled=True).astype(jnp.float32),
        lax.psum_scatter(part_down, "dp", scatter_dimension=0, tiled=True).astype(jnp.float32),
    )
    grad_gate = shares[0]
    grad_up = shares[1]
    grad_down = shares[2]
    return (moe_out, grad_tokens, grad_gate[None], grad_up[None], grad_down[None])


def solution(mesh):
    in_specs = (
        P(("dp", "expert"), None),
        P(("dp", "expert"), None),
        P(("dp", "expert"), None),
        P("expert", "dp", None),
        P("expert", "dp", None),
        P("expert", "dp", None),
        P(("dp", "expert"), None),
    )
    out_specs = (
        P(("dp", "expert"), None),
        P(("dp", "expert"), None),
        P("expert", "dp", None),
        P("expert", "dp", None),
        P("expert", "dp", None),
    )
    return jax.shard_map(shards, mesh=mesh, in_specs=in_specs, out_specs=out_specs, check_vma=False)
```

profile of v0, /device:TPU:1, one launch (start us, length us, event | category | flops | bytes accessed | tf_op | source)
XLA Modules:
  0.0 517.5 jit_solution(14345882446878057339)
XLA Ops:
  14.5 1.6 multiply_convert_fusion
  16.1 3.2 gather_fusion.2
  19.3 3.2 gather_fusion
  22.4 2.2 scatter_custom_fusion.1
  24.6 3.0 select_multiply_fusion
  27.6 33.8 %all_to_all.20 = bf16[8,40,2560]{2,1,0:T(8,128)(2,1)} all-to-all(bf16[8,40,2560]{2,1,0:T(8,128)(2,1)S(1)} %bitcast.60), channel_id=1, replica_groups=mesh['dp'=32,'expert'=8] {'expert'}, dimensions={0} | all-to-all | bytes 3276800 | tf_op jit(solution)/shard_map/all_to_all | solution.py:57
  61.4 3.6 all-to-all-start.2
  65.3 12.2 %all-gather.4.cloned.1.call-done = bf16[1,2560,768]{2,1,0:T(8,128)(2,1)} async-done(((bf16[1,80,768]{2,1,0:T(8,128)(2,1)}), bf16[1,2560,768]{2,1,0:T(8,128)(2,1)}) %all-gather.4.cloned.1.call-update) | async-done | bytes 3932176 | tf_op jit(solution)/shard_map/all_gather | solution.py:50
  77.5 5.0 fusion.9
  82.5 55.5 %all-gather.6.cloned.1.call-done = bf16[1,2560,768]{2,1,0:T(8,128)(2,1)} async-done(((bf16[1,80,768]{2,1,0:T(8,128)(2,1)}), bf16[1,2560,768]{2,1,0:T(8,128)(2,1)}) %all-gather.6.cloned.1.call-update) | async-done | bytes 3932176 | tf_op jit(solution)/shard_map/all_gather | solution.py:51
  138.0 5.0 fusion.5
  143.0 55.1 %all-gather.8.cloned.1.call-done = bf16[1,2560,768]{2,1,0:T(8,128)(2,1)} async-done(((bf16[1,80,768]{2,1,0:T(8,128)(2,1)}), bf16[1,2560,768]{2,1,0:T(8,128)(2,1)}) %all-gather.8.cloned.1.call-update) | async-done | bytes 3932176 | tf_op jit(solution)/shard_map/all_gather | solution.py:52
  198.1 5.4 %multiply_convert_fusion.2 = (bf16[320,768]{1,0:T(8,128)(2,1)}, bf16[320,768]{1,0:T(8,128)(2,1)S(1)}, bf16[320,768]{1,0:T(8,128)(2,1)}) fusion(f32[320,768]{1,0:T(8,128)} %fusion.9, f32[320,768]{1,0:T(8,128)} %fusion.5, bf16[320,2560]{1,0:T(8,128)(2,1)S(1)} %bitcast.61, bf16[1,2560,768]{2,1,0:T(8,128)(2,1)} %all-gather.8.cloned.1.call-done), kind=kOutput, calls=%fused_computation.27 | convolution fusion | flops 1261977600 | bytes 9011200 | tf_op jit(solution)/shard_map/dot_general | solution.py:80
  203.5 4.2 convolution_convert_fusion.2
  209.2 5.2 %convolution_convert_fusion.1 = bf16[2560,768]{1,0:T(8,128)(2,1)} fusion(bf16[320,2560]{1,0:T(8,128)(2,1)S(1)} %bitcast.66, bf16[320,768]{1,0:T(8,128)(2,1)} %get-tuple-element.9), kind=kOutput, calls=%fused_computation.7 | convolution fusion | flops 1260257280 | bytes 6062080 | tf_op jit(solution)/shard_map/dot_general | solution.py:16
  215.4 4.8 convolution_convert_fusion.3
  220.2 4.6 all-to-all-start.1
  225.1 5.7 %convolution_convert_fusion = bf16[2560,768]{1,0:T(8,128)(2,1)} fusion(bf16[320,2560]{1,0:T(8,128)(2,1)} %bitcast.62, bf16[320,768]{1,0:T(8,128)(2,1)} %get-tuple-element.11), kind=kOutput, calls=%fused_computation.6 | convolution fusion | flops 1260257280 | bytes 6062080 | tf_op jit(solution)/shard_map/dot_general | solution.py:16
  230.9 3.8 fusion.7
  234.8 2.7 fusion
  237.4 8.7 %all-to-all-done.1 = bf16[8,40,2560]{2,1,0:T(8,128)(2,1)S(1)} async-done(((bf16[8,40,2560]{2,1,0:T(8,128)(2,1)}), bf16[8,40,2560]{2,1,0:T(8,128)(2,1)S(1)}, u32[]{:S(2)}, u32[]{:S(2)}) %all-to-all-start.1) | async-done | bytes 1638432 | tf_op jit(solution)/shard_map/all_to_all | solution.py:70
  246.2 4.4 all-to-all-start.3
  250.6 2.5 gather_fusion.1
  253.1 32.5 %all-to-all-done.3 = bf16[8,40,2560]{2,1,0:T(8,128)(2,1)} async-done(((bf16[8,40,2560]{2,1,0:T(8,128)(2,1)}), bf16[8,40,2560]{2,1,0:T(8,128)(2,1)}, u32[]{:S(2)}, u32[]{:S(2)}) %all-to-all-start.3) | async-done | bytes 1638432 | tf_op jit(solution)/shard_map/all_to_all | solution.py:88
  285.7 4.4 gather_fusion.3
  291.9 1.4 multiply_convert_fusion.1
  293.3 15.5 %reduce-scatter.4.cloned.1.call-done = bf16[80,768]{1,0:T(8,128)(2,1)} async-done(((bf16[2560,768]{1,0:T(8,128)(2,1)}), bf16[80,768]{1,0:T(8,128)(2,1)}) %reduce-scatter.4.cloned.1.call-update) | async-done | bytes 122896 | tf_op jit(solution)/shard_map/reduce_scatter | solution.py:100
  308.8 1.6 bitcast_convert_fusion.2
  310.4 98.8 %reduce-scatter.6.cloned.1.call-done = bf16[80,768]{1,0:T(8,128)(2,1)} async-done(((bf16[2560,768]{1,0:T(8,128)(2,1)}), bf16[80,768]{1,0:T(8,128)(2,1)}) %reduce-scatter.6.cloned.1.call-update) | async-done | bytes 122896 | tf_op jit(solution)/shard_map/reduce_scatter | solution.py:101
  409.2 1.6 bitcast_convert_fusion.1
  410.8 98.3 %reduce-scatter.8.cloned.1.call-done = bf16[80,768]{1,0:T(8,128)(2,1)} async-done(((bf16[2560,768]{1,0:T(8,128)(2,1)}), bf16[80,768]{1,0:T(8,128)(2,1)}) %reduce-scatter.8.cloned.1.call-update) | async-done | bytes 122896 | tf_op jit(solution)/shard_map/reduce_scatter | solution.py:102
  509.1 1.6 bitcast_convert_fusion
  (50 shorter events, 12.0 us)
Async XLA Ops:
  7.2 12.1 %copy-start = (bf16[256,2560]{1,0:T(8,128)(2,1)S(1)}, bf16[256,2560]{1,0:T(8,128)(2,1)}, u32[]{:S(2)}) copy-start(bf16[256,2560]{1,0:T(8,128)(2,1)} %param.11) | copy-start | bytes 3932164
  7.2 70.3 %all-gather.4.cloned.1.call-start = ((), (), s32[]{:S(2)}) async-start(), calls=%async_computation.7 | async-start | bytes 4055040 | tf_op jit(solution)/shard_map/all_gather | solution.py:50
  7.9 130.1 %all-gather.6.cloned.1.call-start = ((), (), s32[]{:S(2)}) async-start(), calls=%async_computation.8 | async-start | bytes 4055040 | tf_op jit(solution)/shard_map/all_gather | solution.py:51
  8.7 189.4 %all-gather.8.cloned.1.call-start = ((), (), s32[]{:S(2)}) async-start(), calls=%async_computation.9 | async-start | bytes 4055040 | tf_op jit(solution)/shard_map/all_gather | solution.py:52
  19.3 5.4 %copy-start.1 = (bf16[320,2560]{1,0:T(8,128)(2,1)S(1)}, bf16[320,2560]{1,0:T(8,128)(2,1)}, u32[]{:S(2)}) copy-start(bf16[320,2560]{1,0:T(8,128)(2,1)} %gather_fusion.2) | copy-start | bytes 4915204
  61.4 81.5 %all-to-all-start.2 = ((bf16[8,40,2560]{2,1,0:T(8,128)(2,1)}), bf16[8,40,2560]{2,1,0:T(8,128)(2,1)S(1)}, u32[]{:S(2)}, u32[]{:S(2)}) async-start(bf16[8,40,2560]{2,1,0:T(8,128)(2,1)} %bitcast.14), calls=%async_computation.2 | async-start | bytes 3276800 | tf_op jit(solution)/shard_map/all_to_all | solution.py:77
  65.0 243.8 %reduce-scatter.4.cloned.1.call-start = ((), (), s32[]{:S(2)}) async-start(), calls=%async_computation.10 | async-start | bytes 4055040 | tf_op jit(solution)/shard_map/reduce_scatter | solution.py:100
  143.0 60.5 %copy-start.3 = (bf16[8,40,2560]{2,1,0:T(8,128)(2,1)}, bf16[8,40,2560]{2,1,0:T(8,128)(2,1)S(1)}, u32[]{:S(2)}) copy-start(bf16[8,40,2560]{2,1,0:T(8,128)(2,1)S(1)} %all-to-all-done.2) | copy-start | bytes 4915204
  198.1 5.4 %copy-start.4 = (bf16[8,40,2560]{2,1,0:T(8,128)(2,1)S(1)}, bf16[8,40,2560]{2,1,0:T(8,128)(2,1)}, u32[]{:S(2)}) copy-start(bf16[8,40,2560]{2,1,0:T(8,128)(2,1)} %all_to_all.20) | copy-start | bytes 4915204
  207.7 1.4 copy-start.5
  207.8 201.4 %reduce-scatter.6.cloned.1.call-start = ((), (), s32[]{:S(2)}) async-start(), calls=%async_computation.11 | async-start | bytes 4055040 | tf_op jit(solution)/shard_map/reduce_scatter | solution.py:101
  214.4 1.0 copy-start.9
  220.2 25.9 %all-to-all-start.1 = ((bf16[8,40,2560]{2,1,0:T(8,128)(2,1)}), bf16[8,40,2560]{2,1,0:T(8,128)(2,1)S(1)}, u32[]{:S(2)}, u32[]{:S(2)}) async-start(bf16[8,40,2560]{2,1,0:T(8,128)(2,1)} %bitcast.67), calls=%async_computation.1 | async-start | bytes 3276800 | tf_op jit(solution)/shard_map/all_to_all | solution.py:70
  224.9 284.2 %reduce-scatter.8.cloned.1.call-start = ((), (), s32[]{:S(2)}) async-start(), calls=%async_computation.12 | async-start | bytes 4055040 | tf_op jit(solution)/shard_map/reduce_scatter | solution.py:102
  230.9 3.9 copy-start.7
  230.9 3.9 copy-start.8
  246.2 4.4 copy-start.6
  246.2 39.5 %all-to-all-start.3 = ((bf16[8,40,2560]{2,1,0:T(8,128)(2,1)}), bf16[8,40,2560]{2,1,0:T(8,128)(2,1)}, u32[]{:S(2)}, u32[]{:S(2)}) async-start(bf16[8,40,2560]{2,1,0:T(8,128)(2,1)} %bitcast.68), calls=%async_computation.3 | async-start | bytes 3276800 | tf_op jit(solution)/shard_map/all_to_all | solution.py:88
  290.1 1.8 copy-start.2
Sparse Core Ops, SparseCore 0:
  10.6 66.8 all-gather.3
  80.0 57.9 all-gather.5
  140.5 57.4 all-gather.7
  207.9 100.8 reduce-scatter.3
  312.6 96.4 reduce-scatter.5
  413.0 96.0 reduce-scatter.7
where the time goes:
time: 519 us; the launch traced here: 518 us
  waiting for transfers between devices  379 us (73%)
  matrix products  41.9 us (8%)
  blocking collectives  33.8 us (7%)
  local copies, waits for them, and re-layouts  19.9 us (4%)
  other arithmetic  15.6 us (3%)
  between operations  14.3 us (3%)
  starting transfers between devices  13.3 us (3%)
    reduce_scatter x1, waiting for transfers between devices, shards(): lax.psum_scatter(part_up, 'dp', scatter_dimension=0, tiled=True)  98.8 us
    reduce_scatter x1, waiting for transfers between devices, shards(): lax.psum_scatter(part_down, 'dp', scatter_dimension=0, tiled=True)  98.3 us
    all_gather x1, waiting for transfers between devices, shards(): lax.all_gather(w_up, 'dp', axis=1, tiled=True)  55.5 us
    all_gather x1, waiting for transfers between devices, shards(): lax.all_gather(w_down, 'dp', axis=1, tiled=True)  55.1 us
    all_to_all x1, blocking collectives, shards(): lax.all_to_all(pack_rows(tokens), 'expert', split_axis=0, concat_axis=0,...  33.8 us
    all_to_all x1, waiting for transfers between devices, shards(): lax.all_to_all(token_grad.reshape(experts, capacity, model_width), 'exper...  32.5 us
    reduce_scatter x1, waiting for transfers between devices, shards(): lax.psum_scatter(part_gate, 'dp', scatter_dimension=0, tiled=True)  15.5 us
    dot_general x3, matrix products, contract_first(): lax.dot_general(matrix_a, matrix_b, (((0,), (0,)), ((), ())), preferred_e...  15.1 us
  transfers between devices with their start and end apart: 9, of which 8 were waited for; matrix products, arithmetic and copies ran while one was open for 12% of the time, Pallas kernels for 0%

commit v1 on v0

--- a/solution.py
+++ b/solution.py
@@ -1,9 +1,12 @@
 import jax
 import jax.numpy as jnp
 from jax import lax
+from jax.sharding import Mesh
 from jax.sharding import PartitionSpec as P
 
 TOP = 1
+CHIPS = ("x", "zh")
+DP = ("x", "zh", "core")
 
 
 def contract_last(matrix_a, matrix_b):
@@ -16,6 +19,29 @@
     return lax.dot_general(
         matrix_a, matrix_b, (((0,), (0,)), ((), ())), preferred_element_type=jnp.float32
     )
+
+
+def swap_cores(value):
+    return lax.ppermute(value, "core", perm=[(0, 1), (1, 0)])
+
+
+def gather_weight(weight):
+    own = lax.all_to_all(weight, "core", split_axis=1, concat_axis=0, tiled=True)
+    own = lax.all_gather(own, CHIPS, axis=0, tiled=True)
+    other = swap_cores(own)
+    return jnp.concatenate([own, other], axis=1)
+
+
+def scatter_grad(part):
+    half = part.shape[1] // 2
+    rounded = part.astype(jnp.bfloat16)
+    arrived = swap_cores(rounded[:, half:])
+    pair_sum = (rounded[:, :half].astype(jnp.float32) + arrived.astype(jnp.float32)).astype(
+        jnp.bfloat16
+    )
+    chip_sum = lax.psum_scatter(pair_sum, CHIPS, scatter_dimension=0, tiled=True)
+    block = lax.all_to_all(chip_sum, "core", split_axis=0, concat_axis=1, tiled=True)
+    return block.astype(jnp.float32)
 
 
 def shards(tokens, routes, gate_levels, w_gate, w_up, w_down, grad_out):
@@ -46,14 +72,9 @@
             experts, capacity, model_width
         )
 
-    trio_full = (
-        lax.all_gather(w_gate, "dp", axis=1, tiled=True),
-        lax.all_gather(w_up, "dp", axis=1, tiled=True),
-        lax.all_gather(w_down, "dp", axis=1, tiled=True),
-    )
-    gate_full = trio_full[0][0]
-    up_full = trio_full[1][0]
-    down_full = trio_full[2][0]
+    gate_full = gather_weight(w_gate[0])
+    up_full = gather_weight(w_up[0])
+    down_full = gather_weight(w_down[0])
     received = lax.all_to_all(
         pack_rows(tokens), "expert", split_axis=0, concat_axis=0, tiled=True
     ).reshape(slot_count, model_width)
@@ -93,35 +114,20 @@
         tiled=True,
     )
     grad_tokens = jnp.take(arrived.reshape(slot_count, model_width), slot_index, axis=0)
-    part_gate = contract_first(received, gate_delta).astype(jnp.bfloat16)
-    part_up = contract_first(received, up_delta).astype(jnp.bfloat16)
-    part_down = contract_first(grad_rows, hidden).astype(jnp.bfloat16)
-    shares = (
-        lax.psum_scatter(part_gate, "dp", scatter_dimension=0, tiled=True).astype(jnp.float32),
-        lax.psum_scatter(part_up, "dp", scatter_dimension=0, tiled=True).astype(jnp.float32),
-        lax.psum_scatter(part_down, "dp", scatter_dimension=0, tiled=True).astype(jnp.float32),
-    )
-    grad_gate = shares[0]
-    grad_up = shares[1]
-    grad_down = shares[2]
+    grad_down = scatter_grad(contract_first(grad_rows, hidden))
+    grad_gate = scatter_grad(contract_first(received, gate_delta))
+    grad_up = scatter_grad(contract_first(received, up_delta))
     return (moe_out, grad_tokens, grad_gate[None], grad_up[None], grad_down[None])
 
 
 def solution(mesh):
-    in_specs = (
-        P(("dp", "expert"), None),
-        P(("dp", "expert"), None),
-        P(("dp", "expert"), None),
-        P("expert", "dp", None),
-        P("expert", "dp", None),
-        P("expert", "dp", None),
-        P(("dp", "expert"), None),
-    )
-    out_specs = (
-        P(("dp", "expert"), None),
-        P(("dp", "expert"), None),
-        P("expert", "dp", None),
-        P("expert", "dp", None),
-        P("expert", "dp", None),
-    )
-    return jax.shard_map(shards, mesh=mesh, in_specs=in_specs, out_specs=out_specs, check_vma=False)
+    dp_size, expert_size = mesh.devices.shape
+    chips = dp_size // 2
+    x_size = 4 if chips % 4 == 0 else 1
+    grid = mesh.devices.reshape(x_size, chips // x_size, 2, expert_size)
+    fine = Mesh(grid, DP + ("expert",))
+    rows = P(DP + ("expert",), None)
+    weights = P("expert", DP, None)
+    in_specs = (rows, rows, rows, weights, weights, weights, rows)
+    out_specs = (rows, rows, weights, weights, weights)
+    return jax.shard_map(shards, mesh=fine, in_specs=in_specs, out_specs=out_specs, check_vma=False)

time: 519 us -> 518 us (level)
  waiting for transfers between devices: 379 us -> 353 us
  local copies, waits for them, and re-layouts: 19.9 us -> 36.8 us
  starting transfers between devices: 13.3 us -> 25.7 us
  matrix products: 41.9 us -> 34.2 us
    reduce_scatter x3, waiting for transfers between devices: 213 us -> 171 us  [scatter_grad(): lax.psum_scatter(pair_sum, CHIPS, scatter_dimension=0, tiled=True)]
    all_gather x3, waiting for transfers between devices: 123 us -> 145 us  [gather_weight(): own = lax.all_gather(own, CHIPS, axis=0, tiled=True)]
    all_to_all x1, waiting for transfers between devices: 32.5 us -> 14.6 us  [shards(): lax.all_to_all(token_grad.reshape(experts, capacity, model_width), 'exper...]
    concatenate x0 -> x3, local copies, waits for them, and re-layouts: none -> 8.47 us  [gather_weight(): return jnp.concatenate([own, other], axis=1)]
    ppermute x0 -> x6, starting transfers between devices: none -> 7.99 us  [swap_cores(): return lax.ppermute(value, 'core', perm=[(0, 1), (1, 0)])]
    convert_element_type x0 -> x6, other arithmetic: none -> 7.78 us  [the longest x3 7.73 us: scatter_grad(): (rounded[:, :half].astype(jnp.float32) + arrived.astype(jnp.float32)).ast...]
    ppermute x0 -> x6, waiting for transfers between devices: none -> 7.21 us  [swap_cores(): return lax.ppermute(value, 'core', perm=[(0, 1), (1, 0)])]
    all_to_all x1, waiting for transfers between devices: 8.73 us -> 15.6 us  [shards(): lax.all_to_all(expert_out, 'expert', split_axis=0, concat_axis=0, tiled=T...]
  transfers between devices with their start and end apart: 9 -> 16, of which waited for: 8 -> 10; matrix products, arithmetic and copies ran while one was open for 12% -> 13% of each run, Pallas kernels for 0% -> 0%
where the time goes in v1:
time: 518 us; the launch traced here: 517 us
  waiting for transfers between devices  353 us (68%)
  local copies, waits for them, and re-layouts  36.8 us (7%)
  blocking collectives  36.2 us (7%)
  matrix products  34.2 us (7%)
  starting transfers between devices  25.7 us (5%)
  other arithmetic  16.4 us (3%)
  between operations  14.6 us (3%)
    reduce_scatter x3, waiting for transfers between devices, scatter_grad(): lax.psum_scatter(pair_sum, CHIPS, scatter_dimension=0, tiled=True)  171 us
    all_gather x3, waiting for transfers between devices, gather_weight(): own = lax.all_gather(own, CHIPS, axis=0, tiled=True)  145 us
    all_to_all x3, blocking collectives, scatter_grad(): lax.all_to_all(chip_sum, 'core', split_axis=0, concat_axis=1, tiled=True)  19.7 us
    all_to_all x3, blocking collectives, gather_weight(): lax.all_to_all(weight, 'core', split_axis=1, concat_axis=0, tiled=True)  16.5 us
    all_to_all x1, waiting for transfers between devices, shards(): lax.all_to_all(expert_out, 'expert', split_axis=0, concat_axis=0, tiled=T...  15.6 us
    all_to_all x1, waiting for transfers between devices, shards(): lax.all_to_all(token_grad.reshape(experts, capacity, model_width), 'exper...  14.6 us
    dot_general x3, matrix products, contract_last(): lax.dot_general(matrix_a, matrix_b, (((1,), (1,)), ((), ())), preferred_e...  11.4 us
    dot_general x3, matrix products, contract_first(): lax.dot_general(matrix_a, matrix_b, (((0,), (0,)), ((), ())), preferred_e...  11.4 us
  transfers between devices with their start and end apart: 16, of which 10 were waited for; matrix products, arithmetic and copies ran while one was open for 13% of the time, Pallas kernels for 0%

profile of v1, /device:TPU:1, one launch (start us, length us, event | category | flops | bytes accessed | tf_op | source)
XLA Modules:
  0.0 516.7 jit_solution(15889433307063467944)
XLA Ops:
  8.3 7.4 %all_to_all.116 = bf16[80,2,384]{2,0,1:T(8,128)(2,1)} all-to-all(bf16[80,2,384]{2,0,1:T(8,128)(2,1)S(1)} %copy.26), channel_id=1, replica_groups=mesh['x'=4,'zh'=4,'core'=2,'expert'=8] {'core'}, dimensions={1} | all-to-all | bytes 245760 | tf_op jit(solution)/shard_map/all_to_all | solution.py:29
  16.8 4.5 all_to_all.117
  22.3 4.5 all_to_all.118
  31.0 3.2 gather_fusion.2
  34.1 3.2 gather_fusion
  39.5 3.5 select_multiply_fusion
  43.0 4.3 all-to-all-start.5
  47.3 35.1 %all-gather.8.cloned.1.call-done = bf16[2560,384]{1,0:T(8,128)(2,1)} async-done(((bf16[160,384]{1,0:T(8,128)(2,1)}), bf16[2560,384]{1,0:T(8,128)(2,1)}) %all-gather.8.cloned.1.call-update) | async-done | bytes 1966096 | tf_op jit(solution)/shard_map/all_gather | solution.py:30
  82.9 4.4 all-to-all-start
  87.4 53.1 %all-gather.6.cloned.1.call-done = bf16[2560,384]{1,0:T(8,128)(2,1)} async-done(((bf16[160,384]{1,0:T(8,128)(2,1)}), bf16[2560,384]{1,0:T(8,128)(2,1)}) %all-gather.6.cloned.1.call-update) | async-done | bytes 1966096 | tf_op jit(solution)/shard_map/all_gather | solution.py:30
  142.9 56.5 %all-gather.4.cloned.1.call-done = bf16[2560,384]{1,0:T(8,128)(2,1)} async-done(((bf16[160,384]{1,0:T(8,128)(2,1)}), bf16[2560,384]{1,0:T(8,128)(2,1)}) %all-gather.4.cloned.1.call-update) | async-done | bytes 1966096 | tf_op jit(solution)/shard_map/all_gather | solution.py:30
  207.8 4.6 constant_dynamic-update-slice_fusion.2
  215.3 4.2 fusion.9
  221.4 4.4 multiply_convert_fusion.3
  225.9 4.0 convolution_convert_fusion.2
  231.5 3.6 collective-permute-done.3
  237.1 3.7 convolution_convert_fusion.1
  241.7 3.6 collective-permute-done.4
  247.1 4.8 convolution_convert_fusion.3
  252.0 4.7 all-to-all-start.4
  256.7 3.7 convolution_convert_fusion
  264.4 3.9 fusion.11
  271.0 15.6 %all-to-all-done.4 = bf16[8,40,2560]{2,1,0:T(8,128)(2,1)S(1)} async-done(((bf16[8,40,2560]{2,1,0:T(8,128)(2,1)}), bf16[8,40,2560]{2,1,0:T(8,128)(2,1)S(1)}, u32[]{:S(2)}, u32[]{:S(2)}) %all-to-all-start.4) | async-done | bytes 1638432 | tf_op jit(solution)/shard_map/all_to_all | solution.py:91
  286.6 3.9 all-to-all-start.6
  290.6 4.0 add_convert_fusion
  297.1 14.6 %all-to-all-done.6 = bf16[8,40,2560]{2,1,0:T(8,128)(2,1)S(1)} async-done(((bf16[8,40,2560]{2,1,0:T(8,128)(2,1)}), bf16[8,40,2560]{2,1,0:T(8,128)(2,1)S(1)}, u32[]{:S(2)}, u32[]{:S(2)}) %all-to-all-start.6) | async-done | bytes 1638432 | tf_op jit(solution)/shard_map/all_to_all | solution.py:109
  316.4 7.0 %reduce-scatter.4.cloned.1.call-done = bf16[160,384]{1,0:T(8,128)(2,1)} async-done(((bf16[2560,384]{1,0:T(8,128)(2,1)}), bf16[160,384]{1,0:T(8,128)(2,1)}) %reduce-scatter.4.cloned.1.call-update) | async-done | bytes 122896 | tf_op jit(solution)/shard_map/reduce_scatter | solution.py:42
  323.4 6.3 %all_to_all.119 = bf16[2,80,384]{2,1,0:T(8,128)(2,1)S(1)} all-to-all(bf16[2,80,384]{2,1,0:T(8,128)(2,1)} %bitcast.63), channel_id=1, replica_groups=mesh['x'=4,'zh'=4,'core'=2,'expert'=8] {'core'}, dimensions={0} | all-to-all | bytes 245760 | tf_op jit(solution)/shard_map/all_to_all | solution.py:43
  330.7 82.2 %reduce-scatter.6.cloned.1.call-done = bf16[160,384]{1,0:T(8,128)(2,1)} async-done(((bf16[2560,384]{1,0:T(8,128)(2,1)}), bf16[160,384]{1,0:T(8,128)(2,1)}) %reduce-scatter.6.cloned.1.call-update) | async-done | bytes 122896 | tf_op jit(solution)/shard_map/reduce_scatter | solution.py:42
  412.9 6.6 %all_to_all.120 = bf16[2,80,384]{2,1,0:T(8,128)(2,1)S(1)} all-to-all(bf16[2,80,384]{2,1,0:T(8,128)(2,1)} %bitcast.64), channel_id=1, replica_groups=mesh['x'=4,'zh'=4,'core'=2,'expert'=8] {'core'}, dimensions={0} | all-to-all | bytes 245760 | tf_op jit(solution)/shard_map/all_to_all | solution.py:43
  420.6 81.3 %reduce-scatter.8.cloned.1.call-done = bf16[160,384]{1,0:T(8,128)(2,1)} async-done(((bf16[2560,384]{1,0:T(8,128)(2,1)}), bf16[160,384]{1,0:T(8,128)(2,1)}) %reduce-scatter.8.cloned.1.call-update) | async-done | bytes 122896 | tf_op jit(solution)/shard_map/reduce_scatter | solution.py:42
  501.9 6.9 %all_to_all.121 = bf16[2,80,384]{2,1,0:T(8,128)(2,1)S(1)} all-to-all(bf16[2,80,384]{2,1,0:T(8,128)(2,1)} %bitcast.65), channel_id=1, replica_groups=mesh['x'=4,'zh'=4,'core'=2,'expert'=8] {'core'}, dimensions={0} | all-to-all | bytes 245760 | tf_op jit(solution)/shard_map/all_to_all | solution.py:43
  (109 shorter events, 48.7 us)
Async XLA Ops:
  7.2 27.0 %copy-start = (bf16[256,2560]{1,0:T(8,128)(2,1)S(1)}, bf16[256,2560]{1,0:T(8,128)(2,1)}, u32[]{:S(2)}) copy-start(bf16[256,2560]{1,0:T(8,128)(2,1)} %param.11) | copy-start | bytes 3932164
  7.2 19.7 %copy-start.12 = (s32[256,1]{0,1:T(1,128)S(1)}, s32[256,1]{0,1:T(1,128)}, u32[]{:S(2)}) copy-start(s32[256,1]{0,1:T(1,128)} %param.12) | copy-start | bytes 3076
  7.2 22.1 %copy-start.13 = (s32[256,1]{0,1:T(1,128)S(1)}, s32[256,1]{0,1:T(1,128)}, u32[]{:S(2)}) copy-start(s32[256,1]{0,1:T(1,128)} %param.13) | copy-start | bytes 3076
  7.2 75.2 %all-gather.8.cloned.1.call-start = ((), (), s32[]{:S(2)}) async-start(), calls=%async_computation.15 | async-start | bytes 2088960 | tf_op jit(solution)/shard_map/all_gather | solution.py:30
  15.8 124.8 %all-gather.6.cloned.1.call-start = ((), (), s32[]{:S(2)}) async-start(), calls=%async_computation.14 | async-start | bytes 2088960 | tf_op jit(solution)/shard_map/all_gather | solution.py:30
  21.3 178.1 %all-gather.4.cloned.1.call-start = ((), (), s32[]{:S(2)}) async-start(), calls=%async_computation.13 | async-start | bytes 2088960 | tf_op jit(solution)/shard_map/all_gather | solution.py:30
  34.1 5.3 %copy-start.2 = (bf16[320,2560]{1,0:T(8,128)(2,1)S(1)}, bf16[320,2560]{1,0:T(8,128)(2,1)}, u32[]{:S(2)}) copy-start(bf16[320,2560]{1,0:T(8,128)(2,1)} %gather_fusion.2) | copy-start | bytes 4915204
  43.0 39.9 %all-to-all-start.5 = ((bf16[8,40,2560]{2,1,0:T(8,128)(2,1)}), bf16[8,40,2560]{2,1,0:T(8,128)(2,1)}, u32[]{:S(2)}, u32[]{:S(2)}) async-start(bf16[8,40,2560]{2,1,0:T(8,128)(2,1)} %bitcast.17), calls=%async_computation.5 | async-start | bytes 3276800 | tf_op jit(solution)/shard_map/all_to_all | solution.py:98
  82.4 119.3 %copy-start.5 = (bf16[2560,384]{1,0:T(8,128)(2,1)S(1)}, bf16[2560,384]{1,0:T(8,128)(2,1)}, u32[]{:S(2)}) copy-start(bf16[2560,384]{1,0:T(8,128)(2,1)} %all-gather.8.cloned.1.call-done) | copy-start | bytes 5898244
  82.4 123.4 %collective-permute-start.2 = (bf16[2560,384]{1,0:T(8,128)(2,1)}, bf16[2560,384]{1,0:T(8,128)(2,1)}, u32[]{:S(2)}, u32[]{:S(2)}) collective-permute-start(bf16[2560,384]{1,0:T(8,128)(2,1)} %all-gather.8.cloned.1.call-done), channel_id=1, source_target_pairs={{0,8},{8,0},{1,9},{9,1},{2,10},{10,2},{3,11},{11,3},{4,12},{12,4},... | collective-permute-start | bytes 5898248 | tf_op jit(solution)/shard_map/ppermute | solution.py:25
  82.9 132.3 %all-to-all-start = ((bf16[8,40,2560]{2,1,0:T(8,128)(2,1)}), bf16[8,40,2560]{2,1,0:T(8,128)(2,1)}, u32[]{:S(2)}, u32[]{:S(2)}) async-start(bf16[8,40,2560]{2,1,0:T(8,128)(2,1)} %bitcast.7), calls=%async_computation | async-start | bytes 3276800 | tf_op jit(solution)/shard_map/all_to_all | solution.py:78
  87.3 236.0 %reduce-scatter.4.cloned.1.call-start = ((), (), s32[]{:S(2)}) async-start(), calls=%async_computation.16 | async-start | bytes 2088960 | tf_op jit(solution)/shard_map/reduce_scatter | solution.py:42
  140.5 67.2 %collective-permute-start.1 = (bf16[2560,384]{1,0:T(8,128)(2,1)}, bf16[2560,384]{1,0:T(8,128)(2,1)}, u32[]{:S(2)}, u32[]{:S(2)}) collective-permute-start(bf16[2560,384]{1,0:T(8,128)(2,1)} %all-gather.6.cloned.1.call-done), channel_id=1, source_target_pairs={{0,8},{8,0},{1,9},{9,1},{2,10},{10,2},{3,11},{11,3},{4,12},{12,4},... | collective-permute-start | bytes 5898248 | tf_op jit(solution)/shard_map/ppermute | solution.py:25
  199.4 2.6 copy-start.6
  199.4 20.1 %collective-permute-start = (bf16[2560,384]{1,0:T(8,128)(2,1)}, bf16[2560,384]{1,0:T(8,128)(2,1)}, u32[]{:S(2)}, u32[]{:S(2)}) collective-permute-start(bf16[2560,384]{1,0:T(8,128)(2,1)} %all-gather.4.cloned.1.call-done), channel_id=1, source_target_pairs={{0,8},{8,0},{1,9},{9,1},{2,10},{10,2},{3,11},{11,3},{4,12},{12,4},... | collective-permute-start | bytes 5898248 | tf_op jit(solution)/shard_map/ppermute | solution.py:25
  202.0 2.3 copy-start.7
  207.8 4.6 copy-start.11
  215.2 4.2 copy-start.8
  221.4 4.4 copy-start.9
  225.8 4.1 copy-start.14
  225.8 21.3 %copy-start.16 = (bf16[320,768]{1,0:T(8,128)(2,1)}, bf16[320,768]{1,0:T(8,128)(2,1)S(1)}, u32[]{:S(2)}) copy-start(bf16[320,768]{1,0:T(8,128)(2,1)S(1)} %get-tuple-element.11) | copy-start | bytes 1474564
  230.1 5.0 collective-permute-start.3
  237.0 175.9 %reduce-scatter.6.cloned.1.call-start = ((), (), s32[]{:S(2)}) async-start(), calls=%async_computation.17 | async-start | bytes 2088960 | tf_op jit(solution)/shard_map/reduce_scatter | solution.py:42
  241.0 4.3 collective-permute-start.4
  252.0 4.7 copy-start.17
  252.0 34.7 %all-to-all-start.4 = ((bf16[8,40,2560]{2,1,0:T(8,128)(2,1)}), bf16[8,40,2560]{2,1,0:T(8,128)(2,1)S(1)}, u32[]{:S(2)}, u32[]{:S(2)}) async-start(bf16[8,40,2560]{2,1,0:T(8,128)(2,1)} %bitcast.15), calls=%async_computation.4 | async-start | bytes 3276800 | tf_op jit(solution)/shard_map/all_to_all | solution.py:91
  263.7 4.6 copy-start.10
  263.7 4.6 copy-start.15
  263.7 26.9 %collective-permute-start.5 = (bf16[2560,384]{1,0:T(8,128)(2,1)}, bf16[2560,384]{1,0:T(8,128)(2,1)}, u32[]{:S(2)}, u32[]{:S(2)}) collective-permute-start(bf16[2560,384]{1,0:T(8,128)(2,1)} %slice.48), channel_id=1, source_target_pairs={{0,8},{8,0},{1,9},{9,1},{2,10},{10,2},{3,11},{11,3},{4,12},{12,4},... | collective-permute-start | bytes 5898248 | tf_op jit(solution)/shard_map/ppermute | solution.py:25
  286.6 25.1 %all-to-all-start.6 = ((bf16[8,40,2560]{2,1,0:T(8,128)(2,1)}), bf16[8,40,2560]{2,1,0:T(8,128)(2,1)S(1)}, u32[]{:S(2)}, u32[]{:S(2)}) async-start(bf16[8,40,2560]{2,1,0:T(8,128)(2,1)} %bitcast.59), calls=%async_computation.6 | async-start | bytes 3276800 | tf_op jit(solution)/shard_map/all_to_all | solution.py:109
  290.6 211.3 %reduce-scatter.8.cloned.1.call-start = ((), (), s32[]{:S(2)}) async-start(), calls=%async_computation.18 | async-start | bytes 2088960 | tf_op jit(solution)/shard_map/reduce_scatter | solution.py:42
  329.7 180.1 %copy-start.1 = (bf16[256,2560]{1,0:T(8,128)(2,1)S(1)}, bf16[256,2560]{1,0:T(8,128)(2,1)}, u32[]{:S(2)}) copy-start(bf16[256,2560]{1,0:T(8,128)(2,1)} %param.11) | copy-start | bytes 3932164
  (2 other events, 3.7 us)
Sparse Core Ops, SparseCore 0:
  15.9 66.5 all-gather.7
  84.9 55.5 all-gather.5
  143.0 56.3 all-gather.3
  237.2 86.1 reduce-scatter.3
  327.2 85.7 reduce-scatter.5
  416.3 85.5 reduce-scatter.7

commit v2 on v1

--- a/solution.py
+++ b/solution.py
@@ -25,23 +25,30 @@
     return lax.ppermute(value, "core", perm=[(0, 1), (1, 0)])
 
 
-def gather_weight(weight):
-    own = lax.all_to_all(weight, "core", split_axis=1, concat_axis=0, tiled=True)
-    own = lax.all_gather(own, CHIPS, axis=0, tiled=True)
+def gather_weights(*weights):
+    stacked = jnp.stack(weights)
+    own = lax.all_to_all(stacked, "core", split_axis=2, concat_axis=1, tiled=True)
+    own = lax.all_gather(own, CHIPS, axis=1, tiled=True)
     other = swap_cores(own)
-    return jnp.concatenate([own, other], axis=1)
+    return [(own[i], other[i]) for i in range(len(weights))]
 
 
-def scatter_grad(part):
-    half = part.shape[1] // 2
-    rounded = part.astype(jnp.bfloat16)
-    arrived = swap_cores(rounded[:, half:])
-    pair_sum = (rounded[:, :half].astype(jnp.float32) + arrived.astype(jnp.float32)).astype(
-        jnp.bfloat16
+def scatter_grads(*parts):
+    own = jnp.stack([p[0] for p in parts]).astype(jnp.bfloat16)
+    other = jnp.stack([p[1] for p in parts]).astype(jnp.bfloat16)
+    arrived = swap_cores(other)
+    pair_sum = (own.astype(jnp.float32) + arrived.astype(jnp.float32)).astype(jnp.bfloat16)
+    chip_sum = lax.psum_scatter(pair_sum, CHIPS, scatter_dimension=1, tiled=True)
+    block = lax.all_to_all(chip_sum, "core", split_axis=1, concat_axis=2, tiled=True)
+    block = block.astype(jnp.float32)
+    return [block[i] for i in range(len(parts))]
+
+
+def halves(left, pair, dims):
+    return (
+        lax.dot_general(left, pair[0], dims, preferred_element_type=jnp.float32),
+        lax.dot_general(left, pair[1], dims, preferred_element_type=jnp.float32),
     )
-    chip_sum = lax.psum_scatter(pair_sum, CHIPS, scatter_dimension=0, tiled=True)
-    block = lax.all_to_all(chip_sum, "core", split_axis=0, concat_axis=1, tiled=True)
-    return block.astype(jnp.float32)
 
 
 def shards(tokens, routes, gate_levels, w_gate, w_up, w_down, grad_out):
@@ -72,19 +79,23 @@
             experts, capacity, model_width
         )
 
-    gate_full = gather_weight(w_gate[0])
-    up_full = gather_weight(w_up[0])
-    down_full = gather_weight(w_down[0])
+    gate_pair, up_pair, down_pair = gather_weights(w_gate[0], w_up[0], w_down[0])
+    plain = (((1,), (0,)), ((), ()))
+    last = (((1,), (1,)), ((), ()))
     received = lax.all_to_all(
         pack_rows(tokens), "expert", split_axis=0, concat_axis=0, tiled=True
     ).reshape(slot_count, model_width)
-    act_gate = jnp.dot(received, gate_full, preferred_element_type=jnp.float32)
-    act_up = jnp.dot(received, up_full, preferred_element_type=jnp.float32)
+    act_gate = jnp.concatenate(halves(received, gate_pair, plain), axis=1)
+    act_up = jnp.concatenate(halves(received, up_pair, plain), axis=1)
     sigmoid_gate = jax.nn.sigmoid(act_gate)
     silu_gate = act_gate * sigmoid_gate
     hidden = (silu_gate * act_up).astype(jnp.bfloat16)
+    half = hidden.shape[1] // 2
     expert_out = (
-        contract_last(hidden, down_full)
+        (
+            contract_last(hidden[:, :half], down_pair[0])
+            + contract_last(hidden[:, half:], down_pair[1])
+        )
         .astype(jnp.bfloat16)
         .reshape(experts, capacity, model_width)
     )
@@ -98,14 +109,17 @@
     grad_rows = lax.all_to_all(
         pack_rows(out_grad), "expert", split_axis=0, concat_axis=0, tiled=True
     ).reshape(slot_count, model_width)
-    hidden_grad = jnp.dot(grad_rows, down_full, preferred_element_type=jnp.float32)
+    hidden_grad = jnp.concatenate(halves(grad_rows, down_pair, plain), axis=1)
     gate_delta = (
         hidden_grad * act_up * sigmoid_gate * (1.0 + act_gate * (1.0 - sigmoid_gate))
     ).astype(jnp.bfloat16)
     up_delta = (hidden_grad * silu_gate).astype(jnp.bfloat16)
-    token_grad = (contract_last(gate_delta, gate_full) + contract_last(up_delta, up_full)).astype(
-        jnp.bfloat16
-    )
+    token_grad = (
+        contract_last(gate_delta[:, :half], gate_pair[0])
+        + contract_last(gate_delta[:, half:], gate_pair[1])
+        + contract_last(up_delta[:, :half], up_pair[0])
+        + contract_last(up_delta[:, half:], up_pair[1])
+    ).astype(jnp.bfloat16)
     arrived = lax.all_to_all(
         token_grad.reshape(experts, capacity, model_width),
         "expert",
@@ -114,9 +128,11 @@
         tiled=True,
     )
     grad_tokens = jnp.take(arrived.reshape(slot_count, model_width), slot_index, axis=0)
-    grad_down = scatter_grad(contract_first(grad_rows, hidden))
-    grad_gate = scatter_grad(contract_first(received, gate_delta))
-    grad_up = scatter_grad(contract_first(received, up_delta))
+    grad_gate, grad_up, grad_down = scatter_grads(
+        (contract_first(received, gate_delta[:, :half]), contract_first(received, gate_delta[:, half:])),
+        (contract_first(received, up_delta[:, :half]), contract_first(received, up_delta[:, half:])),
+        (contract_first(grad_rows, hidden[:, :half]), contract_first(grad_rows, hidden[:, half:])),
+    )
     return (moe_out, grad_tokens, grad_gate[None], grad_up[None], grad_down[None])
 
 

time: 518 us -> 309 us (0.60)
  waiting for transfers between devices: 353 us -> 179 us
  blocking collectives: 36.2 us -> 12.5 us
  local copies, waits for them, and re-layouts: 36.8 us -> 24.7 us
  matrix products: 34.2 us -> 44.1 us
  starting transfers between devices: 25.7 us -> 18 us
    reduce_scatter x3 -> x1, waiting for transfers between devices: 171 us -> 14.6 us  [scatter_grads(): lax.psum_scatter(pair_sum, CHIPS, scatter_dimension=1, tiled=True)]
    all_gather x3 -> x1, waiting for transfers between devices: 145 us -> 78.8 us  [gather_weights(): own = lax.all_gather(own, CHIPS, axis=1, tiled=True)]
    all_to_all x1, waiting for transfers between devices: 15.6 us -> 39.9 us  [shards(): lax.all_to_all(expert_out, 'expert', split_axis=0, concat_axis=0, tiled=T...]
    all_to_all x6 -> x2, blocking collectives: 36.2 us -> 12.5 us  [the longest x1 6.89 us: gather_weights(): lax.all_to_all(stacked, 'core', split_axis=2, concat_axis=1, tiled=True)]
    all_to_all x1, waiting for transfers between devices: 0.01 us -> 14.4 us  [shards(): lax.all_to_all(pack_rows(out_grad), 'expert', split_axis=0, concat_axis=0...]
    all_to_all x1, waiting for transfers between devices: 14.6 us -> 25.8 us  [shards(): lax.all_to_all(token_grad.reshape(experts, capacity, model_width), 'exper...]
    concatenate x3 -> x0, local copies, waits for them, and re-layouts: 8.47 us -> none  [gather_weight(): return jnp.concatenate([own, other], axis=1)]
    dot_general x3 -> x6, matrix products: 11.4 us -> 18.1 us  [contract_last(): lax.dot_general(matrix_a, matrix_b, (((1,), (1,)), ((), ())), preferred_e...]
  transfers between devices with their start and end apart: 16 -> 8, of which waited for: 10 -> 6; matrix products, arithmetic and copies ran while one was open for 13% -> 18% of each run, Pallas kernels for 0% -> 0%
where the time goes in v2:
time: 309 us; the launch traced here: 308 us
  waiting for transfers between devices  179 us (58%)
  matrix products  44.1 us (14%)
  local copies, waits for them, and re-layouts  24.7 us (8%)
  starting transfers between devices  18 us (6%)
  other arithmetic  15.7 us (5%)
  between operations  14.5 us (5%)
  blocking collectives  12.5 us (4%)
    all_gather x1, waiting for transfers between devices, gather_weights(): own = lax.all_gather(own, CHIPS, axis=1, tiled=True)  78.8 us
    all_to_all x1, waiting for transfers between devices, shards(): lax.all_to_all(expert_out, 'expert', split_axis=0, concat_axis=0, tiled=T...  39.9 us
    all_to_all x1, waiting for transfers between devices, shards(): lax.all_to_all(token_grad.reshape(experts, capacity, model_width), 'exper...  25.8 us
    dot_general x6, matrix products, contract_last(): lax.dot_general(matrix_a, matrix_b, (((1,), (1,)), ((), ())), preferred_e...  18.1 us
    reduce_scatter x1, waiting for transfers between devices, scatter_grads(): lax.psum_scatter(pair_sum, CHIPS, scatter_dimension=1, tiled=True)  14.6 us
    all_to_all x1, waiting for transfers between devices, shards(): lax.all_to_all(pack_rows(out_grad), 'expert', split_axis=0, concat_axis=0...  14.4 us
    dot_general x3, matrix products, halves(): lax.dot_general(left, pair[0], dims, preferred_element_type=jnp.float32)  9.8 us
    dot_general x6, matrix products, contract_first(): lax.dot_general(matrix_a, matrix_b, (((0,), (0,)), ((), ())), preferred_e...  8.45 us
  transfers between devices with their start and end apart: 8, of which 6 were waited for; matrix products, arithmetic and copies ran while one was open for 18% of the time, Pallas kernels for 0%

profile of v2, /device:TPU:1, one launch (start us, length us, event | category | flops | bytes accessed | tf_op | source)
XLA Modules:
  0.0 308.1 jit_solution(261470761299780988)
XLA Ops:
  10.1 6.9 %all_to_all.47 = bf16[2,2,46080]{2,1,0:T(2,128)(2,1)S(1)} all-to-all(bf16[2,2,46080]{2,1,0:T(2,128)(2,1)S(1)} %reshape.145), channel_id=1, replica_groups=mesh['x'=4,'zh'=4,'core'=2,'expert'=8] {'core'}, dimensions={0} | all-to-all | bytes 737280 | tf_op jit(solution)/shard_map/all_to_all | solution.py:30
  22.3 1.6 multiply_convert_fusion
  23.9 3.2 %gather_fusion.2 = bf16[320,2560]{1,0:T(8,128)(2,1)} fusion(bf16[256,2560]{1,0:T(8,128)(2,1)S(1)} %multiply_convert_fusion, s32[1024]{0:T(1024)S(1)} %pad_clamp_fusion.1), kind=kCustom, calls=%fused_computation.2.clone | custom fusion | bytes 3278080 | tf_op jit(solution)/shard_map/jit(_take)/gather | solution.py:78
  27.1 3.2 %gather_fusion = bf16[320,2560]{1,0:T(8,128)(2,1)} fusion(bf16[256,2560]{1,0:T(8,128)(2,1)S(1)} %copy-done, s32[1024]{0:T(1024)S(1)} %pad_clamp_fusion.1), kind=kCustom, calls=%fused_computation.clone | custom fusion | bytes 3278080 | tf_op jit(solution)/shard_map/jit(_take)/gather | solution.py:78
  30.3 2.2 scatter_custom_fusion.1
  32.5 3.7 %select_multiply_fusion = (bf16[320,2560]{1,0:T(8,128)(2,1)}, bf16[320,2560]{1,0:T(8,128)(2,1)}) fusion(bf16[320,2560]{1,0:T(8,128)(2,1)S(1)} %copy-done.2, pred[320]{0:T(512)(128)(4,1)S(1)} %compare_and_fusion.1, bf16[320]{0:T(512)(128)(2,1)S(1)} %scatter_custom_fusion.1, bf16[320,2560]{1,0:T(8,128)(2,1)} %gather_fusion), kind=kLoop, calls=%fused_computation.42 | loop fusion | flops 3276800 | bytes 6554560 | tf_op jit(solution)/shard_map/mul | solution.py:78
  36.2 3.7 %all-to-all-start = ((bf16[8,40,2560]{2,1,0:T(8,128)(2,1)}), bf16[8,40,2560]{2,1,0:T(8,128)(2,1)S(1)}, u32[]{:S(2)}, u32[]{:S(2)}) async-start(bf16[8,40,2560]{2,1,0:T(8,128)(2,1)} %bitcast.7), calls=%async_computation | async-start | bytes 3276800 | tf_op jit(solution)/shard_map/all_to_all | solution.py:85
  39.9 78.8 %all-gather.2.cloned.1.call-done = bf16[3,2560,384]{2,1,0:T(8,128)(2,1)} async-done(((bf16[3,160,384]{2,1,0:T(8,128)(2,1)}), bf16[3,2560,384]{2,1,0:T(8,128)(2,1)}) %all-gather.2.cloned.1.call-update) | async-done | bytes 5898256 | tf_op jit(solution)/shard_map/all_gather | solution.py:31
  119.1 4.4 %all-to-all-start.3 = ((bf16[8,40,2560]{2,1,0:T(8,128)(2,1)}), bf16[8,40,2560]{2,1,0:T(8,128)(2,1)S(1)}, u32[]{:S(2)}, u32[]{:S(2)}) async-start(bf16[8,40,2560]{2,1,0:T(8,128)(2,1)} %bitcast.20), calls=%async_computation.3 | async-start | bytes 3276800 | tf_op jit(solution)/shard_map/all_to_all | solution.py:109
  123.7 3.3 %fusion.9 = f32[320,384]{1,0:T(8,128)} fusion(bf16[320,2560]{1,0:T(8,128)(2,1)S(1)} %bitcast.84, bf16[3,2560,384]{2,1,0:T(8,128)(2,1)} %all-gather.2.cloned.1.call-done), kind=kOutput, calls=%fused_computation.35 | convolution fusion | flops 629145600 | bytes 4096000 | tf_op jit(solution)/shard_map/dot_general | solution.py:49
  127.1 3.3 %fusion.11 = f32[320,384]{1,0:T(8,128)} fusion(bf16[320,2560]{1,0:T(8,128)(2,1)S(1)} %bitcast.85, bf16[3,2560,384]{2,1,0:T(8,128)(2,1)} %all-gather.2.cloned.1.call-done), kind=kOutput, calls=%fused_computation.37 | convolution fusion | flops 629145600 | bytes 4096000 | tf_op jit(solution)/shard_map/dot_general | solution.py:49
  130.4 14.4 %all-to-all-done.3 = bf16[8,40,2560]{2,1,0:T(8,128)(2,1)S(1)} async-done(((bf16[8,40,2560]{2,1,0:T(8,128)(2,1)}), bf16[8,40,2560]{2,1,0:T(8,128)(2,1)S(1)}, u32[]{:S(2)}, u32[]{:S(2)}) %all-to-all-start.3) | async-done | bytes 1638432 | tf_op jit(solution)/shard_map/all_to_all | solution.py:109
  144.8 3.1 %fusion.13 = f32[320,384]{1,0:T(8,128)S(1)} fusion(bf16[320,2560]{1,0:T(8,128)(2,1)S(1)} %bitcast.92, bf16[3,2560,384]{2,1,0:T(8,128)(2,1)} %all-gather.2.cloned.1.call-done), kind=kOutput, calls=%fused_computation.39 | convolution fusion | flops 629145600 | bytes 4096000 | tf_op jit(solution)/shard_map/dot_general | solution.py:49
  148.0 2.5 fusion.15
  150.5 2.5 fusion.10
  153.1 2.6 fusion.12
  168.0 5.0 %collective-permute-done.1 = bf16[3,2560,384]{2,1,0:T(8,128)(2,1)S(1)} collective-permute-done((bf16[3,2560,384]{2,1,0:T(8,128)(2,1)S(1)}, bf16[3,2560,384]{2,1,0:T(8,128)(2,1)S(1)}, u32[]{:S(2)}, u32[]{:S(2)}) %collective-permute-start.1) | collective-permute-done | bytes 5898272 | tf_op jit(solution)/shard_map/ppermute | solution.py:25
  172.9 3.8 %add_convert_fusion = bf16[3,2560,384]{2,1,0:T(8,128)(2,1)} fusion(bf16[3,2560,384]{2,1,0:T(8,128)(2,1)S(1)} %collective-permute-done.1, bf16[1,2560,384]{2,1,0:T(8,128)(2,1)S(1)} %fusion.4, bf16[1,2560,384]{2,1,0:T(8,128)(2,1)S(1)} %fusion.3, bf16[1,2560,384]{2,1,0:T(8,128)(2,1)S(1)} %fusion.2), kind=kLoop, calls=%fused_computation.6 | loop fusion | flops 17694720 | bytes 17694720 | tf_op jit(solution)/shard_map/convert_element_type | solution.py:40
  176.8 2.6 fusion.14
  179.4 3.8 %fusion = bf16[320,2560]{1,0:T(8,128)(2,1)} fusion(f32[320,2560]{1,0:T(8,128)S(1)} %fusion.14, bf16[3,2560,384]{2,1,0:T(8,128)(2,1)} %collective-permute-done, bf16[320,768]{1,0:T(8,128)(2,1)S(1)} %get-tuple-element.11), kind=kOutput, calls=%fused_computation.18 | convolution fusion | flops 630784000 | bytes 7127040 | tf_op jit(solution)/shard_map/dot_general | solution.py:13
  183.2 3.7 %all-to-all-start.2 = ((bf16[8,40,2560]{2,1,0:T(8,128)(2,1)}), bf16[8,40,2560]{2,1,0:T(8,128)(2,1)S(1)}, u32[]{:S(2)}, u32[]{:S(2)}) async-start(bf16[8,40,2560]{2,1,0:T(8,128)(2,1)} %bitcast.18), calls=%async_computation.2 | async-start | bytes 3276800 | tf_op jit(solution)/shard_map/all_to_all | solution.py:102
  186.9 2.6 fusion.8
  189.5 2.6 convolution_add_fusion.2
  192.1 2.6 convolution_add_fusion.1
  194.7 3.9 %fusion.1 = bf16[320,2560]{1,0:T(8,128)(2,1)} fusion(f32[320,2560]{1,0:T(8,128)S(1)} %convolution_add_fusion.1, bf16[3,2560,384]{2,1,0:T(8,128)(2,1)} %collective-permute-done, bf16[320,768]{1,0:T(8,128)(2,1)S(1)} %get-tuple-element.9), kind=kOutput, calls=%fused_computation.19 | convolution fusion | flops 630784000 | bytes 7127040 | tf_op jit(solution)/shard_map/dot_general | solution.py:13
  198.6 39.9 %all-to-all-done.2 = bf16[8,40,2560]{2,1,0:T(8,128)(2,1)S(1)} async-done(((bf16[8,40,2560]{2,1,0:T(8,128)(2,1)}), bf16[8,40,2560]{2,1,0:T(8,128)(2,1)S(1)}, u32[]{:S(2)}, u32[]{:S(2)}) %all-to-all-start.2) | async-done | bytes 1638432 | tf_op jit(solution)/shard_map/all_to_all | solution.py:102
  238.5 4.5 %all-to-all-start.4 = ((bf16[8,40,2560]{2,1,0:T(8,128)(2,1)}), bf16[8,40,2560]{2,1,0:T(8,128)(2,1)S(1)}, u32[]{:S(2)}, u32[]{:S(2)}) async-start(bf16[8,40,2560]{2,1,0:T(8,128)(2,1)} %bitcast.80), calls=%async_computation.4 | async-start | bytes 3276800 | tf_op jit(solution)/shard_map/all_to_all | solution.py:123
  243.0 2.5 gather_fusion.1
  245.5 25.8 %all-to-all-done.4 = bf16[8,40,2560]{2,1,0:T(8,128)(2,1)S(1)} async-done(((bf16[8,40,2560]{2,1,0:T(8,128)(2,1)}), bf16[8,40,2560]{2,1,0:T(8,128)(2,1)S(1)}, u32[]{:S(2)}, u32[]{:S(2)}) %all-to-all-start.4) | async-done | bytes 1638432 | tf_op jit(solution)/shard_map/all_to_all | solution.py:123
  271.4 1.4 gather_fusion.3
  276.0 14.6 %reduce-scatter.2.cloned.1.call-done = bf16[3,160,384]{2,1,0:T(8,128)(2,1)} async-done(((bf16[3,2560,384]{2,1,0:T(8,128)(2,1)}), bf16[3,160,384]{2,1,0:T(8,128)(2,1)}) %reduce-scatter.2.cloned.1.call-update) | async-done | bytes 368656 | tf_op jit(solution)/shard_map/reduce_scatter | solution.py:41
  291.9 5.7 %all_to_all.48 = bf16[3,160,384]{2,0,1:T(4,128)(2,1)S(1)} all-to-all(bf16[3,160,384]{2,0,1:T(4,128)(2,1)S(1)} %copy.34), channel_id=1, replica_groups=mesh['x'=4,'zh'=4,'core'=2,'expert'=8] {'core'}, dimensions={1} | all-to-all | bytes 737280 | tf_op jit(solution)/shard_map/all_to_all | solution.py:42
  (73 shorter events, 29.2 us)
Async XLA Ops:
  7.2 19.9 %copy-start = (bf16[256,2560]{1,0:T(8,128)(2,1)S(1)}, bf16[256,2560]{1,0:T(8,128)(2,1)}, u32[]{:S(2)}) copy-start(bf16[256,2560]{1,0:T(8,128)(2,1)} %param.11) | copy-start | bytes 3932164
  7.2 111.5 %all-gather.2.cloned.1.call-start = ((), (), s32[]{:S(2)}) async-start(), calls=%async_computation.7 | async-start | bytes 6266880 | tf_op jit(solution)/shard_map/all_gather | solution.py:31
  10.1 9.8 %copy-start.10 = (s32[256,1]{0,1:T(1,128)S(1)}, s32[256,1]{0,1:T(1,128)}, u32[]{:S(2)}) copy-start(s32[256,1]{0,1:T(1,128)} %param.12) | copy-start | bytes 3076
  10.1 12.2 %copy-start.11 = (s32[256,1]{0,1:T(1,128)S(1)}, s32[256,1]{0,1:T(1,128)}, u32[]{:S(2)}) copy-start(s32[256,1]{0,1:T(1,128)} %param.13) | copy-start | bytes 3076
  27.1 5.4 %copy-start.2 = (bf16[320,2560]{1,0:T(8,128)(2,1)S(1)}, bf16[320,2560]{1,0:T(8,128)(2,1)}, u32[]{:S(2)}) copy-start(bf16[320,2560]{1,0:T(8,128)(2,1)} %gather_fusion.2) | copy-start | bytes 4915204
  36.2 83.0 %all-to-all-start = ((bf16[8,40,2560]{2,1,0:T(8,128)(2,1)}), bf16[8,40,2560]{2,1,0:T(8,128)(2,1)S(1)}, u32[]{:S(2)}, u32[]{:S(2)}) async-start(bf16[8,40,2560]{2,1,0:T(8,128)(2,1)} %bitcast.7), calls=%async_computation | async-start | bytes 3276800 | tf_op jit(solution)/shard_map/all_to_all | solution.py:85
  118.7 29.3 %collective-permute-start = (bf16[3,2560,384]{2,1,0:T(8,128)(2,1)}, bf16[3,2560,384]{2,1,0:T(8,128)(2,1)}, u32[]{:S(2)}, u32[]{:S(2)}) collective-permute-start(bf16[3,2560,384]{2,1,0:T(8,128)(2,1)} %all-gather.2.cloned.1.call-done), channel_id=1, source_target_pairs={{0,8},{8,0},{1,9},{9,1},{2,10},{10,2},{3,11},{11,3},{4,12},{12,4},... | collective-permute-start | bytes 17694728 | tf_op jit(solution)/shard_map/ppermute | solution.py:25
  119.1 34.0 %copy-start.4 = (bf16[8,40,2560]{2,1,0:T(8,128)(2,1)}, bf16[8,40,2560]{2,1,0:T(8,128)(2,1)S(1)}, u32[]{:S(2)}) copy-start(bf16[8,40,2560]{2,1,0:T(8,128)(2,1)S(1)} %all-to-all-done) | copy-start | bytes 4915204
  119.1 25.7 %all-to-all-start.3 = ((bf16[8,40,2560]{2,1,0:T(8,128)(2,1)}), bf16[8,40,2560]{2,1,0:T(8,128)(2,1)S(1)}, u32[]{:S(2)}, u32[]{:S(2)}) async-start(bf16[8,40,2560]{2,1,0:T(8,128)(2,1)} %bitcast.20), calls=%async_computation.3 | async-start | bytes 3276800 | tf_op jit(solution)/shard_map/all_to_all | solution.py:109
  123.5 167.1 %reduce-scatter.2.cloned.1.call-start = ((), (), s32[]{:S(2)}) async-start(), calls=%async_computation.8 | async-start | bytes 6266880 | tf_op jit(solution)/shard_map/reduce_scatter | solution.py:41
  144.8 3.2 %copy-start.6 = (bf16[8,40,2560]{2,1,0:T(8,128)(2,1)}, bf16[8,40,2560]{2,1,0:T(8,128)(2,1)S(1)}, u32[]{:S(2)}) copy-start(bf16[8,40,2560]{2,1,0:T(8,128)(2,1)S(1)} %all-to-all-done.3) | copy-start | bytes 4915204
  153.1 2.7 copy-start.8
  153.1 2.7 copy-start.9
  155.8 1.4 copy-start.7
  157.2 1.4 copy-start.5
  162.6 10.3 %collective-permute-start.1 = (bf16[3,2560,384]{2,1,0:T(8,128)(2,1)S(1)}, bf16[3,2560,384]{2,1,0:T(8,128)(2,1)S(1)}, u32[]{:S(2)}, u32[]{:S(2)}) collective-permute-start(bf16[3,2560,384]{2,1,0:T(8,128)(2,1)S(1)} %pad_maximum_fusion), channel_id=1, source_target_pairs={{0,8},{8,0},{1,9},{9,1},{2,10},{10,2},{3,11},{11,3},{4,12},{12,4},... | collective-permute-start | bytes 17694728 | tf_op jit(solution)/shard_map/ppermute | solution.py:25
  183.2 55.3 %all-to-all-start.2 = ((bf16[8,40,2560]{2,1,0:T(8,128)(2,1)}), bf16[8,40,2560]{2,1,0:T(8,128)(2,1)S(1)}, u32[]{:S(2)}, u32[]{:S(2)}) async-start(bf16[8,40,2560]{2,1,0:T(8,128)(2,1)} %bitcast.18), calls=%async_computation.2 | async-start | bytes 3276800 | tf_op jit(solution)/shard_map/all_to_all | solution.py:102
  238.5 32.8 %all-to-all-start.4 = ((bf16[8,40,2560]{2,1,0:T(8,128)(2,1)}), bf16[8,40,2560]{2,1,0:T(8,128)(2,1)S(1)}, u32[]{:S(2)}, u32[]{:S(2)}) async-start(bf16[8,40,2560]{2,1,0:T(8,128)(2,1)} %bitcast.80), calls=%async_computation.4 | async-start | bytes 3276800 | tf_op jit(solution)/shard_map/all_to_all | solution.py:123
  272.8 1.8 copy-start.3
  297.5 3.7 %copy-start.1 = (bf16[256,2560]{1,0:T(8,128)(2,1)S(1)}, bf16[256,2560]{1,0:T(8,128)(2,1)}, u32[]{:S(2)}) copy-start(bf16[256,2560]{1,0:T(8,128)(2,1)} %param.11) | copy-start | bytes 3932164
Sparse Core Ops, SparseCore 0:
  20.0 98.5 all-gather.1
  176.9 113.6 reduce-scatter.1

commit v3 on v2

--- a/solution.py
+++ b/solution.py
@@ -34,14 +34,26 @@
 
 
 def scatter_grads(*parts):
-    own = jnp.stack([p[0] for p in parts]).astype(jnp.bfloat16)
-    other = jnp.stack([p[1] for p in parts]).astype(jnp.bfloat16)
-    arrived = swap_cores(other)
-    pair_sum = (own.astype(jnp.float32) + arrived.astype(jnp.float32)).astype(jnp.bfloat16)
-    chip_sum = lax.psum_scatter(pair_sum, CHIPS, scatter_dimension=1, tiled=True)
-    block = lax.all_to_all(chip_sum, "core", split_axis=1, concat_axis=2, tiled=True)
+    core = lax.axis_index("core")
+    stacked = jnp.stack(parts).astype(jnp.bfloat16)
+    count, width, ff = stacked.shape
+    chips = lax.axis_size(CHIPS)
+    grouped = stacked.reshape(count, chips, 2, width // (2 * chips), ff)
+    mine = lax.dynamic_index_in_dim(grouped, core, axis=2, keepdims=False)
+    theirs = lax.dynamic_index_in_dim(grouped, 1 - core, axis=2, keepdims=False)
+    arrived = swap_cores(theirs)
+    pair_sum = (mine.astype(jnp.float32) + arrived.astype(jnp.float32)).astype(jnp.bfloat16)
+    pair_sum = pair_sum.reshape(count, width // 2, ff)
+    block = lax.psum_scatter(pair_sum, CHIPS, scatter_dimension=1, tiled=True)
     block = block.astype(jnp.float32)
-    return [block[i] for i in range(len(parts))]
+    return [block[i] for i in range(count)]
+
+
+def true_order(value):
+    core = lax.axis_index("core")
+    half = value.shape[1] // 2
+    both = jnp.concatenate([value, value], axis=1)
+    return lax.dynamic_slice_in_dim(both, core * half, 2 * half, axis=1)
 
 
 def halves(left, pair, dims):
@@ -82,9 +94,16 @@
     gate_pair, up_pair, down_pair = gather_weights(w_gate[0], w_up[0], w_down[0])
     plain = (((1,), (0,)), ((), ()))
     last = (((1,), (1,)), ((), ()))
-    received = lax.all_to_all(
-        pack_rows(tokens), "expert", split_axis=0, concat_axis=0, tiled=True
-    ).reshape(slot_count, model_width)
+    out_grad = (gate_weight * grad_out.astype(jnp.float32)).astype(jnp.bfloat16)
+    both_rows = lax.all_to_all(
+        jnp.stack([pack_rows(tokens), pack_rows(out_grad)]),
+        "expert",
+        split_axis=1,
+        concat_axis=1,
+        tiled=True,
+    )
+    received = both_rows[0].reshape(slot_count, model_width)
+    grad_rows = both_rows[1].reshape(slot_count, model_width)
     act_gate = jnp.concatenate(halves(received, gate_pair, plain), axis=1)
     act_up = jnp.concatenate(halves(received, up_pair, plain), axis=1)
     sigmoid_gate = jax.nn.sigmoid(act_gate)
@@ -105,10 +124,6 @@
     moe_out = (gate_weight * jnp.take(returned, slot_index, axis=0).astype(jnp.float32)).astype(
         jnp.bfloat16
     )
-    out_grad = (gate_weight * grad_out.astype(jnp.float32)).astype(jnp.bfloat16)
-    grad_rows = lax.all_to_all(
-        pack_rows(out_grad), "expert", split_axis=0, concat_axis=0, tiled=True
-    ).reshape(slot_count, model_width)
     hidden_grad = jnp.concatenate(halves(grad_rows, down_pair, plain), axis=1)
     gate_delta = (
         hidden_grad * act_up * sigmoid_gate * (1.0 + act_gate * (1.0 - sigmoid_gate))
@@ -129,9 +144,9 @@
     )
     grad_tokens = jnp.take(arrived.reshape(slot_count, model_width), slot_index, axis=0)
     grad_gate, grad_up, grad_down = scatter_grads(
-        (contract_first(received, gate_delta[:, :half]), contract_first(received, gate_delta[:, half:])),
-        (contract_first(received, up_delta[:, :half]), contract_first(received, up_delta[:, half:])),
-        (contract_first(grad_rows, hidden[:, :half]), contract_first(grad_rows, hidden[:, half:])),
+        contract_first(received, true_order(gate_delta)),
+        contract_first(received, true_order(up_delta)),
+        contract_first(grad_rows, true_order(hidden)),
     )
     return (moe_out, grad_tokens, grad_gate[None], grad_up[None], grad_down[None])
 

time: 309 us -> 316 us (1.023)
  local copies, waits for them, and re-layouts: 24.7 us -> 37.5 us
  matrix products: 44.1 us -> 37.2 us
  other arithmetic: 15.7 us -> 22.1 us
  blocking collectives: 12.5 us -> 6.89 us
  starting transfers between devices: 18 us -> 12.7 us
  waiting for transfers between devices: 179 us -> 184 us
    all_gather x1, waiting for transfers between devices: 78.8 us -> 95 us  [gather_weights(): own = lax.all_gather(own, CHIPS, axis=1, tiled=True)]
    all_to_all x2 -> x1, waiting for transfers between devices: 14.4 us -> 0.01 us  [shards(): lax.all_to_all(jnp.stack([pack_rows(tokens), pack_rows(out_grad)]), 'expe...]
    dot_general x0 -> x2, local copies, waits for them, and re-layouts: none -> 6.32 us  [contract_first(): lax.dot_general(matrix_a, matrix_b, (((0,), (0,)), ((), ())), preferred_e...]
    all_to_all x1 -> x0, blocking collectives: 5.65 us -> none  [scatter_grads(): lax.all_to_all(chip_sum, 'core', split_axis=1, concat_axis=2, tiled=True)]
    dot_general x3, matrix products: 9.8 us -> 4.72 us  [halves(): lax.dot_general(left, pair[0], dims, preferred_element_type=jnp.float32)]
    ppermute x2, waiting for transfers between devices: 4.98 us -> 9.88 us  [swap_cores(): return lax.ppermute(value, 'core', perm=[(0, 1), (1, 0)])]
    convert_element_type x2 -> x1, other arithmetic: 3.94 us -> 8.39 us  [scatter_grads(): (mine.astype(jnp.float32) + arrived.astype(jnp.float32)).astype(jnp.bfloa...]
    all_to_all x2 -> x1, starting transfers between devices: 8.09 us -> 3.73 us  [shards(): lax.all_to_all(jnp.stack([pack_rows(tokens), pack_rows(out_grad)]), 'expe...]
  transfers between devices with their start and end apart: 8 -> 7, of which waited for: 6 -> 5; matrix products, arithmetic and copies ran while one was open for 18% -> 18% of each run, Pallas kernels for 0% -> 0%
where the time goes in v3:
time: 316 us; the launch traced here: 315 us
  waiting for transfers between devices  184 us (58%)
  local copies, waits for them, and re-layouts  37.5 us (12%)
  matrix products  37.2 us (12%)
  other arithmetic  22.1 us (7%)
  between operations  14.4 us (5%)
  starting transfers between devices  12.7 us (4%)
  blocking collectives  6.89 us (2%)
    all_gather x1, waiting for transfers between devices, gather_weights(): own = lax.all_gather(own, CHIPS, axis=1, tiled=True)  95 us
    all_to_all x1, waiting for transfers between devices, shards(): lax.all_to_all(expert_out, 'expert', split_axis=0, concat_axis=0, tiled=T...  38.3 us
    all_to_all x1, waiting for transfers between devices, shards(): lax.all_to_all(token_grad.reshape(experts, capacity, model_width), 'exper...  27.4 us
    dot_general x6, matrix products, contract_last(): lax.dot_general(matrix_a, matrix_b, (((1,), (1,)), ((), ())), preferred_e...  18.1 us
    reduce_scatter x1, waiting for transfers between devices, scatter_grads(): block = lax.psum_scatter(pair_sum, CHIPS, scatter_dimension=1, tiled=True)  13.7 us
    ppermute x2, waiting for transfers between devices, swap_cores(): return lax.ppermute(value, 'core', perm=[(0, 1), (1, 0)])  9.88 us
    convert_element_type x1, other arithmetic, scatter_grads(): (mine.astype(jnp.float32) + arrived.astype(jnp.float32)).astype(jnp.bfloa...  8.39 us
    dot_general x3, matrix products, halves(): lax.dot_general(left, pair[1], dims, preferred_element_type=jnp.float32)  7.64 us
  transfers between devices with their start and end apart: 7, of which 5 were waited for; matrix products, arithmetic and copies ran while one was open for 18% of the time, Pallas kernels for 0%

profile of v3, /device:TPU:1, one launch (start us, length us, event | category | flops | bytes accessed | tf_op | source)
XLA Modules:
  0.0 315.1 jit_solution(3590791162813516619)
XLA Ops:
  10.1 6.9 %all_to_all.33 = bf16[2,2,46080]{2,1,0:T(2,128)(2,1)S(1)} all-to-all(bf16[2,2,46080]{2,1,0:T(2,128)(2,1)S(1)} %reshape.160), channel_id=1, replica_groups=mesh['x'=4,'zh'=4,'core'=2,'expert'=8] {'core'}, dimensions={0} | all-to-all | bytes 737280 | tf_op jit(solution)/shard_map/all_to_all | solution.py:30
  23.9 3.2 %gather_fusion.1 = bf16[320,2560]{1,0:T(8,128)(2,1)} fusion(bf16[256,2560]{1,0:T(8,128)(2,1)S(1)} %multiply_convert_fusion.1, s32[1024]{0:T(1024)S(1)} %pad_clamp_fusion.1), kind=kCustom, calls=%fused_computation.2.clone | custom fusion | bytes 3278080 | tf_op jit(solution)/shard_map/jit(_take)/gather | solution.py:90
  27.1 3.2 %gather_fusion = bf16[320,2560]{1,0:T(8,128)(2,1)} fusion(bf16[256,2560]{1,0:T(8,128)(2,1)S(1)} %copy-done, s32[1024]{0:T(1024)S(1)} %pad_clamp_fusion.1), kind=kCustom, calls=%fused_computation.clone | custom fusion | bytes 3278080 | tf_op jit(solution)/shard_map/jit(_take)/gather | solution.py:90
  36.4 3.7 %all-to-all-start = ((bf16[2,8,40,2560]{3,2,0,1:T(8,128)(2,1)}), bf16[2,8,40,2560]{3,2,0,1:T(8,128)(2,1)S(1)}, u32[]{:S(2)}, u32[]{:S(2)}) async-start(bf16[2,8,40,2560]{3,2,0,1:T(8,128)(2,1)} %pad_maximum_fusion.1), calls=%async_computation | async-start | bytes 6553600 | tf_op jit(solution)/shard_map/all_to_all | solution.py:98
  40.2 95.0 %all-gather.2.cloned.1.call-done = bf16[3,2560,384]{2,1,0:T(8,128)(2,1)} async-done(((bf16[3,160,384]{2,1,0:T(8,128)(2,1)}), bf16[3,2560,384]{2,1,0:T(8,128)(2,1)}) %all-gather.2.cloned.1.call-update) | async-done | bytes 5898256 | tf_op jit(solution)/shard_map/all_gather | solution.py:31
  137.7 3.9 %copy.37 = bf16[2560,320]{1,0:T(8,128)(2,1)} copy(bf16[2560,320]{0,1:T(8,128)(2,1)} %bitcast.108) | data formatting | bytes 3276800 | tf_op jit(solution)/shard_map/dot_general | solution.py:19
  141.6 2.4 copy.38
  144.0 2.7 fusion.6
  149.3 2.5 fusion.10
  151.9 2.5 fusion.7
  154.4 2.5 fusion.5
  158.5 2.2 convert_bitcast_fusion.1
  160.8 2.2 convert_bitcast_fusion.2
  163.0 2.2 convert_bitcast_fusion
  166.7 3.1 dynamic-slice_bitcast_fusion
  169.8 3.1 copy-done.2
  173.0 9.9 %collective-permute-done.1 = bf16[3,16,80,768]{3,2,1,0:T(8,128)(2,1)} collective-permute-done((bf16[3,16,80,768]{3,2,1,0:T(8,128)(2,1)}, bf16[3,16,80,768]{3,2,1,0:T(8,128)(2,1)}, u32[]{:S(2)}, u32[]{:S(2)}) %collective-permute-start.1) | collective-permute-done | bytes 5898272 | tf_op jit(solution)/shard_map/ppermute | solution.py:25
  182.9 8.4 %fusion = bf16[3,16,80,768]{3,2,1,0:T(8,128)(2,1)} fusion(bf16[3,16,80,768]{3,2,1,0:T(8,128)(2,1)} %collective-permute-done.1, bf16[3,16,2,80,768]{4,3,2,1,0:T(8,128)(2,1)} %copy-done.2, s32[]{:T(128)S(6)} %select_n.33), kind=kLoop, calls=%fused_computation.8 | loop fusion | flops 11796480 | bytes 17694724 | tf_op jit(solution)/shard_map/convert_element_type | solution.py:45
  191.3 2.6 fusion.9
  193.9 3.8 %fusion.1 = bf16[320,2560]{1,0:T(8,128)(2,1)} fusion(f32[320,2560]{1,0:T(8,128)S(1)} %fusion.9, bf16[3,2560,384]{2,1,0:T(8,128)(2,1)} %collective-permute-done, bf16[320,768]{1,0:T(8,128)(2,1)S(1)} %get-tuple-element.13), kind=kOutput, calls=%fused_computation.14 | convolution fusion | flops 630784000 | bytes 7127040 | tf_op jit(solution)/shard_map/dot_general | solution.py:13
  197.7 4.4 %all-to-all-start.2 = ((bf16[8,40,2560]{2,1,0:T(8,128)(2,1)}), bf16[8,40,2560]{2,1,0:T(8,128)(2,1)S(1)}, u32[]{:S(2)}, u32[]{:S(2)}) async-start(bf16[8,40,2560]{2,1,0:T(8,128)(2,1)} %bitcast.21), calls=%async_computation.2 | async-start | bytes 3276800 | tf_op jit(solution)/shard_map/all_to_all | solution.py:121
  202.2 2.6 fusion.3
  204.8 2.6 convolution_add_fusion.2
  207.4 2.6 convolution_add_fusion.1
  210.0 3.8 %fusion.2 = bf16[320,2560]{1,0:T(8,128)(2,1)} fusion(f32[320,2560]{1,0:T(8,128)S(1)} %convolution_add_fusion.1, bf16[3,2560,384]{2,1,0:T(8,128)(2,1)} %collective-permute-done, bf16[320,768]{1,0:T(8,128)(2,1)S(1)} %get-tuple-element.11), kind=kOutput, calls=%fused_computation.15 | convolution fusion | flops 630784000 | bytes 7127040 | tf_op jit(solution)/shard_map/dot_general | solution.py:13
  213.9 38.3 %all-to-all-done.2 = bf16[8,40,2560]{2,1,0:T(8,128)(2,1)S(1)} async-done(((bf16[8,40,2560]{2,1,0:T(8,128)(2,1)}), bf16[8,40,2560]{2,1,0:T(8,128)(2,1)S(1)}, u32[]{:S(2)}, u32[]{:S(2)}) %all-to-all-start.2) | async-done | bytes 1638432 | tf_op jit(solution)/shard_map/all_to_all | solution.py:121
  252.1 3.9 %all-to-all-start.3 = ((bf16[8,40,2560]{2,1,0:T(8,128)(2,1)}), bf16[8,40,2560]{2,1,0:T(8,128)(2,1)S(1)}, u32[]{:S(2)}, u32[]{:S(2)}) async-start(bf16[8,40,2560]{2,1,0:T(8,128)(2,1)} %bitcast.107), calls=%async_computation.3 | async-start | bytes 3276800 | tf_op jit(solution)/shard_map/all_to_all | solution.py:138
  256.1 2.5 gather_fusion.2
  258.6 27.4 %all-to-all-done.3 = bf16[8,40,2560]{2,1,0:T(8,128)(2,1)S(1)} async-done(((bf16[8,40,2560]{2,1,0:T(8,128)(2,1)}), bf16[8,40,2560]{2,1,0:T(8,128)(2,1)S(1)}, u32[]{:S(2)}, u32[]{:S(2)}) %all-to-all-start.3) | async-done | bytes 1638432 | tf_op jit(solution)/shard_map/all_to_all | solution.py:138
  286.0 2.5 gather_fusion.3
  288.5 2.7 broadcast_select_fusion
  292.6 13.7 %reduce-scatter.2.cloned.1.call-done = bf16[3,80,768]{2,1,0:T(8,128)(2,1)} async-done(((bf16[3,1280,768]{2,1,0:T(8,128)(2,1)}), bf16[3,80,768]{2,1,0:T(8,128)(2,1)}) %reduce-scatter.2.cloned.1.call-update) | async-done | bytes 368656 | tf_op jit(solution)/shard_map/reduce_scatter | solution.py:47
  (64 shorter events, 27.3 us)
Async XLA Ops:
  7.2 19.9 %copy-start = (bf16[256,2560]{1,0:T(8,128)(2,1)S(1)}, bf16[256,2560]{1,0:T(8,128)(2,1)}, u32[]{:S(2)}) copy-start(bf16[256,2560]{1,0:T(8,128)(2,1)} %param.11) | copy-start | bytes 3932164
  7.2 128.0 %all-gather.2.cloned.1.call-start = ((), (), s32[]{:S(2)}) async-start(), calls=%async_computation.5 | async-start | bytes 6266880 | tf_op jit(solution)/shard_map/all_gather | solution.py:31
  10.1 9.8 %copy-start.10 = (s32[256,1]{0,1:T(1,128)S(1)}, s32[256,1]{0,1:T(1,128)}, u32[]{:S(2)}) copy-start(s32[256,1]{0,1:T(1,128)} %param.12) | copy-start | bytes 3076
  10.1 12.2 %copy-start.11 = (s32[256,1]{0,1:T(1,128)S(1)}, s32[256,1]{0,1:T(1,128)}, u32[]{:S(2)}) copy-start(s32[256,1]{0,1:T(1,128)} %param.13) | copy-start | bytes 3076
  27.1 5.3 %copy-start.5 = (bf16[320,2560]{1,0:T(8,128)(2,1)S(1)}, bf16[320,2560]{1,0:T(8,128)(2,1)}, u32[]{:S(2)}) copy-start(bf16[320,2560]{1,0:T(8,128)(2,1)} %gather_fusion.1) | copy-start | bytes 4915204
  36.4 99.3 %all-to-all-start = ((bf16[2,8,40,2560]{3,2,0,1:T(8,128)(2,1)}), bf16[2,8,40,2560]{3,2,0,1:T(8,128)(2,1)S(1)}, u32[]{:S(2)}, u32[]{:S(2)}) async-start(bf16[2,8,40,2560]{3,2,0,1:T(8,128)(2,1)} %pad_maximum_fusion.1), calls=%async_computation | async-start | bytes 6553600 | tf_op jit(solution)/shard_map/all_to_all | solution.py:98
  40.1 266.2 %reduce-scatter.2.cloned.1.call-start = ((), (), s32[]{:S(2)}) async-start(), calls=%async_computation.6 | async-start | bytes 6266880 | tf_op jit(solution)/shard_map/reduce_scatter | solution.py:47
  135.2 14.1 %collective-permute-start = (bf16[3,2560,384]{2,1,0:T(8,128)(2,1)}, bf16[3,2560,384]{2,1,0:T(8,128)(2,1)}, u32[]{:S(2)}, u32[]{:S(2)}) collective-permute-start(bf16[3,2560,384]{2,1,0:T(8,128)(2,1)} %all-gather.2.cloned.1.call-done), channel_id=1, source_target_pairs={{0,8},{8,0},{1,9},{9,1},{2,10},{10,2},{3,11},{11,3},{4,12},{12,4},... | collective-permute-start | bytes 17694728 | tf_op jit(solution)/shard_map/ppermute | solution.py:25
  137.7 3.9 %copy-start.4 = (bf16[1,8,40,2560]{3,2,0,1:T(8,128)(2,1)S(1)}, bf16[1,8,40,2560]{3,2,0,1:T(8,128)(2,1)}, u32[]{:S(2)}) copy-start(bf16[1,8,40,2560]{3,2,0,1:T(8,128)(2,1)} %get-tuple-element.9) | copy-start | bytes 4915204
  141.6 2.4 copy-start.3
  144.0 3.3 %copy-start.6 = (bf16[3,2560,384]{2,1,0:T(8,128)(2,1)S(1)}, bf16[3,2560,384]{2,1,0:T(8,128)(2,1)}, u32[]{:S(2)}) copy-start(bf16[3,2560,384]{2,1,0:T(8,128)(2,1)} %all-gather.2.cloned.1.call-done) | copy-start | bytes 17694724
  157.0 1.5 copy-start.9
  160.8 2.3 copy-start.8
  166.7 6.2 %copy-start.2 = (bf16[3,16,2,80,768]{4,3,2,1,0:T(8,128)(2,1)}, bf16[3,16,2,80,768]{4,3,2,1,0:T(8,128)(2,1)S(1)}, u32[]{:S(2)}) copy-start(bf16[3,16,2,80,768]{4,3,2,1,0:T(8,128)(2,1)S(1)} %pad_maximum_fusion) | copy-start | bytes 35389444
  172.9 9.9 %collective-permute-start.1 = (bf16[3,16,80,768]{3,2,1,0:T(8,128)(2,1)}, bf16[3,16,80,768]{3,2,1,0:T(8,128)(2,1)}, u32[]{:S(2)}, u32[]{:S(2)}) collective-permute-start(bf16[3,16,80,768]{3,2,1,0:T(8,128)(2,1)} %dynamic-slice_bitcast_fusion), channel_id=1, source_target_pairs={{0,8},{8,0},{1,9},{9,1},{2,10},{10,2},{3,11},{11,3},{4,12},{12,4},... | collective-permute-start | bytes 17694728 | tf_op jit(solution)/shard_map/ppermute | solution.py:25
  197.7 54.4 %all-to-all-start.2 = ((bf16[8,40,2560]{2,1,0:T(8,128)(2,1)}), bf16[8,40,2560]{2,1,0:T(8,128)(2,1)S(1)}, u32[]{:S(2)}, u32[]{:S(2)}) async-start(bf16[8,40,2560]{2,1,0:T(8,128)(2,1)} %bitcast.21), calls=%async_computation.2 | async-start | bytes 3276800 | tf_op jit(solution)/shard_map/all_to_all | solution.py:121
  252.1 33.8 %all-to-all-start.3 = ((bf16[8,40,2560]{2,1,0:T(8,128)(2,1)}), bf16[8,40,2560]{2,1,0:T(8,128)(2,1)S(1)}, u32[]{:S(2)}, u32[]{:S(2)}) async-start(bf16[8,40,2560]{2,1,0:T(8,128)(2,1)} %bitcast.107), calls=%async_computation.3 | async-start | bytes 3276800 | tf_op jit(solution)/shard_map/all_to_all | solution.py:138
  288.5 2.7 copy-start.7
  288.5 19.8 %copy-start.1 = (bf16[256,2560]{1,0:T(8,128)(2,1)S(1)}, bf16[256,2560]{1,0:T(8,128)(2,1)}, u32[]{:S(2)}) copy-start(bf16[256,2560]{1,0:T(8,128)(2,1)} %param.11) | copy-start | bytes 3932164
Sparse Core Ops, SparseCore 0:
  20.0 115.1 all-gather.1
  191.4 114.8 reduce-scatter.1

commit v4 on v2

--- a/solution.py
+++ b/solution.py
@@ -34,13 +34,26 @@
 
 
 def scatter_grads(*parts):
-    own = jnp.stack([p[0] for p in parts]).astype(jnp.bfloat16)
-    other = jnp.stack([p[1] for p in parts]).astype(jnp.bfloat16)
-    arrived = swap_cores(other)
-    pair_sum = (own.astype(jnp.float32) + arrived.astype(jnp.float32)).astype(jnp.bfloat16)
-    chip_sum = lax.psum_scatter(pair_sum, CHIPS, scatter_dimension=1, tiled=True)
-    block = lax.all_to_all(chip_sum, "core", split_axis=1, concat_axis=2, tiled=True)
-    block = block.astype(jnp.float32)
+    pair_sums = []
+    for own, other in parts:
+        arrived = swap_cores(other.astype(jnp.bfloat16))
+        pair_sums.append(
+            (own.astype(jnp.bfloat16).astype(jnp.float32) + arrived.astype(jnp.float32)).astype(
+                jnp.bfloat16
+            )
+        )
+    chip_sum = lax.psum_scatter(jnp.stack(pair_sums), CHIPS, scatter_dimension=1, tiled=True)
+    first = lax.axis_index("core") == 0
+    rows = chip_sum.shape[1] // 2
+
+    def my_rows(value):
+        return jnp.where(first, value[:, :rows], value[:, rows:]).astype(jnp.float32)
+
+    mine = my_rows(chip_sum)
+    theirs = my_rows(swap_cores(chip_sum))
+    block = jnp.where(
+        first, jnp.concatenate([mine, theirs], axis=2), jnp.concatenate([theirs, mine], axis=2)
+    )
     return [block[i] for i in range(len(parts))]
 
 

time: 309 us -> 300 us (0.971)
  blocking collectives: 12.5 us -> 6.89 us
  local copies, waits for them, and re-layouts: 24.7 us -> 20.3 us
    all_to_all x1 -> x0, blocking collectives: 5.65 us -> none  [scatter_grads(): lax.all_to_all(chip_sum, 'core', split_axis=1, concat_axis=2, tiled=True)]
    convert_element_type x2, other arithmetic: 3.94 us -> 0.06 us  [my_rows(): jnp.where(first, value[:, :rows], value[:, rows:]).astype(jnp.float32)]
  transfers between devices with their start and end apart: 8 -> 11, of which waited for: 6 -> 8; matrix products, arithmetic and copies ran while one was open for 18% -> 19% of each run, Pallas kernels for 0% -> 0%
where the time goes in v4:
time: 300 us; the launch traced here: 299 us
  waiting for transfers between devices  177 us (59%)
  matrix products  44.2 us (15%)
  starting transfers between devices  20.8 us (7%)
  local copies, waits for them, and re-layouts  20.3 us (7%)
  other arithmetic  15.4 us (5%)
  between operations  14.4 us (5%)
  blocking collectives  6.89 us (2%)
    all_gather x1, waiting for transfers between devices, gather_weights(): own = lax.all_gather(own, CHIPS, axis=1, tiled=True)  78.8 us
    all_to_all x1, waiting for transfers between devices, shards(): lax.all_to_all(expert_out, 'expert', split_axis=0, concat_axis=0, tiled=T...  39.9 us
    all_to_all x1, waiting for transfers between devices, shards(): lax.all_to_all(token_grad.reshape(experts, capacity, model_width), 'exper...  25.9 us
    dot_general x6, matrix products, contract_last(): lax.dot_general(matrix_a, matrix_b, (((1,), (1,)), ((), ())), preferred_e...  18.1 us
    reduce_scatter x1, waiting for transfers between devices, scatter_grads(): lax.psum_scatter(jnp.stack(pair_sums), CHIPS, scatter_dimension=1, tiled=...  15.1 us
    all_to_all x1, waiting for transfers between devices, shards(): lax.all_to_all(pack_rows(out_grad), 'expert', split_axis=0, concat_axis=0...  14.4 us
    dot_general x3, matrix products, halves(): lax.dot_general(left, pair[0], dims, preferred_element_type=jnp.float32)  9.8 us
    dot_general x6, matrix products, contract_first(): lax.dot_general(matrix_a, matrix_b, (((0,), (0,)), ((), ())), preferred_e...  8.6 us
  transfers between devices with their start and end apart: 11, of which 8 were waited for; matrix products, arithmetic and copies ran while one was open for 19% of the time, Pallas kernels for 0%

profile of v4, /device:TPU:1, one launch (start us, length us, event | category | flops | bytes accessed | tf_op | source)
XLA Modules:
  0.0 299.0 jit_solution(10449711788493079326)
XLA Ops:
  10.1 6.9 %all_to_all.38 = bf16[2,2,46080]{2,1,0:T(2,128)(2,1)S(1)} all-to-all(bf16[2,2,46080]{2,1,0:T(2,128)(2,1)S(1)} %reshape.138), channel_id=1, replica_groups=mesh['x'=4,'zh'=4,'core'=2,'expert'=8] {'core'}, dimensions={0} | all-to-all | bytes 737280 | tf_op jit(solution)/shard_map/all_to_all | solution.py:30
  22.3 1.6 multiply_convert_fusion
  23.9 3.2 %gather_fusion.2 = bf16[320,2560]{1,0:T(8,128)(2,1)} fusion(bf16[256,2560]{1,0:T(8,128)(2,1)S(1)} %multiply_convert_fusion, s32[1024]{0:T(1024)S(1)} %pad_clamp_fusion.1), kind=kCustom, calls=%fused_computation.2.clone | custom fusion | bytes 3278080 | tf_op jit(solution)/shard_map/jit(_take)/gather | solution.py:91
  27.1 3.2 %gather_fusion = bf16[320,2560]{1,0:T(8,128)(2,1)} fusion(bf16[256,2560]{1,0:T(8,128)(2,1)S(1)} %copy-done, s32[1024]{0:T(1024)S(1)} %pad_clamp_fusion.1), kind=kCustom, calls=%fused_computation.clone | custom fusion | bytes 3278080 | tf_op jit(solution)/shard_map/jit(_take)/gather | solution.py:91
  30.3 2.2 scatter_custom_fusion.1
  32.5 3.7 %select_multiply_fusion = (bf16[320,2560]{1,0:T(8,128)(2,1)}, bf16[320,2560]{1,0:T(8,128)(2,1)}) fusion(bf16[320,2560]{1,0:T(8,128)(2,1)S(1)} %copy-done.2, pred[320]{0:T(512)(128)(4,1)S(1)} %compare_and_fusion.1, bf16[320]{0:T(512)(128)(2,1)S(1)} %scatter_custom_fusion.1, bf16[320,2560]{1,0:T(8,128)(2,1)} %gather_fusion), kind=kLoop, calls=%fused_computation.44 | loop fusion | flops 3276800 | bytes 6554560 | tf_op jit(solution)/shard_map/mul | solution.py:91
  36.1 3.7 %all-to-all-start = ((bf16[8,40,2560]{2,1,0:T(8,128)(2,1)}), bf16[8,40,2560]{2,1,0:T(8,128)(2,1)S(1)}, u32[]{:S(2)}, u32[]{:S(2)}) async-start(bf16[8,40,2560]{2,1,0:T(8,128)(2,1)} %bitcast.7), calls=%async_computation | async-start | bytes 3276800 | tf_op jit(solution)/shard_map/all_to_all | solution.py:98
  39.9 78.8 %all-gather.2.cloned.1.call-done = bf16[3,2560,384]{2,1,0:T(8,128)(2,1)} async-done(((bf16[3,160,384]{2,1,0:T(8,128)(2,1)}), bf16[3,2560,384]{2,1,0:T(8,128)(2,1)}) %all-gather.2.cloned.1.call-update) | async-done | bytes 5898256 | tf_op jit(solution)/shard_map/all_gather | solution.py:31
  119.1 4.4 %all-to-all-start.3 = ((bf16[8,40,2560]{2,1,0:T(8,128)(2,1)}), bf16[8,40,2560]{2,1,0:T(8,128)(2,1)S(1)}, u32[]{:S(2)}, u32[]{:S(2)}) async-start(bf16[8,40,2560]{2,1,0:T(8,128)(2,1)} %bitcast.20), calls=%async_computation.3 | async-start | bytes 3276800 | tf_op jit(solution)/shard_map/all_to_all | solution.py:122
  123.7 3.3 %fusion.9 = f32[320,384]{1,0:T(8,128)} fusion(bf16[320,2560]{1,0:T(8,128)(2,1)S(1)} %bitcast.73, bf16[3,2560,384]{2,1,0:T(8,128)(2,1)} %all-gather.2.cloned.1.call-done), kind=kOutput, calls=%fused_computation.37 | convolution fusion | flops 629145600 | bytes 4096000 | tf_op jit(solution)/shard_map/dot_general | solution.py:62
  127.1 3.3 %fusion.11 = f32[320,384]{1,0:T(8,128)} fusion(bf16[320,2560]{1,0:T(8,128)(2,1)S(1)} %bitcast.74, bf16[3,2560,384]{2,1,0:T(8,128)(2,1)} %all-gather.2.cloned.1.call-done), kind=kOutput, calls=%fused_computation.39 | convolution fusion | flops 629145600 | bytes 4096000 | tf_op jit(solution)/shard_map/dot_general | solution.py:62
  130.4 14.4 %all-to-all-done.3 = bf16[8,40,2560]{2,1,0:T(8,128)(2,1)S(1)} async-done(((bf16[8,40,2560]{2,1,0:T(8,128)(2,1)}), bf16[8,40,2560]{2,1,0:T(8,128)(2,1)S(1)}, u32[]{:S(2)}, u32[]{:S(2)}) %all-to-all-start.3) | async-done | bytes 1638432 | tf_op jit(solution)/shard_map/all_to_all | solution.py:122
  144.8 3.1 %fusion.13 = f32[320,384]{1,0:T(8,128)S(1)} fusion(bf16[320,2560]{1,0:T(8,128)(2,1)S(1)} %bitcast.81, bf16[3,2560,384]{2,1,0:T(8,128)(2,1)} %all-gather.2.cloned.1.call-done), kind=kOutput, calls=%fused_computation.41 | convolution fusion | flops 629145600 | bytes 4096000 | tf_op jit(solution)/shard_map/dot_general | solution.py:62
  148.0 2.5 fusion.15
  150.5 2.5 fusion.10
  153.1 2.6 fusion.12
  165.9 1.5 fusion.6
  170.2 3.3 %pad_maximum_fusion = bf16[3,2560,384]{2,1,0:T(8,128)(2,1)} fusion(bf16[1,2560,384]{2,1,0:T(8,128)(2,1)S(1)} %fusion.7, bf16[1,2560,384]{2,1,0:T(8,128)(2,1)S(1)} %fusion.6, bf16[1,2560,384]{2,1,0:T(8,128)(2,1)S(1)} %fusion.5), kind=kLoop, calls=%fused_computation.6 | loop fusion | flops 5898240 | bytes 11796480 | tf_op jit(solution)/shard_map/stack | solution.py:45
  173.5 2.6 fusion.14
  176.1 3.8 %fusion.3 = bf16[320,2560]{1,0:T(8,128)(2,1)} fusion(f32[320,2560]{1,0:T(8,128)S(1)} %fusion.14, bf16[3,2560,384]{2,1,0:T(8,128)(2,1)} %collective-permute-done, bf16[320,768]{1,0:T(8,128)(2,1)S(1)} %get-tuple-element.11), kind=kOutput, calls=%fused_computation.20 | convolution fusion | flops 630784000 | bytes 7127040 | tf_op jit(solution)/shard_map/dot_general | solution.py:13
  180.0 3.7 %all-to-all-start.2 = ((bf16[8,40,2560]{2,1,0:T(8,128)(2,1)}), bf16[8,40,2560]{2,1,0:T(8,128)(2,1)S(1)}, u32[]{:S(2)}, u32[]{:S(2)}) async-start(bf16[8,40,2560]{2,1,0:T(8,128)(2,1)} %bitcast.18), calls=%async_computation.2 | async-start | bytes 3276800 | tf_op jit(solution)/shard_map/all_to_all | solution.py:115
  183.7 2.6 fusion.8
  186.2 2.6 convolution_add_fusion.2
  188.9 2.6 convolution_add_fusion.1
  191.5 3.8 %fusion.4 = bf16[320,2560]{1,0:T(8,128)(2,1)} fusion(f32[320,2560]{1,0:T(8,128)S(1)} %convolution_add_fusion.1, bf16[3,2560,384]{2,1,0:T(8,128)(2,1)} %collective-permute-done, bf16[320,768]{1,0:T(8,128)(2,1)S(1)} %get-tuple-element.9), kind=kOutput, calls=%fused_computation.21 | convolution fusion | flops 630784000 | bytes 7127040 | tf_op jit(solution)/shard_map/dot_general | solution.py:13
  195.4 39.9 %all-to-all-done.2 = bf16[8,40,2560]{2,1,0:T(8,128)(2,1)S(1)} async-done(((bf16[8,40,2560]{2,1,0:T(8,128)(2,1)}), bf16[8,40,2560]{2,1,0:T(8,128)(2,1)S(1)}, u32[]{:S(2)}, u32[]{:S(2)}) %all-to-all-start.2) | async-done | bytes 1638432 | tf_op jit(solution)/shard_map/all_to_all | solution.py:115
  235.3 4.6 %all-to-all-start.4 = ((bf16[8,40,2560]{2,1,0:T(8,128)(2,1)}), bf16[8,40,2560]{2,1,0:T(8,128)(2,1)S(1)}, u32[]{:S(2)}, u32[]{:S(2)}) async-start(bf16[8,40,2560]{2,1,0:T(8,128)(2,1)} %bitcast.70), calls=%async_computation.4 | async-start | bytes 3276800 | tf_op jit(solution)/shard_map/all_to_all | solution.py:136
  239.9 2.5 gather_fusion.1
  242.4 25.9 %all-to-all-done.4 = bf16[8,40,2560]{2,1,0:T(8,128)(2,1)S(1)} async-done(((bf16[8,40,2560]{2,1,0:T(8,128)(2,1)}), bf16[8,40,2560]{2,1,0:T(8,128)(2,1)S(1)}, u32[]{:S(2)}, u32[]{:S(2)}) %all-to-all-start.4) | async-done | bytes 1638432 | tf_op jit(solution)/shard_map/all_to_all | solution.py:136
  269.8 2.8 multiply_convert_fusion.1
  272.5 15.1 %reduce-scatter.2.cloned.1.call-done = bf16[3,160,384]{2,1,0:T(8,128)(2,1)} async-done(((bf16[3,2560,384]{2,1,0:T(8,128)(2,1)}), bf16[3,160,384]{2,1,0:T(8,128)(2,1)}) %reduce-scatter.2.cloned.1.call-update) | async-done | bytes 368656 | tf_op jit(solution)/shard_map/reduce_scatter | solution.py:45
  287.7 1.9 collective-permute-start.4
  (72 shorter events, 25.7 us)
Async XLA Ops:
  7.2 19.9 %copy-start = (bf16[256,2560]{1,0:T(8,128)(2,1)S(1)}, bf16[256,2560]{1,0:T(8,128)(2,1)}, u32[]{:S(2)}) copy-start(bf16[256,2560]{1,0:T(8,128)(2,1)} %param.11) | copy-start | bytes 3932164
  7.2 111.5 %all-gather.2.cloned.1.call-start = ((), (), s32[]{:S(2)}) async-start(), calls=%async_computation.6 | async-start | bytes 6266880 | tf_op jit(solution)/shard_map/all_gather | solution.py:31
  10.1 9.8 %copy-start.10 = (s32[256,1]{0,1:T(1,128)S(1)}, s32[256,1]{0,1:T(1,128)}, u32[]{:S(2)}) copy-start(s32[256,1]{0,1:T(1,128)} %param.12) | copy-start | bytes 3076
  10.1 12.2 %copy-start.11 = (s32[256,1]{0,1:T(1,128)S(1)}, s32[256,1]{0,1:T(1,128)}, u32[]{:S(2)}) copy-start(s32[256,1]{0,1:T(1,128)} %param.13) | copy-start | bytes 3076
  27.1 5.3 %copy-start.2 = (bf16[320,2560]{1,0:T(8,128)(2,1)S(1)}, bf16[320,2560]{1,0:T(8,128)(2,1)}, u32[]{:S(2)}) copy-start(bf16[320,2560]{1,0:T(8,128)(2,1)} %gather_fusion.2) | copy-start | bytes 4915204
  36.1 83.0 %all-to-all-start = ((bf16[8,40,2560]{2,1,0:T(8,128)(2,1)}), bf16[8,40,2560]{2,1,0:T(8,128)(2,1)S(1)}, u32[]{:S(2)}, u32[]{:S(2)}) async-start(bf16[8,40,2560]{2,1,0:T(8,128)(2,1)} %bitcast.7), calls=%async_computation | async-start | bytes 3276800 | tf_op jit(solution)/shard_map/all_to_all | solution.py:98
  118.7 29.3 %collective-permute-start = (bf16[3,2560,384]{2,1,0:T(8,128)(2,1)}, bf16[3,2560,384]{2,1,0:T(8,128)(2,1)}, u32[]{:S(2)}, u32[]{:S(2)}) collective-permute-start(bf16[3,2560,384]{2,1,0:T(8,128)(2,1)} %all-gather.2.cloned.1.call-done), channel_id=1, source_target_pairs={{0,8},{8,0},{1,9},{9,1},{2,10},{10,2},{3,11},{11,3},{4,12},{12,4},... | collective-permute-start | bytes 17694728 | tf_op jit(solution)/shard_map/ppermute | solution.py:25
  119.1 34.0 %copy-start.3 = (bf16[8,40,2560]{2,1,0:T(8,128)(2,1)}, bf16[8,40,2560]{2,1,0:T(8,128)(2,1)S(1)}, u32[]{:S(2)}) copy-start(bf16[8,40,2560]{2,1,0:T(8,128)(2,1)S(1)} %all-to-all-done) | copy-start | bytes 4915204
  119.1 25.7 %all-to-all-start.3 = ((bf16[8,40,2560]{2,1,0:T(8,128)(2,1)}), bf16[8,40,2560]{2,1,0:T(8,128)(2,1)S(1)}, u32[]{:S(2)}, u32[]{:S(2)}) async-start(bf16[8,40,2560]{2,1,0:T(8,128)(2,1)} %bitcast.20), calls=%async_computation.3 | async-start | bytes 3276800 | tf_op jit(solution)/shard_map/all_to_all | solution.py:122
  123.5 164.2 %reduce-scatter.2.cloned.1.call-start = ((), (), s32[]{:S(2)}) async-start(), calls=%async_computation.7 | async-start | bytes 6266880 | tf_op jit(solution)/shard_map/reduce_scatter | solution.py:45
  144.8 3.2 %copy-start.5 = (bf16[8,40,2560]{2,1,0:T(8,128)(2,1)}, bf16[8,40,2560]{2,1,0:T(8,128)(2,1)S(1)}, u32[]{:S(2)}) copy-start(bf16[8,40,2560]{2,1,0:T(8,128)(2,1)S(1)} %all-to-all-done.3) | copy-start | bytes 4915204
  153.1 2.7 copy-start.7
  153.1 2.7 copy-start.8
  155.8 1.4 copy-start.6
  157.2 2.3 copy-start.4
  158.6 4.6 %collective-permute-start.3 = (bf16[2560,384]{1,0:T(8,128)(2,1)S(1)}, bf16[2560,384]{1,0:T(8,128)(2,1)S(1)}, u32[]{:S(2)}, u32[]{:S(2)}) collective-permute-start(bf16[2560,384]{1,0:T(8,128)(2,1)S(1)} %convolution_convert_fusion), channel_id=1, source_target_pairs={{0,8},{8,0},{1,9},{9,1},{2,10},{10,2},{3,11},{11,3},{4,12},{12,4},... | collective-permute-start | bytes 5898248 | tf_op jit(solution)/shard_map/ppermute | solution.py:25
  160.9 5.0 %collective-permute-start.2 = (bf16[2560,384]{1,0:T(8,128)(2,1)S(1)}, bf16[2560,384]{1,0:T(8,128)(2,1)S(1)}, u32[]{:S(2)}, u32[]{:S(2)}) collective-permute-start(bf16[2560,384]{1,0:T(8,128)(2,1)S(1)} %convolution_convert_fusion.2), channel_id=1, source_target_pairs={{0,8},{8,0},{1,9},{9,1},{2,10},{10,2},{3,11},{11,3},{4,12},{12,4},... | collective-permute-start | bytes 5898248 | tf_op jit(solution)/shard_map/ppermute | solution.py:25
  162.4 6.3 %collective-permute-start.1 = (bf16[2560,384]{1,0:T(8,128)(2,1)S(1)}, bf16[2560,384]{1,0:T(8,128)(2,1)S(1)}, u32[]{:S(2)}, u32[]{:S(2)}) collective-permute-start(bf16[2560,384]{1,0:T(8,128)(2,1)S(1)} %convolution_convert_fusion.4), channel_id=1, source_target_pairs={{0,8},{8,0},{1,9},{9,1},{2,10},{10,2},{3,11},{11,3},{4,12},{12,4},... | collective-permute-start | bytes 5898248 | tf_op jit(solution)/shard_map/ppermute | solution.py:25
  180.0 55.3 %all-to-all-start.2 = ((bf16[8,40,2560]{2,1,0:T(8,128)(2,1)}), bf16[8,40,2560]{2,1,0:T(8,128)(2,1)S(1)}, u32[]{:S(2)}, u32[]{:S(2)}) async-start(bf16[8,40,2560]{2,1,0:T(8,128)(2,1)} %bitcast.18), calls=%async_computation.2 | async-start | bytes 3276800 | tf_op jit(solution)/shard_map/all_to_all | solution.py:115
  235.3 33.0 %all-to-all-start.4 = ((bf16[8,40,2560]{2,1,0:T(8,128)(2,1)}), bf16[8,40,2560]{2,1,0:T(8,128)(2,1)S(1)}, u32[]{:S(2)}, u32[]{:S(2)}) async-start(bf16[8,40,2560]{2,1,0:T(8,128)(2,1)} %bitcast.70), calls=%async_computation.4 | async-start | bytes 3276800 | tf_op jit(solution)/shard_map/all_to_all | solution.py:136
  287.7 3.2 %copy-start.9 = (bf16[3,160,384]{2,1,0:T(8,128)(2,1)S(1)}, bf16[3,160,384]{2,1,0:T(8,128)(2,1)}, u32[]{:S(2)}) copy-start(bf16[3,160,384]{2,1,0:T(8,128)(2,1)} %reduce-scatter.2.cloned.1.call-done) | copy-start | bytes 1105924
  287.7 3.5 %collective-permute-start.4 = (bf16[3,160,384]{2,1,0:T(8,128)(2,1)}, bf16[3,160,384]{2,1,0:T(8,128)(2,1)S(1)}, u32[]{:S(2)}, u32[]{:S(2)}) collective-permute-start(bf16[3,160,384]{2,1,0:T(8,128)(2,1)} %reduce-scatter.2.cloned.1.call-done), channel_id=1, source_target_pairs={{0,8},{8,0},{1,9},{9,1},{2,10},{10,2},{3,11},{11,3},{4,12},{12,4},... | collective-permute-start | bytes 1105928 | tf_op jit(solution)/shard_map/ppermute | solution.py:25
  290.9 1.3 copy-start.1
Sparse Core Ops, SparseCore 0:
  20.0 98.5 all-gather.1
  173.7 113.9 reduce-scatter.1

commit v5 on v4

--- a/solution.py
+++ b/solution.py
@@ -27,7 +27,14 @@
 
 def gather_weights(*weights):
     stacked = jnp.stack(weights)
-    own = lax.all_to_all(stacked, "core", split_axis=2, concat_axis=1, tiled=True)
+    half = stacked.shape[2] // 2
+    first = lax.axis_index("core") == 0
+    kept = jnp.where(first, stacked[:, :, :half], stacked[:, :, half:])
+    sent = jnp.where(first, stacked[:, :, half:], stacked[:, :, :half])
+    came = swap_cores(sent)
+    own = jnp.where(
+        first, jnp.concatenate([kept, came], axis=1), jnp.concatenate([came, kept], axis=1)
+    )
     own = lax.all_gather(own, CHIPS, axis=1, tiled=True)
     other = swap_cores(own)
     return [(own[i], other[i]) for i in range(len(weights))]
@@ -95,9 +102,16 @@
     gate_pair, up_pair, down_pair = gather_weights(w_gate[0], w_up[0], w_down[0])
     plain = (((1,), (0,)), ((), ()))
     last = (((1,), (1,)), ((), ()))
-    received = lax.all_to_all(
-        pack_rows(tokens), "expert", split_axis=0, concat_axis=0, tiled=True
-    ).reshape(slot_count, model_width)
+    out_grad = (gate_weight * grad_out.astype(jnp.float32)).astype(jnp.bfloat16)
+    both_rows = lax.all_to_all(
+        jnp.stack([pack_rows(tokens), pack_rows(out_grad)]),
+        "expert",
+        split_axis=1,
+        concat_axis=1,
+        tiled=True,
+    )
+    received = both_rows[0].reshape(slot_count, model_width)
+    grad_rows = both_rows[1].reshape(slot_count, model_width)
     act_gate = jnp.concatenate(halves(received, gate_pair, plain), axis=1)
     act_up = jnp.concatenate(halves(received, up_pair, plain), axis=1)
     sigmoid_gate = jax.nn.sigmoid(act_gate)
@@ -118,10 +132,6 @@
     moe_out = (gate_weight * jnp.take(returned, slot_index, axis=0).astype(jnp.float32)).astype(
         jnp.bfloat16
     )
-    out_grad = (gate_weight * grad_out.astype(jnp.float32)).astype(jnp.bfloat16)
-    grad_rows = lax.all_to_all(
-        pack_rows(out_grad), "expert", split_axis=0, concat_axis=0, tiled=True
-    ).reshape(slot_count, model_width)
     hidden_grad = jnp.concatenate(halves(grad_rows, down_pair, plain), axis=1)
     gate_delta = (
         hidden_grad * act_up * sigmoid_gate * (1.0 + act_gate * (1.0 - sigmoid_gate))

time: 300 us -> 291 us (0.970)
  waiting for transfers between devices: 177 us -> 184 us
  blocking collectives: 6.89 us -> 0 us
  matrix products: 44.2 us -> 37.4 us
    all_gather x1, waiting for transfers between devices: 78.8 us -> 95.6 us  [gather_weights(): own = lax.all_gather(own, CHIPS, axis=1, tiled=True)]
    all_to_all x2 -> x1, waiting for transfers between devices: 14.4 us -> 0.01 us  [shards(): lax.all_to_all(jnp.stack([pack_rows(tokens), pack_rows(out_grad)]), 'expe...]
    all_to_all x1 -> x0, blocking collectives: 6.89 us -> none  [gather_weights(): lax.all_to_all(stacked, 'core', split_axis=2, concat_axis=1, tiled=True)]
    dot_general x3, matrix products: 9.8 us -> 3.01 us  [halves(): lax.dot_general(left, pair[0], dims, preferred_element_type=jnp.float32)]
    ppermute x5 -> x6, waiting for transfers between devices: 2.79 us -> 7.71 us  [swap_cores(): return lax.ppermute(value, 'core', perm=[(0, 1), (1, 0)])]
    all_to_all x2 -> x1, starting transfers between devices: 8.09 us -> 3.74 us  [shards(): lax.all_to_all(jnp.stack([pack_rows(tokens), pack_rows(out_grad)]), 'expe...]
    ppermute x5 -> x6, starting transfers between devices: 4.15 us -> 6.79 us  [swap_cores(): return lax.ppermute(value, 'core', perm=[(0, 1), (1, 0)])]
  transfers between devices with their start and end apart: 11 -> 11, of which waited for: 8 -> 9; matrix products, arithmetic and copies ran while one was open for 19% -> 18% of each run, Pallas kernels for 0% -> 0%
where the time goes in v5:
time: 291 us; the launch traced here: 290 us
  waiting for transfers between devices  184 us (63%)
  matrix products  37.4 us (13%)
  local copies, waits for them, and re-layouts  19.9 us (7%)
  starting transfers between devices  19 us (7%)
  other arithmetic  15.5 us (5%)
  between operations  14.4 us (5%)
    all_gather x1, waiting for transfers between devices, gather_weights(): own = lax.all_gather(own, CHIPS, axis=1, tiled=True)  95.6 us
    all_to_all x1, waiting for transfers between devices, shards(): lax.all_to_all(expert_out, 'expert', split_axis=0, concat_axis=0, tiled=T...  38.2 us
    all_to_all x1, waiting for transfers between devices, shards(): lax.all_to_all(token_grad.reshape(experts, capacity, model_width), 'exper...  27.5 us
    dot_general x6, matrix products, contract_last(): lax.dot_general(matrix_a, matrix_b, (((1,), (1,)), ((), ())), preferred_e...  18.1 us
    reduce_scatter x1, waiting for transfers between devices, scatter_grads(): lax.psum_scatter(jnp.stack(pair_sums), CHIPS, scatter_dimension=1, tiled=...  14.7 us
    dot_general x6, matrix products, contract_first(): lax.dot_general(matrix_a, matrix_b, (((0,), (0,)), ((), ())), preferred_e...  8.6 us
    ppermute x6, waiting for transfers between devices, swap_cores(): return lax.ppermute(value, 'core', perm=[(0, 1), (1, 0)])  7.71 us
    dot_general x3, matrix products, halves(): lax.dot_general(left, pair[1], dims, preferred_element_type=jnp.float32)  7.64 us
  transfers between devices with their start and end apart: 11, of which 9 were waited for; matrix products, arithmetic and copies ran while one was open for 18% of the time, Pallas kernels for 0%

profile of v5, /device:TPU:1, one launch (start us, length us, event | category | flops | bytes accessed | tf_op | source)
XLA Modules:
  0.0 289.8 jit_solution(14229457043966567120)
XLA Ops:
  10.1 3.3 %collective-permute-start = (bf16[3,80,384]{2,1,0:T(8,128)(2,1)S(1)}, bf16[3,80,384]{2,1,0:T(8,128)(2,1)S(1)}, u32[]{:S(2)}, u32[]{:S(2)}) collective-permute-start(bf16[3,80,384]{2,1,0:T(8,128)(2,1)S(1)} %get-tuple-element.18), channel_id=1, source_target_pairs={{0,8},{8,0},{1,9},{9,1},{2,10},{10,2},{3,11},{11,3},{4,12},{12,4},... | collective-permute-start | bytes 552968 | tf_op jit(solution)/shard_map/ppermute | solution.py:25
  17.8 2.6 gather_fusion
  20.4 1.6 multiply_convert_fusion.1
  22.0 3.2 %gather_fusion.1 = bf16[320,2560]{1,0:T(8,128)(2,1)} fusion(bf16[256,2560]{1,0:T(8,128)(2,1)S(1)} %multiply_convert_fusion.1, s32[1024]{0:T(1024)S(1)} %pad_clamp_fusion.1), kind=kCustom, calls=%fused_computation.2.clone | custom fusion | bytes 3278080 | tf_op jit(solution)/shard_map/jit(_take)/gather | solution.py:98
  25.2 2.2 scatter_custom_fusion.1
  27.4 1.9 select_multiply_fusion.1
  29.3 2.0 pad_maximum_fusion.1
  31.3 3.7 %all-to-all-start = ((bf16[2,8,40,2560]{3,2,0,1:T(8,128)(2,1)}), bf16[2,8,40,2560]{3,2,0,1:T(8,128)(2,1)S(1)}, u32[]{:S(2)}, u32[]{:S(2)}) async-start(bf16[2,8,40,2560]{3,2,0,1:T(8,128)(2,1)} %pad_maximum_fusion.1), calls=%async_computation | async-start | bytes 6553600 | tf_op jit(solution)/shard_map/all_to_all | solution.py:106
  35.1 95.6 %all-gather.2.cloned.1.call-done = bf16[3,2560,384]{2,1,0:T(8,128)(2,1)} async-done(((bf16[3,160,384]{2,1,0:T(8,128)(2,1)}), bf16[3,2560,384]{2,1,0:T(8,128)(2,1)}) %all-gather.2.cloned.1.call-update) | async-done | bytes 5898256 | tf_op jit(solution)/shard_map/all_gather | solution.py:38
  131.4 2.4 copy-done.2
  136.8 3.9 %collective-permute-done.1 = bf16[3,2560,384]{2,1,0:T(8,128)(2,1)} collective-permute-done((bf16[3,2560,384]{2,1,0:T(8,128)(2,1)}, bf16[3,2560,384]{2,1,0:T(8,128)(2,1)}, u32[]{:S(2)}, u32[]{:S(2)}) %collective-permute-start.1) | collective-permute-done | bytes 5898272 | tf_op jit(solution)/shard_map/ppermute | solution.py:25
  140.7 2.5 fusion.15
  143.2 2.5 fusion.10
  145.8 2.5 fusion.12
  154.7 1.5 fusion.7
  157.4 1.5 fusion.6
  160.2 1.5 fusion.5
  161.6 3.4 %pad_maximum_fusion = bf16[3,2560,384]{2,1,0:T(8,128)(2,1)} fusion(bf16[1,2560,384]{2,1,0:T(8,128)(2,1)S(1)} %fusion.7, bf16[1,2560,384]{2,1,0:T(8,128)(2,1)S(1)} %fusion.6, bf16[1,2560,384]{2,1,0:T(8,128)(2,1)S(1)} %fusion.5), kind=kLoop, calls=%fused_computation.6 | loop fusion | flops 5898240 | bytes 11796480 | tf_op jit(solution)/shard_map/stack | solution.py:52
  165.1 2.6 fusion.14
  167.7 3.8 %fusion.3 = bf16[320,2560]{1,0:T(8,128)(2,1)} fusion(f32[320,2560]{1,0:T(8,128)S(1)} %fusion.14, bf16[3,2560,384]{2,1,0:T(8,128)(2,1)} %collective-permute-done.1, bf16[320,768]{1,0:T(8,128)(2,1)S(1)} %get-tuple-element.13), kind=kOutput, calls=%fused_computation.20 | convolution fusion | flops 630784000 | bytes 7127040 | tf_op jit(solution)/shard_map/dot_general | solution.py:13
  171.5 4.5 %all-to-all-start.1 = ((bf16[8,40,2560]{2,1,0:T(8,128)(2,1)}), bf16[8,40,2560]{2,1,0:T(8,128)(2,1)S(1)}, u32[]{:S(2)}, u32[]{:S(2)}) async-start(bf16[8,40,2560]{2,1,0:T(8,128)(2,1)} %bitcast.18), calls=%async_computation.1 | async-start | bytes 3276800 | tf_op jit(solution)/shard_map/all_to_all | solution.py:129
  176.0 2.6 fusion.8
  178.6 2.6 convolution_add_fusion.2
  181.2 2.6 convolution_add_fusion.1
  183.9 3.8 %fusion.4 = bf16[320,2560]{1,0:T(8,128)(2,1)} fusion(f32[320,2560]{1,0:T(8,128)S(1)} %convolution_add_fusion.1, bf16[3,2560,384]{2,1,0:T(8,128)(2,1)} %collective-permute-done.1, bf16[320,768]{1,0:T(8,128)(2,1)S(1)} %get-tuple-element.11), kind=kOutput, calls=%fused_computation.21 | convolution fusion | flops 630784000 | bytes 7127040 | tf_op jit(solution)/shard_map/dot_general | solution.py:13
  187.7 38.2 %all-to-all-done.1 = bf16[8,40,2560]{2,1,0:T(8,128)(2,1)S(1)} async-done(((bf16[8,40,2560]{2,1,0:T(8,128)(2,1)}), bf16[8,40,2560]{2,1,0:T(8,128)(2,1)S(1)}, u32[]{:S(2)}, u32[]{:S(2)}) %all-to-all-start.1) | async-done | bytes 1638432 | tf_op jit(solution)/shard_map/all_to_all | solution.py:129
  225.9 3.9 %all-to-all-start.2 = ((bf16[8,40,2560]{2,1,0:T(8,128)(2,1)}), bf16[8,40,2560]{2,1,0:T(8,128)(2,1)S(1)}, u32[]{:S(2)}, u32[]{:S(2)}) async-start(bf16[8,40,2560]{2,1,0:T(8,128)(2,1)} %bitcast.69), calls=%async_computation.2 | async-start | bytes 3276800 | tf_op jit(solution)/shard_map/all_to_all | solution.py:146
  229.9 2.5 gather_fusion.2
  232.4 27.5 %all-to-all-done.2 = bf16[8,40,2560]{2,1,0:T(8,128)(2,1)S(1)} async-done(((bf16[8,40,2560]{2,1,0:T(8,128)(2,1)}), bf16[8,40,2560]{2,1,0:T(8,128)(2,1)S(1)}, u32[]{:S(2)}, u32[]{:S(2)}) %all-to-all-start.2) | async-done | bytes 1638432 | tf_op jit(solution)/shard_map/all_to_all | solution.py:146
  261.3 2.8 multiply_convert_fusion
  264.1 14.7 %reduce-scatter.2.cloned.1.call-done = bf16[3,160,384]{2,1,0:T(8,128)(2,1)} async-done(((bf16[3,2560,384]{2,1,0:T(8,128)(2,1)}), bf16[3,160,384]{2,1,0:T(8,128)(2,1)}) %reduce-scatter.2.cloned.1.call-update) | async-done | bytes 368656 | tf_op jit(solution)/shard_map/reduce_scatter | solution.py:52
  278.8 1.6 collective-permute-start.5
  (60 shorter events, 23.9 us)
Async XLA Ops:
  7.2 10.6 %copy-start = (bf16[256,2560]{1,0:T(8,128)(2,1)S(1)}, bf16[256,2560]{1,0:T(8,128)(2,1)}, u32[]{:S(2)}) copy-start(bf16[256,2560]{1,0:T(8,128)(2,1)} %param.11) | copy-start | bytes 3932164
  7.2 8.2 %copy-start.4 = (s32[256,1]{0,1:T(1,128)S(1)}, s32[256,1]{0,1:T(1,128)}, u32[]{:S(2)}) copy-start(s32[256,1]{0,1:T(1,128)} %param.12) | copy-start | bytes 3076
  7.2 123.5 %all-gather.2.cloned.1.call-start = ((), (), s32[]{:S(2)}) async-start(), calls=%async_computation.4 | async-start | bytes 6266880 | tf_op jit(solution)/shard_map/all_gather | solution.py:38
  10.1 4.4 %collective-permute-start = (bf16[3,80,384]{2,1,0:T(8,128)(2,1)S(1)}, bf16[3,80,384]{2,1,0:T(8,128)(2,1)S(1)}, u32[]{:S(2)}, u32[]{:S(2)}) collective-permute-start(bf16[3,80,384]{2,1,0:T(8,128)(2,1)S(1)} %get-tuple-element.18), channel_id=1, source_target_pairs={{0,8},{8,0},{1,9},{9,1},{2,10},{10,2},{3,11},{11,3},{4,12},{12,4},... | collective-permute-start | bytes 552968 | tf_op jit(solution)/shard_map/ppermute | solution.py:25
  17.8 2.6 copy-start.5
  31.3 99.8 %all-to-all-start = ((bf16[2,8,40,2560]{3,2,0,1:T(8,128)(2,1)}), bf16[2,8,40,2560]{3,2,0,1:T(8,128)(2,1)S(1)}, u32[]{:S(2)}, u32[]{:S(2)}) async-start(bf16[2,8,40,2560]{3,2,0,1:T(8,128)(2,1)} %pad_maximum_fusion.1), calls=%async_computation | async-start | bytes 6553600 | tf_op jit(solution)/shard_map/all_to_all | solution.py:106
  35.0 243.8 %reduce-scatter.2.cloned.1.call-start = ((), (), s32[]{:S(2)}) async-start(), calls=%async_computation.5 | async-start | bytes 6266880 | tf_op jit(solution)/shard_map/reduce_scatter | solution.py:52
  130.7 10.0 %collective-permute-start.1 = (bf16[3,2560,384]{2,1,0:T(8,128)(2,1)}, bf16[3,2560,384]{2,1,0:T(8,128)(2,1)}, u32[]{:S(2)}, u32[]{:S(2)}) collective-permute-start(bf16[3,2560,384]{2,1,0:T(8,128)(2,1)} %all-gather.2.cloned.1.call-done), channel_id=1, source_target_pairs={{0,8},{8,0},{1,9},{9,1},{2,10},{10,2},{3,11},{11,3},{4,12},{12,4},... | collective-permute-start | bytes 17694728 | tf_op jit(solution)/shard_map/ppermute | solution.py:25
  131.1 2.7 copy-start.2
  150.5 4.2 %collective-permute-start.4 = (bf16[2560,384]{1,0:T(8,128)(2,1)S(1)}, bf16[2560,384]{1,0:T(8,128)(2,1)S(1)}, u32[]{:S(2)}, u32[]{:S(2)}) collective-permute-start(bf16[2560,384]{1,0:T(8,128)(2,1)S(1)} %convolution_convert_fusion), channel_id=1, source_target_pairs={{0,8},{8,0},{1,9},{9,1},{2,10},{10,2},{3,11},{11,3},{4,12},{12,4},... | collective-permute-start | bytes 5898248 | tf_op jit(solution)/shard_map/ppermute | solution.py:25
  152.4 5.0 %collective-permute-start.3 = (bf16[2560,384]{1,0:T(8,128)(2,1)S(1)}, bf16[2560,384]{1,0:T(8,128)(2,1)S(1)}, u32[]{:S(2)}, u32[]{:S(2)}) collective-permute-start(bf16[2560,384]{1,0:T(8,128)(2,1)S(1)} %convolution_convert_fusion.2), channel_id=1, source_target_pairs={{0,8},{8,0},{1,9},{9,1},{2,10},{10,2},{3,11},{11,3},{4,12},{12,4},... | collective-permute-start | bytes 5898248 | tf_op jit(solution)/shard_map/ppermute | solution.py:25
  154.0 6.2 %collective-permute-start.2 = (bf16[2560,384]{1,0:T(8,128)(2,1)S(1)}, bf16[2560,384]{1,0:T(8,128)(2,1)S(1)}, u32[]{:S(2)}, u32[]{:S(2)}) collective-permute-start(bf16[2560,384]{1,0:T(8,128)(2,1)S(1)} %convolution_convert_fusion.4), channel_id=1, source_target_pairs={{0,8},{8,0},{1,9},{9,1},{2,10},{10,2},{3,11},{11,3},{4,12},{12,4},... | collective-permute-start | bytes 5898248 | tf_op jit(solution)/shard_map/ppermute | solution.py:25
  171.5 54.4 %all-to-all-start.1 = ((bf16[8,40,2560]{2,1,0:T(8,128)(2,1)}), bf16[8,40,2560]{2,1,0:T(8,128)(2,1)S(1)}, u32[]{:S(2)}, u32[]{:S(2)}) async-start(bf16[8,40,2560]{2,1,0:T(8,128)(2,1)} %bitcast.18), calls=%async_computation.1 | async-start | bytes 3276800 | tf_op jit(solution)/shard_map/all_to_all | solution.py:129
  225.9 33.9 %all-to-all-start.2 = ((bf16[8,40,2560]{2,1,0:T(8,128)(2,1)}), bf16[8,40,2560]{2,1,0:T(8,128)(2,1)S(1)}, u32[]{:S(2)}, u32[]{:S(2)}) async-start(bf16[8,40,2560]{2,1,0:T(8,128)(2,1)} %bitcast.69), calls=%async_computation.2 | async-start | bytes 3276800 | tf_op jit(solution)/shard_map/all_to_all | solution.py:146
  278.8 2.9 copy-start.3
  278.8 3.2 %collective-permute-start.5 = (bf16[3,160,384]{2,1,0:T(8,128)(2,1)}, bf16[3,160,384]{2,1,0:T(8,128)(2,1)S(1)}, u32[]{:S(2)}, u32[]{:S(2)}) collective-permute-start(bf16[3,160,384]{2,1,0:T(8,128)(2,1)} %reduce-scatter.2.cloned.1.call-done), channel_id=1, source_target_pairs={{0,8},{8,0},{1,9},{9,1},{2,10},{10,2},{3,11},{11,3},{4,12},{12,4},... | collective-permute-start | bytes 1105928 | tf_op jit(solution)/shard_map/ppermute | solution.py:25
  281.7 1.3 copy-start.1
Sparse Core Ops, SparseCore 0:
  15.5 115.1 all-gather.1
  165.2 113.5 reduce-scatter.1

commit v6 on v5

--- a/solution.py
+++ b/solution.py
@@ -35,9 +35,27 @@
     own = jnp.where(
         first, jnp.concatenate([kept, came], axis=1), jnp.concatenate([came, kept], axis=1)
     )
-    own = lax.all_gather(own, CHIPS, axis=1, tiled=True)
-    other = swap_cores(own)
-    return [(own[i], other[i]) for i in range(len(weights))]
+    gathered = lax.all_gather(own[:-1], CHIPS, axis=1, tiled=True)
+    last = ring_gather(own[-1])
+    owns = [gathered[i] for i in range(len(weights) - 1)] + [last]
+    return [(value, swap_cores(value)) for value in owns]
+
+
+def ring_stage(value, axis):
+    size = lax.axis_size(axis)
+    me = lax.axis_index(axis)
+    held = jnp.zeros((size,) + value.shape, value.dtype)
+    held = lax.dynamic_update_index_in_dim(held, value, me, 0)
+    for shift in range(1, size):
+        got = lax.ppermute(value, axis, perm=[(i, (i + shift) % size) for i in range(size)])
+        held = lax.dynamic_update_index_in_dim(held, got, (me - shift) % size, 0)
+    return held
+
+
+def ring_gather(block):
+    by_zh = ring_stage(block, CHIPS[1])
+    by_x = ring_stage(by_zh, CHIPS[0])
+    return by_x.reshape((-1,) + block.shape[1:])
 
 
 def scatter_grads(*parts):

time: 291 us -> 328 us (1.13); the launches traced: 290 us -> 321 us
  starting transfers between devices: 19 us -> 45.5 us
  local copies, waits for them, and re-layouts: 19.9 us -> 34.6 us
  waiting for transfers between devices: 184 us -> 172 us
    all_gather x1, waiting for transfers between devices: 95.6 us -> 0.01 us  [gather_weights(): gathered = lax.all_gather(own[:-1], CHIPS, axis=1, tiled=True)]
    ppermute x0 -> x6, waiting for transfers between devices: none -> 91.2 us  [ring_stage(): lax.ppermute(value, axis, perm=[(i, (i + shift) % size) for i in range(si...]
    ppermute x0 -> x6, starting transfers between devices: none -> 17 us  [ring_stage(): lax.ppermute(value, axis, perm=[(i, (i + shift) % size) for i in range(si...]
    ppermute x6 -> x8, starting transfers between devices: 6.79 us -> 17.1 us  [swap_cores(): return lax.ppermute(value, 'core', perm=[(0, 1), (1, 0)])]
    dynamic_update_slice x0 -> x7, local copies, waits for them, and re-layouts: none -> 7.41 us  [the longest x6 5.52 us: ring_stage(): held = lax.dynamic_update_index_in_dim(held, got, (me - shift) % size, 0)]
    ppermute x6 -> x8, waiting for transfers between devices: 7.71 us -> 1.24 us  [swap_cores(): return lax.ppermute(value, 'core', perm=[(0, 1), (1, 0)])]
    squeeze x0 -> x2, local copies, waits for them, and re-layouts: none -> 5.97 us  [the longest x1 4.4 us: gather_weights(): owns = [gathered[i] for i in range(len(weights) - 1)] + [last]]
    all_to_all x1, waiting for transfers between devices: 38.2 us -> 43.1 us  [shards(): lax.all_to_all(expert_out, 'expert', split_axis=0, concat_axis=0, tiled=T...]
  transfers between devices with their start and end apart: 11 -> 19, of which waited for: 9 -> 9; matrix products, arithmetic and copies ran while one was open for 18% -> 23% of each run, Pallas kernels for 0% -> 0%
where the time goes in v6:
time: 328 us; the launch traced here: 321 us
  waiting for transfers between devices  172 us (52%)
  starting transfers between devices  45.5 us (14%)
  matrix products  37.7 us (11%)
  local copies, waits for them, and re-layouts  34.6 us (11%)
  other arithmetic  16.5 us (5%)
  between operations  14.6 us (4%)
    ppermute x6, waiting for transfers between devices, ring_stage(): lax.ppermute(value, axis, perm=[(i, (i + shift) % size) for i in range(si...  91.2 us
    all_to_all x1, waiting for transfers between devices, shards(): lax.all_to_all(expert_out, 'expert', split_axis=0, concat_axis=0, tiled=T...  43.1 us
    all_to_all x1, waiting for transfers between devices, shards(): lax.all_to_all(token_grad.reshape(experts, capacity, model_width), 'exper...  24.6 us
    ppermute x8, starting transfers between devices, swap_cores(): return lax.ppermute(value, 'core', perm=[(0, 1), (1, 0)])  17.1 us
    ppermute x6, starting transfers between devices, ring_stage(): lax.ppermute(value, axis, perm=[(i, (i + shift) % size) for i in range(si...  17 us
    dot_general x6, matrix products, contract_last(): lax.dot_general(matrix_a, matrix_b, (((1,), (1,)), ((), ())), preferred_e...  16.8 us
    reduce_scatter x1, waiting for transfers between devices, scatter_grads(): lax.psum_scatter(jnp.stack(pair_sums), CHIPS, scatter_dimension=1, tiled=...  12.1 us
    dot_general x6, matrix products, contract_first(): lax.dot_general(matrix_a, matrix_b, (((0,), (0,)), ((), ())), preferred_e...  8.6 us
  transfers between devices with their start and end apart: 19, of which 9 were waited for; matrix products, arithmetic and copies ran while one was open for 23% of the time, Pallas kernels for 0%

profile of v6, /device:TPU:1, one launch (start us, length us, event | category | flops | bytes accessed | tf_op | source)
XLA Modules:
  0.0 321.1 jit_solution(9869517157025766288)
XLA Ops:
  10.1 3.3 %collective-permute-start = (bf16[3,80,384]{2,1,0:T(8,128)(2,1)S(1)}, bf16[3,80,384]{2,1,0:T(8,128)(2,1)S(1)}, u32[]{:S(2)}, u32[]{:S(2)}) collective-permute-start(bf16[3,80,384]{2,1,0:T(8,128)(2,1)S(1)} %get-tuple-element.22), channel_id=1, source_target_pairs={{0,8},{8,0},{1,9},{9,1},{2,10},{10,2},{3,11},{11,3},{4,12},{12,4},... | collective-permute-start | bytes 552968 | tf_op jit(solution)/shard_map/ppermute | solution.py:25
  17.8 2.6 gather_fusion
  23.7 3.2 gather_fusion.1
  32.9 3.8 %all-to-all-start = ((bf16[2,8,40,2560]{3,2,0,1:T(8,128)(2,1)}), bf16[2,8,40,2560]{3,2,0,1:T(8,128)(2,1)S(1)}, u32[]{:S(2)}, u32[]{:S(2)}) async-start(bf16[2,8,40,2560]{3,2,0,1:T(8,128)(2,1)} %pad_maximum_fusion.1), calls=%async_computation | async-start | bytes 6553600 | tf_op jit(solution)/shard_map/all_to_all | solution.py:124
  39.1 3.0 collective-permute-start.3
  42.1 4.2 %collective-permute-start.4 = (bf16[160,384]{1,0:T(8,128)(2,1)S(1)}, bf16[160,384]{1,0:T(8,128)(2,1)S(1)}, u32[]{:S(2)}, u32[]{:S(2)}) collective-permute-start(bf16[160,384]{1,0:T(8,128)(2,1)S(1)} %get-tuple-element.19), channel_id=1, source_target_pairs={{0,32},{16,48},{32,0},{48,16},{1,33},{17,49},{33,1},{49,17},{2,34}... | collective-permute-start | bytes 368648 | tf_op jit(solution)/shard_map/ppermute | solution.py:50
  46.3 2.4 collective-permute-start.5
  48.7 72.3 %collective-permute-done.3 = bf16[160,384]{1,0:T(8,128)(2,1)S(1)} collective-permute-done((bf16[160,384]{1,0:T(8,128)(2,1)S(1)}, bf16[160,384]{1,0:T(8,128)(2,1)S(1)}, u32[]{:S(2)}, u32[]{:S(2)}) %collective-permute-start.3) | collective-permute-done | bytes 122912 | tf_op jit(solution)/shard_map/ppermute | solution.py:50
  121.6 3.7 %collective-permute-done.4 = bf16[160,384]{1,0:T(8,128)(2,1)S(1)} collective-permute-done((bf16[160,384]{1,0:T(8,128)(2,1)S(1)}, bf16[160,384]{1,0:T(8,128)(2,1)S(1)}, u32[]{:S(2)}, u32[]{:S(2)}) %collective-permute-start.4) | collective-permute-done | bytes 122912 | tf_op jit(solution)/shard_map/ppermute | solution.py:50
  126.7 3.8 %collective-permute-start.6 = (bf16[4,160,384]{2,1,0:T(8,128)(2,1)}, bf16[4,160,384]{2,1,0:T(8,128)(2,1)}, u32[]{:S(2)}, u32[]{:S(2)}) collective-permute-start(bf16[4,160,384]{2,1,0:T(8,128)(2,1)} %bitcast_dynamic-update-slice_fusion.4), channel_id=1, source_target_pairs={{0,64},{64,128},{128,192},{192,0},{1,65},{65,129},{129,193},{193,1... | collective-permute-start | bytes 1474568 | tf_op jit(solution)/shard_map/ppermute | solution.py:50
  130.5 2.4 collective-permute-start.7
  137.4 5.3 %collective-permute-done.6 = bf16[4,160,384]{2,1,0:T(8,128)(2,1)} collective-permute-done((bf16[4,160,384]{2,1,0:T(8,128)(2,1)}, bf16[4,160,384]{2,1,0:T(8,128)(2,1)}, u32[]{:S(2)}, u32[]{:S(2)}) %collective-permute-start.6) | collective-permute-done | bytes 491552 | tf_op jit(solution)/shard_map/ppermute | solution.py:50
  144.6 9.9 %collective-permute-done.7 = bf16[4,160,384]{2,1,0:T(8,128)(2,1)S(1)} collective-permute-done((bf16[4,160,384]{2,1,0:T(8,128)(2,1)}, bf16[4,160,384]{2,1,0:T(8,128)(2,1)S(1)}, u32[]{:S(2)}, u32[]{:S(2)}) %collective-permute-start.7) | collective-permute-done | bytes 491552 | tf_op jit(solution)/shard_map/ppermute | solution.py:50
  157.7 4.4 %slice_bitcast_fusion.1 = (bf16[2560,384]{1,0:T(8,128)(2,1)}, bf16[2560,384]{1,0:T(8,128)(2,1)}) fusion(bf16[2,2560,384]{2,1,0:T(8,128)(2,1)} %all-gather.2.cloned.1.call-done), kind=kLoop, calls=%fused_computation.32 | loop fusion | bytes 7864320 | tf_op jit(solution)/shard_map/squeeze | solution.py:40
  162.9 2.5 fusion.44
  165.5 2.7 fusion.45
  170.2 2.5 fusion.42
  172.8 2.5 fusion.43
  181.0 9.4 %collective-permute-start.10 = (bf16[2560,384]{1,0:T(8,128)(2,1)S(1)}, bf16[2560,384]{1,0:T(8,128)(2,1)S(1)}, u32[]{:S(2)}, u32[]{:S(2)}) collective-permute-start(bf16[2560,384]{1,0:T(8,128)(2,1)S(1)} %convolution_convert_fusion.4), channel_id=1, source_target_pairs={{0,8},{8,0},{1,9},{9,1},{2,10},{10,2},{3,11},{11,3},{4,12},{12,4},... | collective-permute-start | bytes 5898248 | tf_op jit(solution)/shard_map/ppermute | solution.py:25
  195.8 3.3 %pad_maximum_fusion = bf16[3,2560,384]{2,1,0:T(8,128)(2,1)} fusion(bf16[1,2560,384]{2,1,0:T(8,128)(2,1)S(1)} %fusion.7, bf16[1,2560,384]{2,1,0:T(8,128)(2,1)S(1)} %fusion.6, bf16[1,2560,384]{2,1,0:T(8,128)(2,1)S(1)} %fusion.5), kind=kLoop, calls=%fused_computation.6 | loop fusion | flops 5898240 | bytes 11796480 | tf_op jit(solution)/shard_map/stack | solution.py:70
  199.1 2.6 fusion.23
  201.7 3.9 %fusion.3 = bf16[320,2560]{1,0:T(8,128)(2,1)} fusion(f32[320,2560]{1,0:T(8,128)S(1)} %fusion.23, bf16[2560,384]{1,0:T(8,128)(2,1)} %bitcast.22, bf16[320,768]{1,0:T(8,128)(2,1)S(1)} %get-tuple-element.15), kind=kOutput, calls=%fused_computation.20 | convolution fusion | flops 630784000 | bytes 7127040 | tf_op jit(solution)/shard_map/dot_general | solution.py:13
  205.5 3.6 %all-to-all-start.1 = ((bf16[8,40,2560]{2,1,0:T(8,128)(2,1)}), bf16[8,40,2560]{2,1,0:T(8,128)(2,1)S(1)}, u32[]{:S(2)}, u32[]{:S(2)}) async-start(bf16[8,40,2560]{2,1,0:T(8,128)(2,1)} %bitcast.23), calls=%async_computation.1 | async-start | bytes 3276800 | tf_op jit(solution)/shard_map/all_to_all | solution.py:147
  209.1 2.6 fusion.18
  211.7 2.8 convolution_add_fusion.2
  215.6 3.8 %fusion.4 = bf16[320,2560]{1,0:T(8,128)(2,1)} fusion(f32[320,2560]{1,0:T(8,128)S(1)} %convolution_add_fusion.1, bf16[2560,384]{1,0:T(8,128)(2,1)} %collective-permute-done.2, bf16[320,768]{1,0:T(8,128)(2,1)S(1)} %get-tuple-element.13), kind=kOutput, calls=%fused_computation.21 | convolution fusion | flops 630784000 | bytes 7127040 | tf_op jit(solution)/shard_map/dot_general | solution.py:13
  219.5 43.1 %all-to-all-done.1 = bf16[8,40,2560]{2,1,0:T(8,128)(2,1)S(1)} async-done(((bf16[8,40,2560]{2,1,0:T(8,128)(2,1)}), bf16[8,40,2560]{2,1,0:T(8,128)(2,1)S(1)}, u32[]{:S(2)}, u32[]{:S(2)}) %all-to-all-start.1) | async-done | bytes 1638432 | tf_op jit(solution)/shard_map/all_to_all | solution.py:147
  262.5 3.9 %all-to-all-start.2 = ((bf16[8,40,2560]{2,1,0:T(8,128)(2,1)}), bf16[8,40,2560]{2,1,0:T(8,128)(2,1)S(1)}, u32[]{:S(2)}, u32[]{:S(2)}) async-start(bf16[8,40,2560]{2,1,0:T(8,128)(2,1)} %bitcast.78), calls=%async_computation.2 | async-start | bytes 3276800 | tf_op jit(solution)/shard_map/all_to_all | solution.py:164
  266.5 2.5 gather_fusion.2
  269.0 24.6 %all-to-all-done.2 = bf16[8,40,2560]{2,1,0:T(8,128)(2,1)S(1)} async-done(((bf16[8,40,2560]{2,1,0:T(8,128)(2,1)}), bf16[8,40,2560]{2,1,0:T(8,128)(2,1)S(1)}, u32[]{:S(2)}, u32[]{:S(2)}) %all-to-all-start.2) | async-done | bytes 1638432 | tf_op jit(solution)/shard_map/all_to_all | solution.py:164
  295.1 2.8 multiply_convert_fusion
  297.8 12.1 %reduce-scatter.2.cloned.1.call-done = bf16[3,160,384]{2,1,0:T(8,128)(2,1)} async-done(((bf16[3,2560,384]{2,1,0:T(8,128)(2,1)}), bf16[3,160,384]{2,1,0:T(8,128)(2,1)}) %reduce-scatter.2.cloned.1.call-update) | async-done | bytes 368656 | tf_op jit(solution)/shard_map/reduce_scatter | solution.py:70
  (92 shorter events, 51.0 us)
Async XLA Ops:
  7.2 10.7 %copy-start = (bf16[256,2560]{1,0:T(8,128)(2,1)S(1)}, bf16[256,2560]{1,0:T(8,128)(2,1)}, u32[]{:S(2)}) copy-start(bf16[256,2560]{1,0:T(8,128)(2,1)} %param.11) | copy-start | bytes 3932164
  7.2 150.5 %all-gather.2.cloned.1.call-start = ((), (), s32[]{:S(2)}) async-start(), calls=%async_computation.4 | async-start | bytes 4177920 | tf_op jit(solution)/shard_map/all_gather | solution.py:38
  10.1 10.3 %collective-permute-start = (bf16[3,80,384]{2,1,0:T(8,128)(2,1)S(1)}, bf16[3,80,384]{2,1,0:T(8,128)(2,1)S(1)}, u32[]{:S(2)}, u32[]{:S(2)}) collective-permute-start(bf16[3,80,384]{2,1,0:T(8,128)(2,1)S(1)} %get-tuple-element.22), channel_id=1, source_target_pairs={{0,8},{8,0},{1,9},{9,1},{2,10},{10,2},{3,11},{11,3},{4,12},{12,4},... | collective-permute-start | bytes 552968 | tf_op jit(solution)/shard_map/ppermute | solution.py:25
  17.8 4.2 %copy-start.7 = (s32[256,1]{0,1:T(1,128)S(1)}, s32[256,1]{0,1:T(1,128)}, u32[]{:S(2)}) copy-start(s32[256,1]{0,1:T(1,128)} %param.13) | copy-start | bytes 3076
  20.6 0.7 copy-start.4
  32.9 129.8 %all-to-all-start = ((bf16[2,8,40,2560]{3,2,0,1:T(8,128)(2,1)}), bf16[2,8,40,2560]{3,2,0,1:T(8,128)(2,1)S(1)}, u32[]{:S(2)}, u32[]{:S(2)}) async-start(bf16[2,8,40,2560]{3,2,0,1:T(8,128)(2,1)} %pad_maximum_fusion.1), calls=%async_computation | async-start | bytes 6553600 | tf_op jit(solution)/shard_map/all_to_all | solution.py:124
  36.7 273.2 %reduce-scatter.2.cloned.1.call-start = ((), (), s32[]{:S(2)}) async-start(), calls=%async_computation.5 | async-start | bytes 6266880 | tf_op jit(solution)/shard_map/reduce_scatter | solution.py:70
  39.1 81.9 %collective-permute-start.3 = (bf16[160,384]{1,0:T(8,128)(2,1)S(1)}, bf16[160,384]{1,0:T(8,128)(2,1)S(1)}, u32[]{:S(2)}, u32[]{:S(2)}) collective-permute-start(bf16[160,384]{1,0:T(8,128)(2,1)S(1)} %get-tuple-element.19), channel_id=1, source_target_pairs={{0,16},{16,32},{32,48},{48,0},{1,17},{17,33},{33,49},{49,1},{2,18}... | collective-permute-start | bytes 368648 | tf_op jit(solution)/shard_map/ppermute | solution.py:50
  42.1 83.3 %collective-permute-start.4 = (bf16[160,384]{1,0:T(8,128)(2,1)S(1)}, bf16[160,384]{1,0:T(8,128)(2,1)S(1)}, u32[]{:S(2)}, u32[]{:S(2)}) collective-permute-start(bf16[160,384]{1,0:T(8,128)(2,1)S(1)} %get-tuple-element.19), channel_id=1, source_target_pairs={{0,32},{16,48},{32,0},{48,16},{1,33},{17,49},{33,1},{49,17},{2,34}... | collective-permute-start | bytes 368648 | tf_op jit(solution)/shard_map/ppermute | solution.py:50
  46.3 79.7 %collective-permute-start.5 = (bf16[160,384]{1,0:T(8,128)(2,1)S(1)}, bf16[160,384]{1,0:T(8,128)(2,1)S(1)}, u32[]{:S(2)}, u32[]{:S(2)}) collective-permute-start(bf16[160,384]{1,0:T(8,128)(2,1)S(1)} %get-tuple-element.19), channel_id=1, source_target_pairs={{0,48},{16,0},{32,16},{48,32},{1,49},{17,1},{33,17},{49,33},{2,50}... | collective-permute-start | bytes 368648 | tf_op jit(solution)/shard_map/ppermute | solution.py:50
  126.7 16.0 %collective-permute-start.6 = (bf16[4,160,384]{2,1,0:T(8,128)(2,1)}, bf16[4,160,384]{2,1,0:T(8,128)(2,1)}, u32[]{:S(2)}, u32[]{:S(2)}) collective-permute-start(bf16[4,160,384]{2,1,0:T(8,128)(2,1)} %bitcast_dynamic-update-slice_fusion.4), channel_id=1, source_target_pairs={{0,64},{64,128},{128,192},{192,0},{1,65},{65,129},{129,193},{193,1... | collective-permute-start | bytes 1474568 | tf_op jit(solution)/shard_map/ppermute | solution.py:50
  130.5 24.0 %collective-permute-start.7 = (bf16[4,160,384]{2,1,0:T(8,128)(2,1)}, bf16[4,160,384]{2,1,0:T(8,128)(2,1)S(1)}, u32[]{:S(2)}, u32[]{:S(2)}) collective-permute-start(bf16[4,160,384]{2,1,0:T(8,128)(2,1)} %bitcast_dynamic-update-slice_fusion.4), channel_id=1, source_target_pairs={{0,128},{64,192},{128,0},{192,64},{1,129},{65,193},{129,1},{193,65... | collective-permute-start | bytes 1474568 | tf_op jit(solution)/shard_map/ppermute | solution.py:50
  132.9 22.4 %collective-permute-start.8 = (bf16[4,160,384]{2,1,0:T(8,128)(2,1)}, bf16[4,160,384]{2,1,0:T(8,128)(2,1)S(1)}, u32[]{:S(2)}, u32[]{:S(2)}) collective-permute-start(bf16[4,160,384]{2,1,0:T(8,128)(2,1)} %bitcast_dynamic-update-slice_fusion.4), channel_id=1, source_target_pairs={{0,192},{64,0},{128,64},{192,128},{1,193},{65,1},{129,65},{193,129... | collective-permute-start | bytes 1474568 | tf_op jit(solution)/shard_map/ppermute | solution.py:50
  156.2 9.3 %collective-permute-start.9 = (bf16[2560,384]{1,0:T(8,128)(2,1)}, bf16[2560,384]{1,0:T(8,128)(2,1)}, u32[]{:S(2)}, u32[]{:S(2)}) collective-permute-start(bf16[2560,384]{1,0:T(8,128)(2,1)} %bitcast.22), channel_id=1, source_target_pairs={{0,8},{8,0},{1,9},{9,1},{2,10},{10,2},{3,11},{11,3},{4,12},{12,4},... | collective-permute-start | bytes 5898248 | tf_op jit(solution)/shard_map/ppermute | solution.py:25
  162.1 8.1 %collective-permute-start.1 = (bf16[2560,384]{1,0:T(8,128)(2,1)}, bf16[2560,384]{1,0:T(8,128)(2,1)}, u32[]{:S(2)}, u32[]{:S(2)}) collective-permute-start(bf16[2560,384]{1,0:T(8,128)(2,1)} %get-tuple-element.9), channel_id=1, source_target_pairs={{0,8},{8,0},{1,9},{9,1},{2,10},{10,2},{3,11},{11,3},{4,12},{12,4},... | collective-permute-start | bytes 5898248 | tf_op jit(solution)/shard_map/ppermute | solution.py:25
  162.2 10.6 %collective-permute-start.2 = (bf16[2560,384]{1,0:T(8,128)(2,1)}, bf16[2560,384]{1,0:T(8,128)(2,1)}, u32[]{:S(2)}, u32[]{:S(2)}) collective-permute-start(bf16[2560,384]{1,0:T(8,128)(2,1)} %get-tuple-element.10), channel_id=1, source_target_pairs={{0,8},{8,0},{1,9},{9,1},{2,10},{10,2},{3,11},{11,3},{4,12},{12,4},... | collective-permute-start | bytes 5898248 | tf_op jit(solution)/shard_map/ppermute | solution.py:25
  165.5 2.7 copy-start.2
  177.5 12.9 %collective-permute-start.12 = (bf16[2560,384]{1,0:T(8,128)(2,1)S(1)}, bf16[2560,384]{1,0:T(8,128)(2,1)S(1)}, u32[]{:S(2)}, u32[]{:S(2)}) collective-permute-start(bf16[2560,384]{1,0:T(8,128)(2,1)S(1)} %convolution_convert_fusion), channel_id=1, source_target_pairs={{0,8},{8,0},{1,9},{9,1},{2,10},{10,2},{3,11},{11,3},{4,12},{12,4},... | collective-permute-start | bytes 5898248 | tf_op jit(solution)/shard_map/ppermute | solution.py:25
  179.0 12.8 %collective-permute-start.11 = (bf16[2560,384]{1,0:T(8,128)(2,1)S(1)}, bf16[2560,384]{1,0:T(8,128)(2,1)S(1)}, u32[]{:S(2)}, u32[]{:S(2)}) collective-permute-start(bf16[2560,384]{1,0:T(8,128)(2,1)S(1)} %convolution_convert_fusion.2), channel_id=1, source_target_pairs={{0,8},{8,0},{1,9},{9,1},{2,10},{10,2},{3,11},{11,3},{4,12},{12,4},... | collective-permute-start | bytes 5898248 | tf_op jit(solution)/shard_map/ppermute | solution.py:25
  181.0 13.3 %collective-permute-start.10 = (bf16[2560,384]{1,0:T(8,128)(2,1)S(1)}, bf16[2560,384]{1,0:T(8,128)(2,1)S(1)}, u32[]{:S(2)}, u32[]{:S(2)}) collective-permute-start(bf16[2560,384]{1,0:T(8,128)(2,1)S(1)} %convolution_convert_fusion.4), channel_id=1, source_target_pairs={{0,8},{8,0},{1,9},{9,1},{2,10},{10,2},{3,11},{11,3},{4,12},{12,4},... | collective-permute-start | bytes 5898248 | tf_op jit(solution)/shard_map/ppermute | solution.py:25
  205.5 57.0 %all-to-all-start.1 = ((bf16[8,40,2560]{2,1,0:T(8,128)(2,1)}), bf16[8,40,2560]{2,1,0:T(8,128)(2,1)S(1)}, u32[]{:S(2)}, u32[]{:S(2)}) async-start(bf16[8,40,2560]{2,1,0:T(8,128)(2,1)} %bitcast.23), calls=%async_computation.1 | async-start | bytes 3276800 | tf_op jit(solution)/shard_map/all_to_all | solution.py:147
  211.7 2.8 copy-start.3
  219.5 47.0 %copy-start.6 = (s32[256,1]{0,1:T(1,128)S(1)}, s32[256,1]{0,1:T(1,128)}, u32[]{:S(2)}) copy-start(s32[256,1]{0,1:T(1,128)} %param.12) | copy-start | bytes 3076
  262.5 31.1 %all-to-all-start.2 = ((bf16[8,40,2560]{2,1,0:T(8,128)(2,1)}), bf16[8,40,2560]{2,1,0:T(8,128)(2,1)S(1)}, u32[]{:S(2)}, u32[]{:S(2)}) async-start(bf16[8,40,2560]{2,1,0:T(8,128)(2,1)} %bitcast.78), calls=%async_computation.2 | async-start | bytes 3276800 | tf_op jit(solution)/shard_map/all_to_all | solution.py:164
  309.9 2.9 copy-start.5
  309.9 3.2 collective-permute-start.13
  312.8 1.3 copy-start.1
Sparse Core Ops, SparseCore 0:
  22.2 96.9 all-gather.1
  199.2 110.6 reduce-scatter.1

commit v7 on v5

--- a/solution.py
+++ b/solution.py
@@ -36,8 +36,7 @@
         first, jnp.concatenate([kept, came], axis=1), jnp.concatenate([came, kept], axis=1)
     )
     own = lax.all_gather(own, CHIPS, axis=1, tiled=True)
-    other = swap_cores(own)
-    return [(own[i], other[i]) for i in range(len(weights))]
+    return [(own[i], swap_cores(own[i])) for i in range(len(weights))]
 
 
 def scatter_grads(*parts):

time: 291 us -> 293 us (level)
  local copies, waits for them, and re-layouts: 19.9 us -> 25.4 us
  waiting for transfers between devices: 184 us -> 180 us
    squeeze x0 -> x1, local copies, waits for them, and re-layouts: none -> 5.53 us  [gather_weights(): return [(own[i], swap_cores(own[i])) for i in range(len(weights))]]
    ppermute x6 -> x8, waiting for transfers between devices: 7.71 us -> 4.18 us  [swap_cores(): return lax.ppermute(value, 'core', perm=[(0, 1), (1, 0)])]
    ppermute x6 -> x8, starting transfers between devices: 6.79 us -> 7.12 us  [swap_cores(): return lax.ppermute(value, 'core', perm=[(0, 1), (1, 0)])]
  transfers between devices with their start and end apart: 11 -> 13, of which waited for: 9 -> 9; matrix products, arithmetic and copies ran while one was open for 18% -> 21% of each run, Pallas kernels for 0% -> 0%
where the time goes in v7:
time: 293 us; the launch traced here: 292 us
  waiting for transfers between devices  180 us (61%)
  matrix products  37.4 us (13%)
  local copies, waits for them, and re-layouts  25.4 us (9%)
  starting transfers between devices  19.7 us (7%)
  other arithmetic  15.5 us (5%)
  between operations  14.4 us (5%)
    all_gather x1, waiting for transfers between devices, gather_weights(): own = lax.all_gather(own, CHIPS, axis=1, tiled=True)  95.5 us
    all_to_all x1, waiting for transfers between devices, shards(): lax.all_to_all(expert_out, 'expert', split_axis=0, concat_axis=0, tiled=T...  38 us
    all_to_all x1, waiting for transfers between devices, shards(): lax.all_to_all(token_grad.reshape(experts, capacity, model_width), 'exper...  27.3 us
    dot_general x6, matrix products, contract_last(): lax.dot_general(matrix_a, matrix_b, (((1,), (1,)), ((), ())), preferred_e...  18.1 us
    reduce_scatter x1, waiting for transfers between devices, scatter_grads(): lax.psum_scatter(jnp.stack(pair_sums), CHIPS, scatter_dimension=1, tiled=...  14.8 us
    dot_general x6, matrix products, contract_first(): lax.dot_general(matrix_a, matrix_b, (((0,), (0,)), ((), ())), preferred_e...  8.6 us
    dot_general x3, matrix products, halves(): lax.dot_general(left, pair[1], dims, preferred_element_type=jnp.float32)  7.64 us
    ppermute x8, starting transfers between devices, swap_cores(): return lax.ppermute(value, 'core', perm=[(0, 1), (1, 0)])  7.12 us
  transfers between devices with their start and end apart: 13, of which 9 were waited for; matrix products, arithmetic and copies ran while one was open for 21% of the time, Pallas kernels for 0%

profile of v7, /device:TPU:1, one launch (start us, length us, event | category | flops | bytes accessed | tf_op | source)
XLA Modules:
  0.0 292.2 jit_solution(5272646648434722241)
XLA Ops:
  10.1 3.3 %collective-permute-start = (bf16[3,80,384]{2,1,0:T(8,128)(2,1)S(1)}, bf16[3,80,384]{2,1,0:T(8,128)(2,1)S(1)}, u32[]{:S(2)}, u32[]{:S(2)}) collective-permute-start(bf16[3,80,384]{2,1,0:T(8,128)(2,1)S(1)} %get-tuple-element.21), channel_id=1, source_target_pairs={{0,8},{8,0},{1,9},{9,1},{2,10},{10,2},{3,11},{11,3},{4,12},{12,4},... | collective-permute-start | bytes 552968 | tf_op jit(solution)/shard_map/ppermute | solution.py:25
  17.8 2.6 gather_fusion
  20.4 1.6 multiply_convert_fusion.1
  22.0 3.2 %gather_fusion.1 = bf16[320,2560]{1,0:T(8,128)(2,1)} fusion(bf16[256,2560]{1,0:T(8,128)(2,1)S(1)} %multiply_convert_fusion.1, s32[1024]{0:T(1024)S(1)} %pad_clamp_fusion.1), kind=kCustom, calls=%fused_computation.2.clone | custom fusion | bytes 3278080 | tf_op jit(solution)/shard_map/jit(_take)/gather | solution.py:97
  25.2 2.2 scatter_custom_fusion.1
  27.4 1.9 select_multiply_fusion.1
  29.3 2.0 pad_maximum_fusion.1
  31.3 3.7 %all-to-all-start = ((bf16[2,8,40,2560]{3,2,0,1:T(8,128)(2,1)}), bf16[2,8,40,2560]{3,2,0,1:T(8,128)(2,1)S(1)}, u32[]{:S(2)}, u32[]{:S(2)}) async-start(bf16[2,8,40,2560]{3,2,0,1:T(8,128)(2,1)} %pad_maximum_fusion.1), calls=%async_computation | async-start | bytes 6553600 | tf_op jit(solution)/shard_map/all_to_all | solution.py:105
  35.1 95.5 %all-gather.2.cloned.1.call-done = bf16[3,2560,384]{2,1,0:T(8,128)(2,1)} async-done(((bf16[3,160,384]{2,1,0:T(8,128)(2,1)}), bf16[3,2560,384]{2,1,0:T(8,128)(2,1)}) %all-gather.2.cloned.1.call-update) | async-done | bytes 5898256 | tf_op jit(solution)/shard_map/all_gather | solution.py:38
  130.7 5.5 %slice_bitcast_fusion = (bf16[2560,384]{1,0:T(8,128)(2,1)}, bf16[2560,384]{1,0:T(8,128)(2,1)}, bf16[2560,384]{1,0:T(8,128)(2,1)}) fusion(bf16[3,2560,384]{2,1,0:T(8,128)(2,1)} %all-gather.2.cloned.1.call-done), kind=kLoop, calls=%fused_computation.31 | loop fusion | bytes 11796480 | tf_op jit(solution)/shard_map/squeeze | solution.py:39
  137.4 2.4 copy-done.2
  142.9 2.5 fusion.45
  145.4 2.5 fusion.43
  148.0 2.5 fusion.44
  156.8 1.5 fusion.7
  159.6 1.5 fusion.6
  162.4 1.5 fusion.5
  163.9 3.4 %pad_maximum_fusion = bf16[3,2560,384]{2,1,0:T(8,128)(2,1)} fusion(bf16[1,2560,384]{2,1,0:T(8,128)(2,1)S(1)} %fusion.7, bf16[1,2560,384]{2,1,0:T(8,128)(2,1)S(1)} %fusion.6, bf16[1,2560,384]{2,1,0:T(8,128)(2,1)S(1)} %fusion.5), kind=kLoop, calls=%fused_computation.6 | loop fusion | flops 5898240 | bytes 11796480 | tf_op jit(solution)/shard_map/stack | solution.py:51
  167.3 2.6 fusion.25
  169.9 3.9 %fusion.3 = bf16[320,2560]{1,0:T(8,128)(2,1)} fusion(f32[320,2560]{1,0:T(8,128)S(1)} %fusion.25, bf16[2560,384]{1,0:T(8,128)(2,1)} %collective-permute-done.3, bf16[320,768]{1,0:T(8,128)(2,1)S(1)} %get-tuple-element.16), kind=kOutput, calls=%fused_computation.20 | convolution fusion | flops 630784000 | bytes 7127040 | tf_op jit(solution)/shard_map/dot_general | solution.py:13
  173.8 4.5 %all-to-all-start.1 = ((bf16[8,40,2560]{2,1,0:T(8,128)(2,1)}), bf16[8,40,2560]{2,1,0:T(8,128)(2,1)S(1)}, u32[]{:S(2)}, u32[]{:S(2)}) async-start(bf16[8,40,2560]{2,1,0:T(8,128)(2,1)} %bitcast.15), calls=%async_computation.1 | async-start | bytes 3276800 | tf_op jit(solution)/shard_map/all_to_all | solution.py:128
  178.2 2.6 fusion.18
  180.8 2.6 convolution_add_fusion.2
  183.5 2.6 convolution_add_fusion.1
  186.1 3.8 %fusion.4 = bf16[320,2560]{1,0:T(8,128)(2,1)} fusion(f32[320,2560]{1,0:T(8,128)S(1)} %convolution_add_fusion.1, bf16[2560,384]{1,0:T(8,128)(2,1)} %collective-permute-done.2, bf16[320,768]{1,0:T(8,128)(2,1)S(1)} %get-tuple-element.14), kind=kOutput, calls=%fused_computation.21 | convolution fusion | flops 630784000 | bytes 7127040 | tf_op jit(solution)/shard_map/dot_general | solution.py:13
  189.9 38.0 %all-to-all-done.1 = bf16[8,40,2560]{2,1,0:T(8,128)(2,1)S(1)} async-done(((bf16[8,40,2560]{2,1,0:T(8,128)(2,1)}), bf16[8,40,2560]{2,1,0:T(8,128)(2,1)S(1)}, u32[]{:S(2)}, u32[]{:S(2)}) %all-to-all-start.1) | async-done | bytes 1638432 | tf_op jit(solution)/shard_map/all_to_all | solution.py:128
  228.0 4.3 %all-to-all-start.2 = ((bf16[8,40,2560]{2,1,0:T(8,128)(2,1)}), bf16[8,40,2560]{2,1,0:T(8,128)(2,1)S(1)}, u32[]{:S(2)}, u32[]{:S(2)}) async-start(bf16[8,40,2560]{2,1,0:T(8,128)(2,1)} %bitcast.63), calls=%async_computation.2 | async-start | bytes 3276800 | tf_op jit(solution)/shard_map/all_to_all | solution.py:145
  232.3 2.5 gather_fusion.2
  234.8 27.3 %all-to-all-done.2 = bf16[8,40,2560]{2,1,0:T(8,128)(2,1)S(1)} async-done(((bf16[8,40,2560]{2,1,0:T(8,128)(2,1)}), bf16[8,40,2560]{2,1,0:T(8,128)(2,1)S(1)}, u32[]{:S(2)}, u32[]{:S(2)}) %all-to-all-start.2) | async-done | bytes 1638432 | tf_op jit(solution)/shard_map/all_to_all | solution.py:145
  263.5 2.8 multiply_convert_fusion
  266.3 14.8 %reduce-scatter.2.cloned.1.call-done = bf16[3,160,384]{2,1,0:T(8,128)(2,1)} async-done(((bf16[3,2560,384]{2,1,0:T(8,128)(2,1)}), bf16[3,160,384]{2,1,0:T(8,128)(2,1)}) %reduce-scatter.2.cloned.1.call-update) | async-done | bytes 368656 | tf_op jit(solution)/shard_map/reduce_scatter | solution.py:51
  281.1 1.8 collective-permute-start.7
  (65 shorter events, 24.4 us)
Async XLA Ops:
  7.2 10.6 %copy-start = (bf16[256,2560]{1,0:T(8,128)(2,1)S(1)}, bf16[256,2560]{1,0:T(8,128)(2,1)}, u32[]{:S(2)}) copy-start(bf16[256,2560]{1,0:T(8,128)(2,1)} %param.11) | copy-start | bytes 3932164
  7.2 8.2 %copy-start.4 = (s32[256,1]{0,1:T(1,128)S(1)}, s32[256,1]{0,1:T(1,128)}, u32[]{:S(2)}) copy-start(s32[256,1]{0,1:T(1,128)} %param.12) | copy-start | bytes 3076
  7.2 123.5 %all-gather.2.cloned.1.call-start = ((), (), s32[]{:S(2)}) async-start(), calls=%async_computation.4 | async-start | bytes 6266880 | tf_op jit(solution)/shard_map/all_gather | solution.py:38
  10.1 4.4 %collective-permute-start = (bf16[3,80,384]{2,1,0:T(8,128)(2,1)S(1)}, bf16[3,80,384]{2,1,0:T(8,128)(2,1)S(1)}, u32[]{:S(2)}, u32[]{:S(2)}) collective-permute-start(bf16[3,80,384]{2,1,0:T(8,128)(2,1)S(1)} %get-tuple-element.21), channel_id=1, source_target_pairs={{0,8},{8,0},{1,9},{9,1},{2,10},{10,2},{3,11},{11,3},{4,12},{12,4},... | collective-permute-start | bytes 552968 | tf_op jit(solution)/shard_map/ppermute | solution.py:25
  17.8 2.6 copy-start.5
  31.3 105.8 %all-to-all-start = ((bf16[2,8,40,2560]{3,2,0,1:T(8,128)(2,1)}), bf16[2,8,40,2560]{3,2,0,1:T(8,128)(2,1)S(1)}, u32[]{:S(2)}, u32[]{:S(2)}) async-start(bf16[2,8,40,2560]{3,2,0,1:T(8,128)(2,1)} %pad_maximum_fusion.1), calls=%async_computation | async-start | bytes 6553600 | tf_op jit(solution)/shard_map/all_to_all | solution.py:105
  35.1 246.0 %reduce-scatter.2.cloned.1.call-start = ((), (), s32[]{:S(2)}) async-start(), calls=%async_computation.5 | async-start | bytes 6266880 | tf_op jit(solution)/shard_map/reduce_scatter | solution.py:51
  136.2 6.7 %collective-permute-start.3 = (bf16[2560,384]{1,0:T(8,128)(2,1)}, bf16[2560,384]{1,0:T(8,128)(2,1)}, u32[]{:S(2)}, u32[]{:S(2)}) collective-permute-start(bf16[2560,384]{1,0:T(8,128)(2,1)} %get-tuple-element.9), channel_id=1, source_target_pairs={{0,8},{8,0},{1,9},{9,1},{2,10},{10,2},{3,11},{11,3},{4,12},{12,4},... | collective-permute-start | bytes 5898248 | tf_op jit(solution)/shard_map/ppermute | solution.py:25
  136.6 8.8 %collective-permute-start.1 = (bf16[2560,384]{1,0:T(8,128)(2,1)}, bf16[2560,384]{1,0:T(8,128)(2,1)}, u32[]{:S(2)}, u32[]{:S(2)}) collective-permute-start(bf16[2560,384]{1,0:T(8,128)(2,1)} %get-tuple-element.11), channel_id=1, source_target_pairs={{0,8},{8,0},{1,9},{9,1},{2,10},{10,2},{3,11},{11,3},{4,12},{12,4},... | collective-permute-start | bytes 5898248 | tf_op jit(solution)/shard_map/ppermute | solution.py:25
  136.7 11.3 %collective-permute-start.2 = (bf16[2560,384]{1,0:T(8,128)(2,1)}, bf16[2560,384]{1,0:T(8,128)(2,1)}, u32[]{:S(2)}, u32[]{:S(2)}) collective-permute-start(bf16[2560,384]{1,0:T(8,128)(2,1)} %get-tuple-element.10), channel_id=1, source_target_pairs={{0,8},{8,0},{1,9},{9,1},{2,10},{10,2},{3,11},{11,3},{4,12},{12,4},... | collective-permute-start | bytes 5898248 | tf_op jit(solution)/shard_map/ppermute | solution.py:25
  137.2 2.7 copy-start.2
  152.7 4.1 %collective-permute-start.6 = (bf16[2560,384]{1,0:T(8,128)(2,1)S(1)}, bf16[2560,384]{1,0:T(8,128)(2,1)S(1)}, u32[]{:S(2)}, u32[]{:S(2)}) collective-permute-start(bf16[2560,384]{1,0:T(8,128)(2,1)S(1)} %convolution_convert_fusion), channel_id=1, source_target_pairs={{0,8},{8,0},{1,9},{9,1},{2,10},{10,2},{3,11},{11,3},{4,12},{12,4},... | collective-permute-start | bytes 5898248 | tf_op jit(solution)/shard_map/ppermute | solution.py:25
  154.3 5.3 %collective-permute-start.5 = (bf16[2560,384]{1,0:T(8,128)(2,1)S(1)}, bf16[2560,384]{1,0:T(8,128)(2,1)S(1)}, u32[]{:S(2)}, u32[]{:S(2)}) collective-permute-start(bf16[2560,384]{1,0:T(8,128)(2,1)S(1)} %convolution_convert_fusion.2), channel_id=1, source_target_pairs={{0,8},{8,0},{1,9},{9,1},{2,10},{10,2},{3,11},{11,3},{4,12},{12,4},... | collective-permute-start | bytes 5898248 | tf_op jit(solution)/shard_map/ppermute | solution.py:25
  156.2 6.2 %collective-permute-start.4 = (bf16[2560,384]{1,0:T(8,128)(2,1)S(1)}, bf16[2560,384]{1,0:T(8,128)(2,1)S(1)}, u32[]{:S(2)}, u32[]{:S(2)}) collective-permute-start(bf16[2560,384]{1,0:T(8,128)(2,1)S(1)} %convolution_convert_fusion.4), channel_id=1, source_target_pairs={{0,8},{8,0},{1,9},{9,1},{2,10},{10,2},{3,11},{11,3},{4,12},{12,4},... | collective-permute-start | bytes 5898248 | tf_op jit(solution)/shard_map/ppermute | solution.py:25
  173.8 54.2 %all-to-all-start.1 = ((bf16[8,40,2560]{2,1,0:T(8,128)(2,1)}), bf16[8,40,2560]{2,1,0:T(8,128)(2,1)S(1)}, u32[]{:S(2)}, u32[]{:S(2)}) async-start(bf16[8,40,2560]{2,1,0:T(8,128)(2,1)} %bitcast.15), calls=%async_computation.1 | async-start | bytes 3276800 | tf_op jit(solution)/shard_map/all_to_all | solution.py:128
  228.0 34.1 %all-to-all-start.2 = ((bf16[8,40,2560]{2,1,0:T(8,128)(2,1)}), bf16[8,40,2560]{2,1,0:T(8,128)(2,1)S(1)}, u32[]{:S(2)}, u32[]{:S(2)}) async-start(bf16[8,40,2560]{2,1,0:T(8,128)(2,1)} %bitcast.63), calls=%async_computation.2 | async-start | bytes 3276800 | tf_op jit(solution)/shard_map/all_to_all | solution.py:145
  281.1 3.0 %copy-start.3 = (bf16[3,160,384]{2,1,0:T(8,128)(2,1)S(1)}, bf16[3,160,384]{2,1,0:T(8,128)(2,1)}, u32[]{:S(2)}) copy-start(bf16[3,160,384]{2,1,0:T(8,128)(2,1)} %reduce-scatter.2.cloned.1.call-done) | copy-start | bytes 1105924
  281.1 3.3 %collective-permute-start.7 = (bf16[3,160,384]{2,1,0:T(8,128)(2,1)}, bf16[3,160,384]{2,1,0:T(8,128)(2,1)S(1)}, u32[]{:S(2)}, u32[]{:S(2)}) collective-permute-start(bf16[3,160,384]{2,1,0:T(8,128)(2,1)} %reduce-scatter.2.cloned.1.call-done), channel_id=1, source_target_pairs={{0,8},{8,0},{1,9},{9,1},{2,10},{10,2},{3,11},{11,3},{4,12},{12,4},... | collective-permute-start | bytes 1105928 | tf_op jit(solution)/shard_map/ppermute | solution.py:25
  284.1 1.3 copy-start.1
Sparse Core Ops, SparseCore 0:
  15.5 115.1 all-gather.1
  167.4 113.5 reduce-scatter.1

commit v8 on v5

--- a/solution.py
+++ b/solution.py
@@ -40,16 +40,16 @@
     return [(own[i], other[i]) for i in range(len(weights))]
 
 
-def scatter_grads(*parts):
-    pair_sums = []
-    for own, other in parts:
-        arrived = swap_cores(other.astype(jnp.bfloat16))
-        pair_sums.append(
-            (own.astype(jnp.bfloat16).astype(jnp.float32) + arrived.astype(jnp.float32)).astype(
-                jnp.bfloat16
-            )
-        )
-    chip_sum = lax.psum_scatter(jnp.stack(pair_sums), CHIPS, scatter_dimension=1, tiled=True)
+def scatter_grads(lefts, rights):
+    half = rights.shape[2] // 2
+    batched = (((1,), (1,)), ((0,), (0,)))
+    other = lax.dot_general(lefts, rights[:, :, half:], batched, preferred_element_type=jnp.float32)
+    arrived = swap_cores(other.astype(jnp.bfloat16))
+    own = lax.dot_general(lefts, rights[:, :, :half], batched, preferred_element_type=jnp.float32)
+    pair_sum = (own.astype(jnp.bfloat16).astype(jnp.float32) + arrived.astype(jnp.float32)).astype(
+        jnp.bfloat16
+    )
+    chip_sum = lax.psum_scatter(pair_sum, CHIPS, scatter_dimension=1, tiled=True)
     first = lax.axis_index("core") == 0
     rows = chip_sum.shape[1] // 2
 
@@ -61,7 +61,7 @@
     block = jnp.where(
         first, jnp.concatenate([mine, theirs], axis=2), jnp.concatenate([theirs, mine], axis=2)
     )
-    return [block[i] for i in range(len(parts))]
+    return [block[i] for i in range(block.shape[0])]
 
 
 def halves(left, pair, dims):
@@ -152,9 +152,7 @@
     )
     grad_tokens = jnp.take(arrived.reshape(slot_count, model_width), slot_index, axis=0)
     grad_gate, grad_up, grad_down = scatter_grads(
-        (contract_first(received, gate_delta[:, :half]), contract_first(received, gate_delta[:, half:])),
-        (contract_first(received, up_delta[:, :half]), contract_first(received, up_delta[:, half:])),
-        (contract_first(grad_rows, hidden[:, :half]), contract_first(grad_rows, hidden[:, half:])),
+        jnp.stack([received, received, grad_rows]), jnp.stack([gate_delta, up_delta, hidden])
     )
     return (moe_out, grad_tokens, grad_gate[None], grad_up[None], grad_down[None])
 

time: 291 us -> 297 us (1.021)
  waiting for transfers between devices: 184 us -> 188 us
  matrix products: 37.4 us -> 40.8 us
    ppermute x6 -> x4, waiting for transfers between devices: 7.71 us -> 14.5 us  [swap_cores(): return lax.ppermute(value, 'core', perm=[(0, 1), (1, 0)])]
    another operation x3, other arithmetic: 4.06 us -> 0.78 us  [the longest x1 3.44 us: scatter_grads(): jnp.stack(pair_sums)]
    all_to_all x1, waiting for transfers between devices: 27.5 us -> 24.3 us  [shards(): lax.all_to_all(token_grad.reshape(experts, capacity, model_width), 'exper...]
    dot_general x6 -> x2, matrix products: 8.6 us -> 11.8 us  [the longest x1 7.71 us: scatter_grads(): lax.dot_general(lefts, rights[:, :, :half], batched, preferred_element_ty...]
    all_to_all x1, waiting for transfers between devices: 38.2 us -> 41.3 us  [shards(): lax.all_to_all(expert_out, 'expert', split_axis=0, concat_axis=0, tiled=T...]
    ppermute x6 -> x4, starting transfers between devices: 6.79 us -> 6.24 us  [swap_cores(): return lax.ppermute(value, 'core', perm=[(0, 1), (1, 0)])]
  transfers between devices with their start and end apart: 11 -> 9, of which waited for: 9 -> 8; matrix products, arithmetic and copies ran while one was open for 18% -> 16% of each run, Pallas kernels for 0% -> 0%
where the time goes in v8:
time: 297 us; the launch traced here: 296 us
  waiting for transfers between devices  188 us (63%)
  matrix products  40.8 us (14%)
  local copies, waits for them, and re-layouts  20.7 us (7%)
  starting transfers between devices  18 us (6%)
  between operations  14.4 us (5%)
  other arithmetic  13.9 us (5%)
    all_gather x1, waiting for transfers between devices, gather_weights(): own = lax.all_gather(own, CHIPS, axis=1, tiled=True)  94.9 us
    all_to_all x1, waiting for transfers between devices, shards(): lax.all_to_all(expert_out, 'expert', split_axis=0, concat_axis=0, tiled=T...  41.3 us
    all_to_all x1, waiting for transfers between devices, shards(): lax.all_to_all(token_grad.reshape(experts, capacity, model_width), 'exper...  24.3 us
    dot_general x6, matrix products, contract_last(): lax.dot_general(matrix_a, matrix_b, (((1,), (1,)), ((), ())), preferred_e...  18.1 us
    ppermute x4, waiting for transfers between devices, swap_cores(): return lax.ppermute(value, 'core', perm=[(0, 1), (1, 0)])  14.5 us
    reduce_scatter x1, waiting for transfers between devices, scatter_grads(): lax.psum_scatter(pair_sum, CHIPS, scatter_dimension=1, tiled=True)  13.3 us
    dot_general x3, matrix products, halves(): lax.dot_general(left, pair[1], dims, preferred_element_type=jnp.float32)  7.83 us
    dot_general x1, matrix products, scatter_grads(): lax.dot_general(lefts, rights[:, :, :half], batched, preferred_element_ty...  7.71 us
  transfers between devices with their start and end apart: 9, of which 8 were waited for; matrix products, arithmetic and copies ran while one was open for 16% of the time, Pallas kernels for 0%

profile of v8, /device:TPU:1, one launch (start us, length us, event | category | flops | bytes accessed | tf_op | source)
XLA Modules:
  0.0 296.1 jit_solution(7710126701006663529)
XLA Ops:
  10.1 3.3 %collective-permute-start = (bf16[3,80,384]{2,1,0:T(8,128)(2,1)S(1)}, bf16[3,80,384]{2,1,0:T(8,128)(2,1)S(1)}, u32[]{:S(2)}, u32[]{:S(2)}) collective-permute-start(bf16[3,80,384]{2,1,0:T(8,128)(2,1)S(1)} %get-tuple-element.21), channel_id=1, source_target_pairs={{0,8},{8,0},{1,9},{9,1},{2,10},{10,2},{3,11},{11,3},{4,12},{12,4},... | collective-permute-start | bytes 552968 | tf_op jit(solution)/shard_map/ppermute | solution.py:25
  17.8 1.6 multiply_convert_fusion.1
  19.4 3.2 %gather_fusion.1 = bf16[320,2560]{1,0:T(8,128)(2,1)} fusion(bf16[256,2560]{1,0:T(8,128)(2,1)S(1)} %multiply_convert_fusion.1, s32[1024]{0:T(1024)S(1)} %pad_clamp_fusion.1), kind=kCustom, calls=%fused_computation.2.clone | custom fusion | bytes 3278080 | tf_op jit(solution)/shard_map/jit(_take)/gather | solution.py:98
  22.6 3.2 %gather_fusion = bf16[320,2560]{1,0:T(8,128)(2,1)} fusion(bf16[256,2560]{1,0:T(8,128)(2,1)S(1)} %copy-done, s32[1024]{0:T(1024)S(1)} %pad_clamp_fusion.1), kind=kCustom, calls=%fused_computation.clone | custom fusion | bytes 3278080 | tf_op jit(solution)/shard_map/jit(_take)/gather | solution.py:98
  25.8 2.2 scatter_custom_fusion.1
  28.0 1.9 select_multiply_fusion.1
  29.9 2.0 pad_maximum_fusion.1
  31.9 3.7 %all-to-all-start = ((bf16[2,8,40,2560]{3,2,0,1:T(8,128)(2,1)}), bf16[2,8,40,2560]{3,2,0,1:T(8,128)(2,1)S(1)}, u32[]{:S(2)}, u32[]{:S(2)}) async-start(bf16[2,8,40,2560]{3,2,0,1:T(8,128)(2,1)} %pad_maximum_fusion.1), calls=%async_computation | async-start | bytes 6553600 | tf_op jit(solution)/shard_map/all_to_all | solution.py:106
  35.7 94.9 %all-gather.2.cloned.1.call-done = bf16[3,2560,384]{2,1,0:T(8,128)(2,1)} async-done(((bf16[3,160,384]{2,1,0:T(8,128)(2,1)}), bf16[3,2560,384]{2,1,0:T(8,128)(2,1)}) %all-gather.2.cloned.1.call-update) | async-done | bytes 5898256 | tf_op jit(solution)/shard_map/all_gather | solution.py:38
  131.4 2.4 copy-done.3
  136.9 3.8 %collective-permute-done.1 = bf16[3,2560,384]{2,1,0:T(8,128)(2,1)} collective-permute-done((bf16[3,2560,384]{2,1,0:T(8,128)(2,1)}, bf16[3,2560,384]{2,1,0:T(8,128)(2,1)}, u32[]{:S(2)}, u32[]{:S(2)}) %collective-permute-start.1) | collective-permute-done | bytes 5898272 | tf_op jit(solution)/shard_map/ppermute | solution.py:25
  140.7 2.5 fusion.9
  143.2 2.5 fusion.6
  145.8 2.7 fusion.4
  149.5 4.1 %convolution_convert_fusion = bf16[3,2560,384]{2,1,0:T(8,128)(2,1)S(1)} fusion(bf16[1,320,2560]{2,1,0:T(8,128)(2,1)S(1)} %bitcast.78, bf16[1,320,2560]{2,1,0:T(8,128)(2,1)S(1)} %bitcast.84, bf16[3,320,768]{2,1,0:T(8,128)(2,1)S(1)} %pad_maximum_fusion.4), kind=kOutput, calls=%fused_computation.7 | convolution fusion | flops 1895301120 | bytes 9912320 | tf_op jit(solution)/shard_map/dot_general | solution.py:46
  154.1 9.4 %collective-permute-done.2 = bf16[3,2560,384]{2,1,0:T(8,128)(2,1)} collective-permute-done((bf16[3,2560,384]{2,1,0:T(8,128)(2,1)S(1)}, bf16[3,2560,384]{2,1,0:T(8,128)(2,1)}, u32[]{:S(2)}, u32[]{:S(2)}) %collective-permute-start.2) | collective-permute-done | bytes 5898272 | tf_op jit(solution)/shard_map/ppermute | solution.py:25
  163.4 7.7 %add_convert_fusion = bf16[3,2560,384]{2,1,0:T(8,128)(2,1)} fusion(bf16[3,2560,384]{2,1,0:T(8,128)(2,1)} %collective-permute-done.2, bf16[1,320,2560]{2,1,0:T(8,128)(2,1)S(1)} %bitcast.79, bf16[1,320,2560]{2,1,0:T(8,128)(2,1)S(1)} %bitcast.85, bf16[3,320,768]{2,1,0:T(8,128)(2,1)S(1)} %pad_maximum_fusion.4), kind=kOutput, calls=%fused_computation.6 | convolution fusion | flops 1907097600 | bytes 15810560 | tf_op jit(solution)/shard_map/dot_general | solution.py:48
  171.1 1.7 multiply_convert_fusion.5
  172.9 2.6 fusion.8
  175.5 3.8 %fusion = bf16[320,2560]{1,0:T(8,128)(2,1)} fusion(f32[320,2560]{1,0:T(8,128)S(1)} %fusion.8, bf16[3,2560,384]{2,1,0:T(8,128)(2,1)} %collective-permute-done.1, bf16[320,768]{1,0:T(8,128)(2,1)S(1)} %get-tuple-element.16), kind=kOutput, calls=%fused_computation.14 | convolution fusion | flops 630784000 | bytes 7127040 | tf_op jit(solution)/shard_map/dot_general | solution.py:13
  179.3 4.4 %all-to-all-start.1 = ((bf16[8,40,2560]{2,1,0:T(8,128)(2,1)}), bf16[8,40,2560]{2,1,0:T(8,128)(2,1)S(1)}, u32[]{:S(2)}, u32[]{:S(2)}) async-start(bf16[8,40,2560]{2,1,0:T(8,128)(2,1)} %bitcast.18), calls=%async_computation.1 | async-start | bytes 3276800 | tf_op jit(solution)/shard_map/all_to_all | solution.py:129
  183.7 2.6 fusion.2
  186.3 2.7 convolution_add_fusion.2
  189.0 2.6 convolution_add_fusion.1
  191.6 3.8 %fusion.1 = bf16[320,2560]{1,0:T(8,128)(2,1)} fusion(f32[320,2560]{1,0:T(8,128)S(1)} %convolution_add_fusion.1, bf16[3,2560,384]{2,1,0:T(8,128)(2,1)} %collective-permute-done.1, bf16[320,768]{1,0:T(8,128)(2,1)S(1)} %get-tuple-element.14), kind=kOutput, calls=%fused_computation.15 | convolution fusion | flops 630784000 | bytes 7127040 | tf_op jit(solution)/shard_map/dot_general | solution.py:13
  195.5 41.3 %all-to-all-done.1 = bf16[8,40,2560]{2,1,0:T(8,128)(2,1)S(1)} async-done(((bf16[8,40,2560]{2,1,0:T(8,128)(2,1)}), bf16[8,40,2560]{2,1,0:T(8,128)(2,1)S(1)}, u32[]{:S(2)}, u32[]{:S(2)}) %all-to-all-start.1) | async-done | bytes 1638432 | tf_op jit(solution)/shard_map/all_to_all | solution.py:129
  236.7 3.6 %all-to-all-start.2 = ((bf16[8,40,2560]{2,1,0:T(8,128)(2,1)}), bf16[8,40,2560]{2,1,0:T(8,128)(2,1)S(1)}, u32[]{:S(2)}, u32[]{:S(2)}) async-start(bf16[8,40,2560]{2,1,0:T(8,128)(2,1)} %bitcast.67), calls=%async_computation.2 | async-start | bytes 3276800 | tf_op jit(solution)/shard_map/all_to_all | solution.py:146
  240.4 2.5 gather_fusion.2
  242.9 24.3 %all-to-all-done.2 = bf16[8,40,2560]{2,1,0:T(8,128)(2,1)S(1)} async-done(((bf16[8,40,2560]{2,1,0:T(8,128)(2,1)}), bf16[8,40,2560]{2,1,0:T(8,128)(2,1)S(1)}, u32[]{:S(2)}, u32[]{:S(2)}) %all-to-all-start.2) | async-done | bytes 1638432 | tf_op jit(solution)/shard_map/all_to_all | solution.py:146
  268.6 2.8 multiply_convert_fusion
  271.3 13.3 %reduce-scatter.2.cloned.1.call-done = bf16[3,160,384]{2,1,0:T(8,128)(2,1)} async-done(((bf16[3,2560,384]{2,1,0:T(8,128)(2,1)}), bf16[3,160,384]{2,1,0:T(8,128)(2,1)}) %reduce-scatter.2.cloned.1.call-update) | async-done | bytes 368656 | tf_op jit(solution)/shard_map/reduce_scatter | solution.py:52
  284.7 2.0 collective-permute-start.3
  (59 shorter events, 16.4 us)
Async XLA Ops:
  7.2 15.5 %copy-start = (bf16[256,2560]{1,0:T(8,128)(2,1)S(1)}, bf16[256,2560]{1,0:T(8,128)(2,1)}, u32[]{:S(2)}) copy-start(bf16[256,2560]{1,0:T(8,128)(2,1)} %param.11) | copy-start | bytes 3932164
  7.2 8.2 %copy-start.7 = (s32[256,1]{0,1:T(1,128)S(1)}, s32[256,1]{0,1:T(1,128)}, u32[]{:S(2)}) copy-start(s32[256,1]{0,1:T(1,128)} %param.12) | copy-start | bytes 3076
  7.2 10.6 %copy-start.8 = (s32[256,1]{0,1:T(1,128)S(1)}, s32[256,1]{0,1:T(1,128)}, u32[]{:S(2)}) copy-start(s32[256,1]{0,1:T(1,128)} %param.13) | copy-start | bytes 3076
  7.2 123.5 %all-gather.2.cloned.1.call-start = ((), (), s32[]{:S(2)}) async-start(), calls=%async_computation.4 | async-start | bytes 6266880 | tf_op jit(solution)/shard_map/all_gather | solution.py:38
  10.1 4.4 %collective-permute-start = (bf16[3,80,384]{2,1,0:T(8,128)(2,1)S(1)}, bf16[3,80,384]{2,1,0:T(8,128)(2,1)S(1)}, u32[]{:S(2)}, u32[]{:S(2)}) collective-permute-start(bf16[3,80,384]{2,1,0:T(8,128)(2,1)S(1)} %get-tuple-element.21), channel_id=1, source_target_pairs={{0,8},{8,0},{1,9},{9,1},{2,10},{10,2},{3,11},{11,3},{4,12},{12,4},... | collective-permute-start | bytes 552968 | tf_op jit(solution)/shard_map/ppermute | solution.py:25
  22.6 5.3 %copy-start.2 = (bf16[320,2560]{1,0:T(8,128)(2,1)S(1)}, bf16[320,2560]{1,0:T(8,128)(2,1)}, u32[]{:S(2)}) copy-start(bf16[320,2560]{1,0:T(8,128)(2,1)} %gather_fusion.1) | copy-start | bytes 4915204
  31.9 99.2 %all-to-all-start = ((bf16[2,8,40,2560]{3,2,0,1:T(8,128)(2,1)}), bf16[2,8,40,2560]{3,2,0,1:T(8,128)(2,1)S(1)}, u32[]{:S(2)}, u32[]{:S(2)}) async-start(bf16[2,8,40,2560]{3,2,0,1:T(8,128)(2,1)} %pad_maximum_fusion.1), calls=%async_computation | async-start | bytes 6553600 | tf_op jit(solution)/shard_map/all_to_all | solution.py:106
  35.7 249.0 %reduce-scatter.2.cloned.1.call-start = ((), (), s32[]{:S(2)}) async-start(), calls=%async_computation.5 | async-start | bytes 6266880 | tf_op jit(solution)/shard_map/reduce_scatter | solution.py:52
  130.7 10.0 %collective-permute-start.1 = (bf16[3,2560,384]{2,1,0:T(8,128)(2,1)}, bf16[3,2560,384]{2,1,0:T(8,128)(2,1)}, u32[]{:S(2)}, u32[]{:S(2)}) collective-permute-start(bf16[3,2560,384]{2,1,0:T(8,128)(2,1)} %all-gather.2.cloned.1.call-done), channel_id=1, source_target_pairs={{0,8},{8,0},{1,9},{9,1},{2,10},{10,2},{3,11},{11,3},{4,12},{12,4},... | collective-permute-start | bytes 17694728 | tf_op jit(solution)/shard_map/ppermute | solution.py:25
  131.1 2.7 copy-start.3
  145.8 2.8 copy-start.4
  148.6 0.8 copy-start.5
  153.6 9.8 %collective-permute-start.2 = (bf16[3,2560,384]{2,1,0:T(8,128)(2,1)S(1)}, bf16[3,2560,384]{2,1,0:T(8,128)(2,1)}, u32[]{:S(2)}, u32[]{:S(2)}) collective-permute-start(bf16[3,2560,384]{2,1,0:T(8,128)(2,1)S(1)} %convolution_convert_fusion), channel_id=1, source_target_pairs={{0,8},{8,0},{1,9},{9,1},{2,10},{10,2},{3,11},{11,3},{4,12},{12,4},... | collective-permute-start | bytes 17694728 | tf_op jit(solution)/shard_map/ppermute | solution.py:25
  179.3 57.4 %all-to-all-start.1 = ((bf16[8,40,2560]{2,1,0:T(8,128)(2,1)}), bf16[8,40,2560]{2,1,0:T(8,128)(2,1)S(1)}, u32[]{:S(2)}, u32[]{:S(2)}) async-start(bf16[8,40,2560]{2,1,0:T(8,128)(2,1)} %bitcast.18), calls=%async_computation.1 | async-start | bytes 3276800 | tf_op jit(solution)/shard_map/all_to_all | solution.py:129
  236.7 30.4 %all-to-all-start.2 = ((bf16[8,40,2560]{2,1,0:T(8,128)(2,1)}), bf16[8,40,2560]{2,1,0:T(8,128)(2,1)S(1)}, u32[]{:S(2)}, u32[]{:S(2)}) async-start(bf16[8,40,2560]{2,1,0:T(8,128)(2,1)} %bitcast.67), calls=%async_computation.2 | async-start | bytes 3276800 | tf_op jit(solution)/shard_map/all_to_all | solution.py:146
  284.7 3.2 %copy-start.6 = (bf16[3,160,384]{2,1,0:T(8,128)(2,1)S(1)}, bf16[3,160,384]{2,1,0:T(8,128)(2,1)}, u32[]{:S(2)}) copy-start(bf16[3,160,384]{2,1,0:T(8,128)(2,1)} %reduce-scatter.2.cloned.1.call-done) | copy-start | bytes 1105924
  284.7 3.5 %collective-permute-start.3 = (bf16[3,160,384]{2,1,0:T(8,128)(2,1)}, bf16[3,160,384]{2,1,0:T(8,128)(2,1)S(1)}, u32[]{:S(2)}, u32[]{:S(2)}) collective-permute-start(bf16[3,160,384]{2,1,0:T(8,128)(2,1)} %reduce-scatter.2.cloned.1.call-done), channel_id=1, source_target_pairs={{0,8},{8,0},{1,9},{9,1},{2,10},{10,2},{3,11},{11,3},{4,12},{12,4},... | collective-permute-start | bytes 1105928 | tf_op jit(solution)/shard_map/ppermute | solution.py:25
  287.9 1.3 copy-start.1
Sparse Core Ops, SparseCore 0:
  15.5 115.1 all-gather.1
  171.3 113.3 reduce-scatter.1

commit v9 on v7

v9 whole, which is shorter than its diff:
```python
import jax
import jax.numpy as jnp
from jax import lax
from jax.sharding import Mesh
from jax.sharding import PartitionSpec as P

TOP = 1
CHIPS = ("x", "zh")
DP = ("x", "zh", "core")


def contract_last(matrix_a, matrix_b):
    return lax.dot_general(
        matrix_a, matrix_b, (((1,), (1,)), ((), ())), preferred_element_type=jnp.float32
    )


def contract_first(matrix_a, matrix_b):
    return lax.dot_general(
        matrix_a, matrix_b, (((0,), (0,)), ((), ())), preferred_element_type=jnp.float32
    )


def swap_cores(value):
    return lax.ppermute(value, "core", perm=[(0, 1), (1, 0)])


def gather_weights(*weights):
    half = weights[0].shape[1] // 2
    first = lax.axis_index("core") == 0
    kept = jnp.stack([jnp.where(first, w[:, :half], w[:, half:]) for w in weights])
    sent = jnp.stack([jnp.where(first, w[:, half:], w[:, :half]) for w in weights])
    came = swap_cores(sent)
    own = jnp.where(
        first, jnp.concatenate([kept, came], axis=1), jnp.concatenate([came, kept], axis=1)
    )
    own = lax.all_gather(own, CHIPS, axis=1, tiled=True)
    return [own[i] for i in range(len(weights))]


def scatter_grads(*parts):
    stacked = jnp.stack(parts).astype(jnp.bfloat16)
    chip_sum = lax.psum_scatter(stacked, CHIPS, scatter_dimension=1, tiled=True)
    first = lax.axis_index("core") == 0
    rows = chip_sum.shape[1] // 2

    def my_rows(value):
        return jnp.where(first, value[:, :rows], value[:, rows:]).astype(jnp.float32)

    mine = my_rows(chip_sum)
    theirs = my_rows(swap_cores(chip_sum))
    block = jnp.where(
        first, jnp.concatenate([mine, theirs], axis=2), jnp.concatenate([theirs, mine], axis=2)
    )
    return [block[i] for i in range(len(parts))]


def pair_total(partial, slots):
    arrived = swap_cores(partial[slots:])
    return (partial[:slots] + arrived).astype(jnp.bfloat16)


def shards(tokens, routes, gate_levels, w_gate, w_up, w_down, grad_out):
    experts = lax.axis_size("expert")
    tok_rows = tokens.shape[0]
    model_width = tokens.shape[1]
    capacity = min(tok_rows, tok_rows * TOP * 5 // (4 * experts))
    slot_count = experts * capacity
    expert_of = routes[:, 0]
    onehot = (expert_of[:, None] == jnp.arange(experts, dtype=jnp.int32)[None, :]).astype(jnp.int32)
    earlier = jnp.cumsum(onehot, axis=0) - onehot
    slot_rank = jnp.sum(earlier * onehot, axis=1)
    slot_index = expert_of * capacity + slot_rank
    source_row = (
        jnp.zeros((slot_count,), jnp.int32)
        .at[slot_index]
        .set(jnp.arange(tok_rows, dtype=jnp.int32))
    )
    filled = (
        jnp.zeros((slot_count, 1), jnp.bfloat16)
        .at[slot_index, 0]
        .set(jnp.ones((tok_rows,), jnp.bfloat16))
    )
    gate_weight = gate_levels.astype(jnp.float32) / 64.0

    def pack_rows(values):
        return (jnp.take(values, source_row, axis=0) * filled).reshape(
            experts, capacity, model_width
        )

    gate_own, up_own, down_own = gather_weights(w_gate[0], w_up[0], w_down[0])
    out_grad = (gate_weight * grad_out.astype(jnp.float32)).astype(jnp.bfloat16)
    both_rows = lax.all_to_all(
        jnp.stack([pack_rows(tokens), pack_rows(out_grad)]),
        "expert",
        split_axis=1,
        concat_axis=1,
        tiled=True,
    ).reshape(2, slot_count, model_width)
    pair_rows = jnp.concatenate([both_rows, swap_cores(both_rows)], axis=1)
    received = pair_rows[0]
    grad_rows = pair_rows[1]
    act_gate = jnp.dot(received, gate_own, preferred_element_type=jnp.float32)
    act_up = jnp.dot(received, up_own, preferred_element_type=jnp.float32)
    sigmoid_gate = jax.nn.sigmoid(act_gate)
    silu_gate = act_gate * sigmoid_gate
    hidden = (silu_gate * act_up).astype(jnp.bfloat16)
    hidden_grad = jnp.dot(grad_rows, down_own, preferred_element_type=jnp.float32)
    gate_delta = (
        hidden_grad * act_up * sigmoid_gate * (1.0 + act_gate * (1.0 - sigmoid_gate))
    ).astype(jnp.bfloat16)
    up_delta = (hidden_grad * silu_gate).astype(jnp.bfloat16)
    grad_gate, grad_up, grad_down = scatter_grads(
        contract_first(received, gate_delta),
        contract_first(received, up_delta),
        contract_first(grad_rows, hidden),
    )
    expert_out = pair_total(contract_last(hidden, down_own), slot_count).reshape(
        experts, capacity, model_width
    )
    returned = lax.all_to_all(
        expert_out, "expert", split_axis=0, concat_axis=0, tiled=True
    ).reshape(slot_count, model_width)
    moe_out = (gate_weight * jnp.take(returned, slot_index, axis=0).astype(jnp.float32)).astype(
        jnp.bfloat16
    )
    token_grad = pair_total(
        contract_last(gate_delta, gate_own) + contract_last(up_delta, up_own), slot_count
    )
    arrived = lax.all_to_all(
        token_grad.reshape(experts, capacity, model_width),
        "expert",
        split_axis=0,
        concat_axis=0,
        tiled=True,
    )
    grad_tokens = jnp.take(arrived.reshape(slot_count, model_width), slot_index, axis=0)
    return (moe_out, grad_tokens, grad_gate[None], grad_up[None], grad_down[None])


def solution(mesh):
    dp_size, expert_size = mesh.devices.shape
    chips = dp_size // 2
    x_size = 4 if chips % 4 == 0 else 1
    grid = mesh.devices.reshape(x_size, chips // x_size, 2, expert_size)
    fine = Mesh(grid, DP + ("expert",))
    rows = P(DP + ("expert",), None)
    weights = P("expert", DP, None)
    in_specs = (rows, rows, rows, weights, weights, weights, rows)
    out_specs = (rows, rows, weights, weights, weights)
    return jax.shard_map(shards, mesh=fine, in_specs=in_specs, out_specs=out_specs, check_vma=False)
```

time: 293 us -> 281 us (0.959)
  waiting for transfers between devices: 180 us -> 86.3 us
  blocking collectives: 0 us -> 90.2 us
  matrix products: 37.4 us -> 22.2 us
  other arithmetic: 15.5 us -> 26.5 us
  starting transfers between devices: 19.7 us -> 15.4 us
    all_gather x1, waiting for transfers between devices: 95.5 us -> 2.63 us  [gather_weights(): own = lax.all_gather(own, CHIPS, axis=1, tiled=True)]
    all_to_all x0 -> x1, blocking collectives: none -> 90.2 us  [shards(): lax.all_to_all(jnp.stack([pack_rows(tokens), pack_rows(out_grad)]), 'expe...]
    all_to_all x1, waiting for transfers between devices: 27.3 us -> 51.4 us  [shards(): lax.all_to_all(token_grad.reshape(experts, capacity, model_width), 'exper...]
    all_to_all x1, waiting for transfers between devices: 38 us -> 23.6 us  [shards(): lax.all_to_all(expert_out, 'expert', split_axis=0, concat_axis=0, tiled=T...]
    reduce_scatter x1, waiting for transfers between devices: 14.8 us -> 2.93 us  [scatter_grads(): chip_sum = lax.psum_scatter(stacked, CHIPS, scatter_dimension=1, tiled=True)]
    dot_general x6 -> x3, matrix products: 18.1 us -> 7.39 us  [contract_last(): lax.dot_general(matrix_a, matrix_b, (((1,), (1,)), ((), ())), preferred_e...]
    squeeze x1 -> x0, local copies, waits for them, and re-layouts: 5.53 us -> none  [gather_weights(): return [(own[i], swap_cores(own[i])) for i in range(len(weights))]]
    convert_element_type x1 -> x2, other arithmetic: 0.72 us -> 6.07 us  [pair_total(): return (partial[:slots] + arrived).astype(jnp.bfloat16)]
  transfers between devices with their start and end apart: 13 -> 9, of which waited for: 9 -> 6; matrix products, arithmetic and copies ran while one was open for 21% -> 16% of each run, Pallas kernels for 0% -> 0%
where the time goes in v9:
time: 281 us; the launch traced here: 280 us
  blocking collectives  90.2 us (32%)
  waiting for transfers between devices  86.3 us (31%)
  other arithmetic  26.5 us (9%)
  local copies, waits for them, and re-layouts  24.9 us (9%)
  matrix products  22.2 us (8%)
  starting transfers between devices  15.4 us (5%)
  between operations  14.4 us (5%)
    all_to_all x1, blocking collectives, shards(): lax.all_to_all(jnp.stack([pack_rows(tokens), pack_rows(out_grad)]), 'expe...  90.2 us
    all_to_all x1, waiting for transfers between devices, shards(): lax.all_to_all(token_grad.reshape(experts, capacity, model_width), 'exper...  51.4 us
    all_to_all x1, waiting for transfers between devices, shards(): lax.all_to_all(expert_out, 'expert', split_axis=0, concat_axis=0, tiled=T...  23.6 us
    dot_general x3, matrix products, contract_last(): lax.dot_general(matrix_a, matrix_b, (((1,), (1,)), ((), ())), preferred_e...  7.39 us
    ppermute x5, starting transfers between devices, swap_cores(): return lax.ppermute(value, 'core', perm=[(0, 1), (1, 0)])  7.16 us
    unnamed x36, local copies, waits for them, and re-layouts  6.51 us
    gather x2, local copies, waits for them, and re-layouts, pack_rows(): jnp.take(values, source_row, axis=0) * filled  6.36 us
    dot_general x3, matrix products, contract_first(): lax.dot_general(matrix_a, matrix_b, (((0,), (0,)), ((), ())), preferred_e...  6.27 us
  transfers between devices with their start and end apart: 9, of which 6 were waited for; matrix products, arithmetic and copies ran while one was open for 16% of the time, Pallas kernels for 0%

profile of v9, /device:TPU:1, one launch (start us, length us, event | category | flops | bytes accessed | tf_op | source)
XLA Modules:
  0.0 280.0 jit_solution(12015024029465041838)
XLA Ops:
  9.2 3.3 %collective-permute-start.1 = (bf16[3,80,384]{2,1,0:T(8,128)(2,1)S(1)}, bf16[3,80,384]{2,1,0:T(8,128)(2,1)S(1)}, u32[]{:S(2)}, u32[]{:S(2)}) collective-permute-start(bf16[3,80,384]{2,1,0:T(8,128)(2,1)S(1)} %pad_maximum_fusion.3), channel_id=1, source_target_pairs={{0,8},{8,0},{1,9},{9,1},{2,10},{10,2},{3,11},{11,3},{4,12},{12,4},... | collective-permute-start | bytes 552968 | tf_op jit(solution)/shard_map/ppermute | solution.py:25
  20.2 3.2 %gather_fusion.1 = bf16[320,2560]{1,0:T(8,128)(2,1)} fusion(bf16[256,2560]{1,0:T(8,128)(2,1)S(1)} %multiply_convert_fusion.1, s32[1024]{0:T(1024)S(1)} %pad_clamp_fusion.1), kind=kCustom, calls=%fused_computation.2.clone | custom fusion | bytes 3278080 | tf_op jit(solution)/shard_map/jit(_take)/gather | solution.py:87
  23.4 3.2 %gather_fusion = bf16[320,2560]{1,0:T(8,128)(2,1)} fusion(bf16[256,2560]{1,0:T(8,128)(2,1)S(1)} %copy-done, s32[1024]{0:T(1024)S(1)} %pad_clamp_fusion.1), kind=kCustom, calls=%fused_computation.clone | custom fusion | bytes 3278080 | tf_op jit(solution)/shard_map/jit(_take)/gather | solution.py:87
  26.5 2.2 scatter_custom_fusion.1
  28.7 1.8 select_multiply_fusion.1
  30.9 90.2 %all_to_all.15 = bf16[2,8,40,2560]{3,2,0,1:T(8,128)(2,1)S(1)} all-to-all(bf16[2,8,40,2560]{3,2,0,1:T(8,128)(2,1)S(1)} %pad_maximum_fusion.2), channel_id=1, replica_groups=mesh['x'=4,'zh'=4,'core'=2,'expert'=8] {'expert'}, dimensions={1} | all-to-all | bytes 6553600 | tf_op jit(solution)/shard_map/all_to_all | solution.py:93
  122.6 5.5 %collective-permute-done = bf16[2,320,2560]{2,1,0:T(8,128)(2,1)S(1)} collective-permute-done((bf16[2,320,2560]{2,1,0:T(8,128)(2,1)S(1)}, bf16[2,320,2560]{2,1,0:T(8,128)(2,1)S(1)}, u32[]{:S(2)}, u32[]{:S(2)}) %collective-permute-start) | collective-permute-done | bytes 3276832 | tf_op jit(solution)/shard_map/ppermute | solution.py:25
  128.0 1.7 copy-done.6
  129.8 1.8 fusion.4
  131.6 2.6 all-gather.2.cloned.1.call-done
  134.2 4.5 %fusion.10 = f32[640,384]{1,0:T(8,128)S(1)} fusion(bf16[640,2560]{1,0:T(8,128)(2,1)} %fusion.4, bf16[3,2560,384]{2,1,0:T(8,128)(2,1)} %all-gather.2.cloned.1.call-done), kind=kOutput, calls=%fused_computation.32 | convolution fusion | flops 1258291200 | bytes 6225920 | tf_op jit(solution)/shard_map/dot_general | solution.py:104
  139.4 1.9 fusion.9
  141.4 2.2 multiply_convert_fusion.2
  143.6 2.1 fusion
  145.7 2.1 fusion.1
  147.8 2.1 fusion.2
  149.9 3.3 %pad_maximum_fusion = bf16[3,2560,384]{2,1,0:T(8,128)(2,1)} fusion(bf16[1,2560,384]{2,1,0:T(8,128)(2,1)S(1)} %fusion.2, bf16[1,2560,384]{2,1,0:T(8,128)(2,1)S(1)} %fusion.1, bf16[1,2560,384]{2,1,0:T(8,128)(2,1)S(1)} %fusion), kind=kLoop, calls=%fused_computation.8 | loop fusion | flops 5898240 | bytes 11796480 | tf_op jit(solution)/shard_map/stack | solution.py:42
  154.2 3.6 %fusion.8 = f32[640,2560]{1,0:T(8,128)S(1)} fusion(bf16[640,384]{1,0:T(8,128)(2,1)S(1)} %copy-done.12, bf16[3,2560,384]{2,1,0:T(8,128)(2,1)} %all-gather.2.cloned.1.call-done), kind=kOutput, calls=%fused_computation.30 | convolution fusion | flops 1258291200 | bytes 9011200 | tf_op jit(solution)/shard_map/dot_general | solution.py:13
  157.9 1.9 convolution_add_fusion
  160.8 1.9 fusion.12
  162.7 2.7 copy-done.2
  165.4 1.9 slice.125
  169.4 4.0 %all-to-all-start.2 = ((bf16[8,40,2560]{2,1,0:T(8,128)(2,1)}), bf16[8,40,2560]{2,1,0:T(8,128)(2,1)S(1)}, u32[]{:S(2)}, u32[]{:S(2)}) async-start(bf16[8,40,2560]{2,1,0:T(8,128)(2,1)} %bitcast.28), calls=%async_computation.2 | async-start | bytes 3276800 | tf_op jit(solution)/shard_map/all_to_all | solution.py:130
  173.6 4.5 %fusion.7 = bf16[320,2560]{1,0:T(8,128)(2,1)} fusion(f32[320,2560]{1,0:T(8,128)} %collective-permute-done.2, f32[640,2560]{1,0:T(8,128)} %copy-done.2), kind=kLoop, calls=%fused_computation.23 | loop fusion | flops 1638400 | bytes 8192000 | tf_op jit(solution)/shard_map/convert_element_type | solution.py:60
  178.1 51.4 %all-to-all-done.2 = bf16[8,40,2560]{2,1,0:T(8,128)(2,1)S(1)} async-done(((bf16[8,40,2560]{2,1,0:T(8,128)(2,1)}), bf16[8,40,2560]{2,1,0:T(8,128)(2,1)S(1)}, u32[]{:S(2)}, u32[]{:S(2)}) %all-to-all-start.2) | async-done | bytes 1638432 | tf_op jit(solution)/shard_map/all_to_all | solution.py:130
  229.5 4.2 %all-to-all-start.1 = ((bf16[8,40,2560]{2,1,0:T(8,128)(2,1)}), bf16[8,40,2560]{2,1,0:T(8,128)(2,1)S(1)}, u32[]{:S(2)}, u32[]{:S(2)}) async-start(bf16[8,40,2560]{2,1,0:T(8,128)(2,1)} %bitcast.85), calls=%async_computation.1 | async-start | bytes 3276800 | tf_op jit(solution)/shard_map/all_to_all | solution.py:121
  233.7 2.5 gather_fusion.3
  236.3 23.6 %all-to-all-done.1 = bf16[8,40,2560]{2,1,0:T(8,128)(2,1)S(1)} async-done(((bf16[8,40,2560]{2,1,0:T(8,128)(2,1)}), bf16[8,40,2560]{2,1,0:T(8,128)(2,1)S(1)}, u32[]{:S(2)}, u32[]{:S(2)}) %all-to-all-start.1) | async-done | bytes 1638432 | tf_op jit(solution)/shard_map/all_to_all | solution.py:121
  259.9 2.5 gather_fusion.2
  262.4 2.9 %multiply_convert_fusion = bf16[256,2560]{1,0:T(8,128)(2,1)} fusion(bf16[256,2560]{1,0:T(8,128)(2,1)} %gather_fusion.2, f32[256]{0:T(256)S(1)} %bitcast.95, pred[256]{0:T(512)(128)(4,1)S(1)} %get-tuple-element.7), kind=kLoop, calls=%fused_computation.25 | loop fusion | flops 2621440 | bytes 2622720 | tf_op jit(solution)/shard_map/convert_element_type | solution.py:124
  265.3 2.9 %reduce-scatter.2.cloned.1.call-done = bf16[3,160,384]{2,1,0:T(8,128)(2,1)} async-done(((bf16[3,2560,384]{2,1,0:T(8,128)(2,1)}), bf16[3,160,384]{2,1,0:T(8,128)(2,1)}) %reduce-scatter.2.cloned.1.call-update) | async-done | bytes 368656 | tf_op jit(solution)/shard_map/reduce_scatter | solution.py:43
  268.3 1.6 collective-permute-start.4
  (76 shorter events, 19.7 us)
Async XLA Ops:
  7.2 16.2 %copy-start = (bf16[256,2560]{1,0:T(8,128)(2,1)S(1)}, bf16[256,2560]{1,0:T(8,128)(2,1)}, u32[]{:S(2)}) copy-start(bf16[256,2560]{1,0:T(8,128)(2,1)} %param.11) | copy-start | bytes 3932164
  7.2 127.0 %all-gather.2.cloned.1.call-start = ((), (), s32[]{:S(2)}) async-start(), calls=%async_computation.4 | async-start | bytes 6266880 | tf_op jit(solution)/shard_map/all_gather | solution.py:37
  9.2 10.0 %collective-permute-start.1 = (bf16[3,80,384]{2,1,0:T(8,128)(2,1)S(1)}, bf16[3,80,384]{2,1,0:T(8,128)(2,1)S(1)}, u32[]{:S(2)}, u32[]{:S(2)}) collective-permute-start(bf16[3,80,384]{2,1,0:T(8,128)(2,1)S(1)} %pad_maximum_fusion.3), channel_id=1, source_target_pairs={{0,8},{8,0},{1,9},{9,1},{2,10},{10,2},{3,11},{11,3},{4,12},{12,4},... | collective-permute-start | bytes 552968 | tf_op jit(solution)/shard_map/ppermute | solution.py:25
  20.1 248.2 %reduce-scatter.2.cloned.1.call-start = ((), (), s32[]{:S(2)}) async-start(), calls=%async_computation.5 | async-start | bytes 6266880 | tf_op jit(solution)/shard_map/reduce_scatter | solution.py:43
  23.4 5.3 %copy-start.3 = (bf16[320,2560]{1,0:T(8,128)(2,1)S(1)}, bf16[320,2560]{1,0:T(8,128)(2,1)}, u32[]{:S(2)}) copy-start(bf16[320,2560]{1,0:T(8,128)(2,1)} %gather_fusion.1) | copy-start | bytes 4915204
  121.4 6.7 %collective-permute-start = (bf16[2,320,2560]{2,1,0:T(8,128)(2,1)S(1)}, bf16[2,320,2560]{2,1,0:T(8,128)(2,1)S(1)}, u32[]{:S(2)}, u32[]{:S(2)}) collective-permute-start(bf16[2,320,2560]{2,1,0:T(8,128)(2,1)S(1)} %bitcast.79), channel_id=1, source_target_pairs={{0,8},{8,0},{1,9},{9,1},{2,10},{10,2},{3,11},{11,3},{4,12},{12,4},... | collective-permute-start | bytes 9830408 | tf_op jit(solution)/shard_map/ppermute | solution.py:25
  128.0 1.7 copy-start.6
  134.2 4.5 %copy-start.4 = (bf16[3,2560,384]{2,1,0:T(8,128)(2,1)S(1)}, bf16[3,2560,384]{2,1,0:T(8,128)(2,1)}, u32[]{:S(2)}) copy-start(bf16[3,2560,384]{2,1,0:T(8,128)(2,1)} %all-gather.2.cloned.1.call-done) | copy-start | bytes 17694724
  134.2 5.2 %copy-start.8 = (bf16[640,2560]{1,0:T(8,128)(2,1)S(1)}, bf16[640,2560]{1,0:T(8,128)(2,1)}, u32[]{:S(2)}) copy-start(bf16[640,2560]{1,0:T(8,128)(2,1)} %fusion.4) | copy-start | bytes 9830404
  139.4 1.9 copy-start.7
  143.5 2.1 copy-start.11
  143.5 2.1 copy-start.13
  143.6 4.2 %copy-start.9 = (bf16[640,384]{1,0:T(8,128)(2,1)}, bf16[640,384]{1,0:T(8,128)(2,1)S(1)}, u32[]{:S(2)}) copy-start(bf16[640,384]{1,0:T(8,128)(2,1)S(1)} %get-tuple-element.11) | copy-start | bytes 1474564
  153.2 1.0 copy-start.12
  153.2 4.6 %slice-start = ((s8[5898240]{0:T(1024)(128)(4,1)}), s8[1703936]{0:T(1024)(128)(4,1)S(1)}, s32[]{:S(2)}) async-start(s8[5898240]{0:T(1024)(128)(4,1)} %bitcast.86), calls=%async_computation.6 | async-start | bytes 3407872
  154.2 3.6 %slice-start.1 = ((s8[5898240]{0:T(1024)(128)(4,1)}), s8[4194304]{0:T(1024)(128)(4,1)S(1)}, s32[]{:S(2)}) async-start(s8[5898240]{0:T(1024)(128)(4,1)} %bitcast.86), calls=%async_computation.7 | async-start | bytes 8388608
  154.2 3.6 %copy-start.14 = (bf16[640,384]{1,0:T(8,128)(2,1)S(1)}, bf16[640,384]{1,0:T(8,128)(2,1)}, u32[]{:S(2)}) copy-start(bf16[640,384]{1,0:T(8,128)(2,1)} %copy-done.13) | copy-start | bytes 1474564
  159.8 1.0 copy-start.10
  160.0 7.8 %collective-permute-start.3 = (f32[320,2560]{1,0:T(8,128)S(1)}, f32[320,2560]{1,0:T(8,128)S(1)}, u32[]{:S(2)}, u32[]{:S(2)}) collective-permute-start(f32[320,2560]{1,0:T(8,128)S(1)} %slice.127), channel_id=1, source_target_pairs={{0,8},{8,0},{1,9},{9,1},{2,10},{10,2},{3,11},{11,3},{4,12},{12,4},... | collective-permute-start | bytes 9830408 | tf_op jit(solution)/shard_map/ppermute | solution.py:25
  162.7 2.7 copy-start.2
  167.3 6.3 %collective-permute-start.2 = (f32[320,2560]{1,0:T(8,128)}, f32[320,2560]{1,0:T(8,128)}, u32[]{:S(2)}, u32[]{:S(2)}) collective-permute-start(f32[320,2560]{1,0:T(8,128)} %slice.125), channel_id=1, source_target_pairs={{0,8},{8,0},{1,9},{9,1},{2,10},{10,2},{3,11},{11,3},{4,12},{12,4},... | collective-permute-start | bytes 9830408 | tf_op jit(solution)/shard_map/ppermute | solution.py:25
  169.4 60.1 %all-to-all-start.2 = ((bf16[8,40,2560]{2,1,0:T(8,128)(2,1)}), bf16[8,40,2560]{2,1,0:T(8,128)(2,1)S(1)}, u32[]{:S(2)}, u32[]{:S(2)}) async-start(bf16[8,40,2560]{2,1,0:T(8,128)(2,1)} %bitcast.28), calls=%async_computation.2 | async-start | bytes 3276800 | tf_op jit(solution)/shard_map/all_to_all | solution.py:130
  178.1 55.6 %copy-start.15 = (s32[256,1]{0,1:T(1,128)S(1)}, s32[256,1]{0,1:T(1,128)}, u32[]{:S(2)}) copy-start(s32[256,1]{0,1:T(1,128)} %param.12) | copy-start | bytes 3076
  229.5 30.4 %all-to-all-start.1 = ((bf16[8,40,2560]{2,1,0:T(8,128)(2,1)}), bf16[8,40,2560]{2,1,0:T(8,128)(2,1)S(1)}, u32[]{:S(2)}, u32[]{:S(2)}) async-start(bf16[8,40,2560]{2,1,0:T(8,128)(2,1)} %bitcast.85), calls=%async_computation.1 | async-start | bytes 3276800 | tf_op jit(solution)/shard_map/all_to_all | solution.py:121
  262.4 7.5 %copy-start.5 = (bf16[256,2560]{1,0:T(8,128)(2,1)S(1)}, bf16[256,2560]{1,0:T(8,128)(2,1)}, u32[]{:S(2)}) copy-start(bf16[256,2560]{1,0:T(8,128)(2,1)} %gather_fusion.3) | copy-start | bytes 3932164
  262.4 10.8 %copy-start.1 = (bf16[256,2560]{1,0:T(8,128)(2,1)S(1)}, bf16[256,2560]{1,0:T(8,128)(2,1)}, u32[]{:S(2)}) copy-start(bf16[256,2560]{1,0:T(8,128)(2,1)} %param.11) | copy-start | bytes 3932164
  268.3 3.9 %collective-permute-start.4 = (bf16[3,160,384]{2,1,0:T(8,128)(2,1)}, bf16[3,160,384]{2,1,0:T(8,128)(2,1)S(1)}, u32[]{:S(2)}, u32[]{:S(2)}) collective-permute-start(bf16[3,160,384]{2,1,0:T(8,128)(2,1)} %reduce-scatter.2.cloned.1.call-done), channel_id=1, source_target_pairs={{0,8},{8,0},{1,9},{9,1},{2,10},{10,2},{3,11},{11,3},{4,12},{12,4},... | collective-permute-start | bytes 1105928 | tf_op jit(solution)/shard_map/ppermute | solution.py:25
Sparse Core Ops, SparseCore 0:
  20.2 113.9 all-gather.1
  153.3 114.8 reduce-scatter.1

commit v10 on v9

--- a/solution.py
+++ b/solution.py
@@ -39,7 +39,7 @@
 
 
 def scatter_grads(*parts):
-    stacked = jnp.stack(parts).astype(jnp.bfloat16)
+    stacked = jnp.stack([part.astype(jnp.bfloat16) for part in parts])
     chip_sum = lax.psum_scatter(stacked, CHIPS, scatter_dimension=1, tiled=True)
     first = lax.axis_index("core") == 0
     rows = chip_sum.shape[1] // 2
@@ -115,26 +115,21 @@
         contract_first(received, up_delta),
         contract_first(grad_rows, hidden),
     )
-    expert_out = pair_total(contract_last(hidden, down_own), slot_count).reshape(
-        experts, capacity, model_width
-    )
-    returned = lax.all_to_all(
-        expert_out, "expert", split_axis=0, concat_axis=0, tiled=True
-    ).reshape(slot_count, model_width)
-    moe_out = (gate_weight * jnp.take(returned, slot_index, axis=0).astype(jnp.float32)).astype(
-        jnp.bfloat16
-    )
+    expert_out = pair_total(contract_last(hidden, down_own), slot_count)
     token_grad = pair_total(
         contract_last(gate_delta, gate_own) + contract_last(up_delta, up_own), slot_count
     )
-    arrived = lax.all_to_all(
-        token_grad.reshape(experts, capacity, model_width),
+    back = lax.all_to_all(
+        jnp.stack([expert_out, token_grad]).reshape(2, experts, capacity, model_width),
         "expert",
-        split_axis=0,
-        concat_axis=0,
+        split_axis=1,
+        concat_axis=1,
         tiled=True,
+    ).reshape(2, slot_count, model_width)
+    moe_out = (gate_weight * jnp.take(back[0], slot_index, axis=0).astype(jnp.float32)).astype(
+        jnp.bfloat16
     )
-    grad_tokens = jnp.take(arrived.reshape(slot_count, model_width), slot_index, axis=0)
+    grad_tokens = jnp.take(back[1], slot_index, axis=0)
     return (moe_out, grad_tokens, grad_gate[None], grad_up[None], grad_down[None])
 
 

time: 281 us -> 296 us (1.053)
  waiting for transfers between devices: 86.3 us -> 99.4 us
  local copies, waits for them, and re-layouts: 24.9 us -> 31.3 us
  starting transfers between devices: 15.4 us -> 11.7 us
    all_to_all x2 -> x1, waiting for transfers between devices: 75 us -> 82.3 us  [shards(): lax.all_to_all(jnp.stack([expert_out, token_grad]).reshape(2, experts, ca...]
    reduce_scatter x1, waiting for transfers between devices: 2.93 us -> 8.87 us  [scatter_grads(): chip_sum = lax.psum_scatter(stacked, CHIPS, scatter_dimension=1, tiled=True)]
    all_to_all x2 -> x1, starting transfers between devices: 8.21 us -> 4.63 us  [shards(): lax.all_to_all(jnp.stack([expert_out, token_grad]).reshape(2, experts, ca...]
    unnamed x36 -> x26, local copies, waits for them, and re-layouts: 6.51 us -> 8.91 us
    another operation x3 -> x4, other arithmetic: 3.91 us -> 5.92 us  [the longest x1 3.32 us: scatter_grads(): stacked = jnp.stack([part.astype(jnp.bfloat16) for part in parts])]
  transfers between devices with their start and end apart: 9 -> 8, of which waited for: 6 -> 4; matrix products, arithmetic and copies ran while one was open for 16% -> 18% of each run, Pallas kernels for 0% -> 0%
where the time goes in v10:
time: 296 us; the launch traced here: 295 us
  waiting for transfers between devices  99.4 us (34%)
  blocking collectives  90.2 us (30%)
  local copies, waits for them, and re-layouts  31.3 us (11%)
  other arithmetic  28.3 us (10%)
  matrix products  20.1 us (7%)
  between operations  14.3 us (5%)
  starting transfers between devices  11.7 us (4%)
    all_to_all x1, blocking collectives, shards(): lax.all_to_all(jnp.stack([pack_rows(tokens), pack_rows(out_grad)]), 'expe...  90.2 us
    all_to_all x1, waiting for transfers between devices, shards(): lax.all_to_all(jnp.stack([expert_out, token_grad]).reshape(2, experts, ca...  82.3 us
    unnamed x26, local copies, waits for them, and re-layouts  8.91 us
    reduce_scatter x1, waiting for transfers between devices, scatter_grads(): chip_sum = lax.psum_scatter(stacked, CHIPS, scatter_dimension=1, tiled=True)  8.87 us
    ppermute x5, starting transfers between devices, swap_cores(): return lax.ppermute(value, 'core', perm=[(0, 1), (1, 0)])  6.96 us
    dot_general x3, matrix products, contract_first(): lax.dot_general(matrix_a, matrix_b, (((0,), (0,)), ((), ())), preferred_e...  6.38 us
    gather x2, local copies, waits for them, and re-layouts, pack_rows(): jnp.take(values, source_row, axis=0) * filled  6.33 us
  transfers between devices with their start and end apart: 8, of which 4 were waited for; matrix products, arithmetic and copies ran while one was open for 18% of the time, Pallas kernels for 0%

profile of v10, /device:TPU:1, one launch (start us, length us, event | category | flops | bytes accessed | tf_op | source)
XLA Modules:
  0.0 295.4 jit_solution(2490178560465489114)
XLA Ops:
  9.2 3.3 %collective-permute-start.1 = (bf16[3,80,384]{2,1,0:T(8,128)(2,1)S(1)}, bf16[3,80,384]{2,1,0:T(8,128)(2,1)S(1)}, u32[]{:S(2)}, u32[]{:S(2)}) collective-permute-start(bf16[3,80,384]{2,1,0:T(8,128)(2,1)S(1)} %pad_maximum_fusion.4), channel_id=1, source_target_pairs={{0,8},{8,0},{1,9},{9,1},{2,10},{10,2},{3,11},{11,3},{4,12},{12,4},... | collective-permute-start | bytes 552968 | tf_op jit(solution)/shard_map/ppermute | solution.py:25
  20.2 3.2 %gather_fusion.1 = bf16[320,2560]{1,0:T(8,128)(2,1)} fusion(bf16[256,2560]{1,0:T(8,128)(2,1)S(1)} %multiply_convert_fusion.1, s32[1024]{0:T(1024)S(1)} %pad_clamp_fusion.1), kind=kCustom, calls=%fused_computation.2.clone | custom fusion | bytes 3278080 | tf_op jit(solution)/shard_map/jit(_take)/gather | solution.py:87
  23.4 3.1 %gather_fusion = bf16[320,2560]{1,0:T(8,128)(2,1)} fusion(bf16[256,2560]{1,0:T(8,128)(2,1)S(1)} %copy-done, s32[1024]{0:T(1024)S(1)} %pad_clamp_fusion.1), kind=kCustom, calls=%fused_computation.clone | custom fusion | bytes 3278080 | tf_op jit(solution)/shard_map/jit(_take)/gather | solution.py:87
  26.5 2.2 scatter_custom_fusion.1
  30.9 90.2 %all_to_all.10 = bf16[2,8,40,2560]{3,2,0,1:T(8,128)(2,1)S(1)} all-to-all(bf16[2,8,40,2560]{3,2,0,1:T(8,128)(2,1)S(1)} %pad_maximum_fusion.2), channel_id=1, replica_groups=mesh['x'=4,'zh'=4,'core'=2,'expert'=8] {'expert'}, dimensions={1} | all-to-all | bytes 6553600 | tf_op jit(solution)/shard_map/all_to_all | solution.py:93
  122.5 5.5 %collective-permute-done = bf16[2,320,2560]{2,1,0:T(8,128)(2,1)S(1)} collective-permute-done((bf16[2,320,2560]{2,1,0:T(8,128)(2,1)S(1)}, bf16[2,320,2560]{2,1,0:T(8,128)(2,1)S(1)}, u32[]{:S(2)}, u32[]{:S(2)}) %collective-permute-start) | collective-permute-done | bytes 3276832 | tf_op jit(solution)/shard_map/ppermute | solution.py:25
  129.7 1.9 fusion.4
  131.5 2.7 all-gather.2.cloned.1.call-done
  134.2 4.0 %fusion.11 = f32[640,384]{1,0:T(8,128)S(1)} fusion(bf16[3,2560,384]{2,1,0:T(8,128)(2,1)} %all-gather.2.cloned.1.call-done, bf16[2,320,2560]{2,1,0:T(8,128)(2,1)} %copy-done.7, bf16[2,320,2560]{2,1,0:T(8,128)(2,1)S(1)} %bitcast.85), kind=kOutput, calls=%fused_computation.34 | convolution fusion | flops 1264844800 | bytes 9502720 | tf_op jit(solution)/shard_map/dot_general | solution.py:108
  140.8 2.2 multiply_convert_fusion.4
  143.0 2.1 fusion
  145.1 1.9 fusion.12
  147.0 2.7 copy-done.2
  149.8 1.9 slice.135
  152.2 1.9 fusion.8
  154.1 1.9 convolution_add_fusion
  156.0 1.9 slice.137
  157.9 2.5 copy-done.3
  160.4 2.1 fusion.2
  162.5 2.1 fusion.1
  164.6 3.3 %pad_maximum_fusion = bf16[3,2560,384]{2,1,0:T(8,128)(2,1)} fusion(bf16[1,2560,384]{2,1,0:T(8,128)(2,1)S(1)} %fusion.2, bf16[1,2560,384]{2,1,0:T(8,128)(2,1)S(1)} %fusion.1, bf16[1,2560,384]{2,1,0:T(8,128)(2,1)S(1)} %fusion), kind=kLoop, calls=%fused_computation.8 | loop fusion | flops 5898240 | bytes 11796480 | tf_op jit(solution)/shard_map/stack | solution.py:42
  168.0 3.5 %fusion.7 = bf16[320,2560]{1,0:T(8,128)(2,1)S(1)} fusion(f32[320,2560]{1,0:T(8,128)} %collective-permute-done.2, f32[640,2560]{1,0:T(8,128)} %copy-done.2), kind=kLoop, calls=%fused_computation.23 | loop fusion | flops 1638400 | bytes 8192000 | tf_op jit(solution)/shard_map/convert_element_type | solution.py:60
  172.8 2.3 fusion.5
  175.1 2.0 pad_maximum_fusion.3
  177.1 4.6 %all-to-all-start.1 = ((bf16[2,8,40,2560]{3,2,0,1:T(8,128)(2,1)}), bf16[2,8,40,2560]{3,2,0,1:T(8,128)(2,1)}, u32[]{:S(2)}, u32[]{:S(2)}) async-start(bf16[2,8,40,2560]{3,2,0,1:T(8,128)(2,1)} %pad_maximum_fusion.3), calls=%async_computation.1 | async-start | bytes 6553600 | tf_op jit(solution)/shard_map/all_to_all | solution.py:122
  181.8 82.3 %all-to-all-done.1 = bf16[2,8,40,2560]{3,2,0,1:T(8,128)(2,1)} async-done(((bf16[2,8,40,2560]{3,2,0,1:T(8,128)(2,1)}), bf16[2,8,40,2560]{3,2,0,1:T(8,128)(2,1)}, u32[]{:S(2)}, u32[]{:S(2)}) %all-to-all-start.1) | async-done | bytes 3276832 | tf_op jit(solution)/shard_map/all_to_all | solution.py:122
  264.1 2.4 fusion.27
  266.6 2.5 gather_fusion.3
  269.1 2.5 gather_fusion.2
  271.6 2.9 multiply_convert_fusion
  274.5 8.9 %reduce-scatter.2.cloned.1.call-done = bf16[3,160,384]{2,1,0:T(8,128)(2,1)} async-done(((bf16[3,2560,384]{2,1,0:T(8,128)(2,1)}), bf16[3,160,384]{2,1,0:T(8,128)(2,1)}) %reduce-scatter.2.cloned.1.call-update) | async-done | bytes 368656 | tf_op jit(solution)/shard_map/reduce_scatter | solution.py:43
  283.3 1.9 collective-permute-start.4
  (66 shorter events, 22.5 us)
Async XLA Ops:
  7.2 16.2 %copy-start = (bf16[256,2560]{1,0:T(8,128)(2,1)S(1)}, bf16[256,2560]{1,0:T(8,128)(2,1)}, u32[]{:S(2)}) copy-start(bf16[256,2560]{1,0:T(8,128)(2,1)} %param.11) | copy-start | bytes 3932164
  7.2 127.0 %all-gather.2.cloned.1.call-start = ((), (), s32[]{:S(2)}) async-start(), calls=%async_computation.3 | async-start | bytes 6266880 | tf_op jit(solution)/shard_map/all_gather | solution.py:37
  9.2 10.0 %collective-permute-start.1 = (bf16[3,80,384]{2,1,0:T(8,128)(2,1)S(1)}, bf16[3,80,384]{2,1,0:T(8,128)(2,1)S(1)}, u32[]{:S(2)}, u32[]{:S(2)}) collective-permute-start(bf16[3,80,384]{2,1,0:T(8,128)(2,1)S(1)} %pad_maximum_fusion.4), channel_id=1, source_target_pairs={{0,8},{8,0},{1,9},{9,1},{2,10},{10,2},{3,11},{11,3},{4,12},{12,4},... | collective-permute-start | bytes 552968 | tf_op jit(solution)/shard_map/ppermute | solution.py:25
  20.1 263.2 %reduce-scatter.2.cloned.1.call-start = ((), (), s32[]{:S(2)}) async-start(), calls=%async_computation.4 | async-start | bytes 6266880 | tf_op jit(solution)/shard_map/reduce_scatter | solution.py:43
  23.4 5.3 %copy-start.4 = (bf16[320,2560]{1,0:T(8,128)(2,1)S(1)}, bf16[320,2560]{1,0:T(8,128)(2,1)}, u32[]{:S(2)}) copy-start(bf16[320,2560]{1,0:T(8,128)(2,1)} %gather_fusion.1) | copy-start | bytes 4915204
  121.3 6.7 %collective-permute-start = (bf16[2,320,2560]{2,1,0:T(8,128)(2,1)S(1)}, bf16[2,320,2560]{2,1,0:T(8,128)(2,1)S(1)}, u32[]{:S(2)}, u32[]{:S(2)}) collective-permute-start(bf16[2,320,2560]{2,1,0:T(8,128)(2,1)S(1)} %bitcast.83), channel_id=1, source_target_pairs={{0,8},{8,0},{1,9},{9,1},{2,10},{10,2},{3,11},{11,3},{4,12},{12,4},... | collective-permute-start | bytes 9830408 | tf_op jit(solution)/shard_map/ppermute | solution.py:25
  128.0 1.7 copy-start.7
  134.2 4.0 %copy-start.5 = (bf16[3,2560,384]{2,1,0:T(8,128)(2,1)S(1)}, bf16[3,2560,384]{2,1,0:T(8,128)(2,1)}, u32[]{:S(2)}) copy-start(bf16[3,2560,384]{2,1,0:T(8,128)(2,1)} %all-gather.2.cloned.1.call-done) | copy-start | bytes 17694724
  134.2 4.7 %copy-start.9 = (bf16[640,2560]{1,0:T(8,128)(2,1)S(1)}, bf16[640,2560]{1,0:T(8,128)(2,1)}, u32[]{:S(2)}) copy-start(bf16[640,2560]{1,0:T(8,128)(2,1)} %fusion.4) | copy-start | bytes 9830404
  147.0 2.8 copy-start.2
  151.7 16.3 %collective-permute-start.2 = (f32[320,2560]{1,0:T(8,128)}, f32[320,2560]{1,0:T(8,128)}, u32[]{:S(2)}, u32[]{:S(2)}) collective-permute-start(f32[320,2560]{1,0:T(8,128)} %slice.135), channel_id=1, source_target_pairs={{0,8},{8,0},{1,9},{9,1},{2,10},{10,2},{3,11},{11,3},{4,12},{12,4},... | collective-permute-start | bytes 9830408 | tf_op jit(solution)/shard_map/ppermute | solution.py:25
  156.0 4.4 %copy-start.3 = (f32[640,2560]{1,0:T(8,128)}, f32[640,2560]{1,0:T(8,128)S(1)}, u32[]{:S(2)}) copy-start(f32[640,2560]{1,0:T(8,128)S(1)} %convolution_add_fusion) | copy-start | bytes 19660804
  156.0 4.4 %copy-start.8 = (bf16[2,320,2560]{2,1,0:T(8,128)(2,1)S(1)}, bf16[2,320,2560]{2,1,0:T(8,128)(2,1)}, u32[]{:S(2)}) copy-start(bf16[2,320,2560]{2,1,0:T(8,128)(2,1)} %copy-done.7) | copy-start | bytes 9830404
  160.3 11.1 %collective-permute-start.3 = (f32[320,2560]{1,0:T(8,128)}, f32[320,2560]{1,0:T(8,128)}, u32[]{:S(2)}, u32[]{:S(2)}) collective-permute-start(f32[320,2560]{1,0:T(8,128)} %slice.137), channel_id=1, source_target_pairs={{0,8},{8,0},{1,9},{9,1},{2,10},{10,2},{3,11},{11,3},{4,12},{12,4},... | collective-permute-start | bytes 9830408 | tf_op jit(solution)/shard_map/ppermute | solution.py:25
  168.0 3.6 %slice-start = ((s8[6553600]{0:T(1024)(128)(4,1)}), s8[2359296]{0:T(1024)(128)(4,1)S(1)}, s32[]{:S(2)}) async-start(s8[6553600]{0:T(1024)(128)(4,1)} %bitcast.81), calls=%async_computation.5 | async-start | bytes 4718592
  168.0 4.8 %slice-start.1 = ((s8[6553600]{0:T(1024)(128)(4,1)}), s8[4194304]{0:T(1024)(128)(4,1)S(1)}, s32[]{:S(2)}) async-start(s8[6553600]{0:T(1024)(128)(4,1)} %bitcast.81), calls=%async_computation.6 | async-start | bytes 8388608
  177.1 4.6 %copy-start.10 = (s32[256,1]{0,1:T(1,128)S(1)}, s32[256,1]{0,1:T(1,128)}, u32[]{:S(2)}) copy-start(s32[256,1]{0,1:T(1,128)} %param.12) | copy-start | bytes 3076
  177.1 87.0 %all-to-all-start.1 = ((bf16[2,8,40,2560]{3,2,0,1:T(8,128)(2,1)}), bf16[2,8,40,2560]{3,2,0,1:T(8,128)(2,1)}, u32[]{:S(2)}, u32[]{:S(2)}) async-start(bf16[2,8,40,2560]{3,2,0,1:T(8,128)(2,1)} %pad_maximum_fusion.3), calls=%async_computation.1 | async-start | bytes 6553600 | tf_op jit(solution)/shard_map/all_to_all | solution.py:122
  271.6 13.7 %copy-start.6 = (bf16[256,2560]{1,0:T(8,128)(2,1)S(1)}, bf16[256,2560]{1,0:T(8,128)(2,1)}, u32[]{:S(2)}) copy-start(bf16[256,2560]{1,0:T(8,128)(2,1)} %gather_fusion.3) | copy-start | bytes 3932164
  271.6 17.0 %copy-start.1 = (bf16[256,2560]{1,0:T(8,128)(2,1)S(1)}, bf16[256,2560]{1,0:T(8,128)(2,1)}, u32[]{:S(2)}) copy-start(bf16[256,2560]{1,0:T(8,128)(2,1)} %param.11) | copy-start | bytes 3932164
  283.3 4.2 %collective-permute-start.4 = (bf16[3,160,384]{2,1,0:T(8,128)(2,1)}, bf16[3,160,384]{2,1,0:T(8,128)(2,1)S(1)}, u32[]{:S(2)}, u32[]{:S(2)}) collective-permute-start(bf16[3,160,384]{2,1,0:T(8,128)(2,1)} %reduce-scatter.2.cloned.1.call-done), channel_id=1, source_target_pairs={{0,8},{8,0},{1,9},{9,1},{2,10},{10,2},{3,11},{11,3},{4,12},{12,4},... | collective-permute-start | bytes 1105928 | tf_op jit(solution)/shard_map/ppermute | solution.py:25
Sparse Core Ops, SparseCore 0:
  20.2 113.9 all-gather.1
  168.1 115.1 reduce-scatter.1

commit v11 on v9

--- a/solution.py
+++ b/solution.py
@@ -38,21 +38,23 @@
     return [own[i] for i in range(len(weights))]
 
 
-def scatter_grads(*parts):
-    stacked = jnp.stack(parts).astype(jnp.bfloat16)
-    chip_sum = lax.psum_scatter(stacked, CHIPS, scatter_dimension=1, tiled=True)
+def scatter_grads(parts, count):
+    chip_sum = lax.psum_scatter(parts.astype(jnp.bfloat16), CHIPS, scatter_dimension=0, tiled=True)
     first = lax.axis_index("core") == 0
-    rows = chip_sum.shape[1] // 2
+    rows = chip_sum.shape[0] // 2
 
     def my_rows(value):
-        return jnp.where(first, value[:, :rows], value[:, rows:]).astype(jnp.float32)
+        return jnp.where(first, value[:rows], value[rows:]).astype(jnp.float32)
 
     mine = my_rows(chip_sum)
     theirs = my_rows(swap_cores(chip_sum))
-    block = jnp.where(
-        first, jnp.concatenate([mine, theirs], axis=2), jnp.concatenate([theirs, mine], axis=2)
-    )
-    return [block[i] for i in range(len(parts))]
+    half = parts.shape[1] // count
+    blocks = []
+    for i in range(count):
+        a = mine[:, i * half:(i + 1) * half]
+        b = theirs[:, i * half:(i + 1) * half]
+        blocks.append(jnp.where(first, jnp.concatenate([a, b], axis=1), jnp.concatenate([b, a], axis=1)))
+    return blocks
 
 
 def pair_total(partial, slots):
@@ -110,11 +112,16 @@
         hidden_grad * act_up * sigmoid_gate * (1.0 + act_gate * (1.0 - sigmoid_gate))
     ).astype(jnp.bfloat16)
     up_delta = (hidden_grad * silu_gate).astype(jnp.bfloat16)
-    grad_gate, grad_up, grad_down = scatter_grads(
-        contract_first(received, gate_delta),
-        contract_first(received, up_delta),
-        contract_first(grad_rows, hidden),
+    empty = jnp.zeros_like(hidden)
+    rights = jnp.concatenate(
+        [
+            jnp.concatenate([gate_delta, up_delta, empty], axis=1),
+            jnp.concatenate([empty, empty, hidden], axis=1),
+        ],
+        axis=0,
     )
+    lefts = pair_rows.reshape(-1, model_width)
+    grad_gate, grad_up, grad_down = scatter_grads(contract_first(lefts, rights), 3)
     expert_out = pair_total(contract_last(hidden, down_own), slot_count).reshape(
         experts, capacity, model_width
     )

time: 281 us -> 290 us (1.032)
  blocking collectives: 90.2 us -> 72.3 us
  waiting for transfers between devices: 86.3 us -> 103 us
  matrix products: 22.2 us -> 28.9 us
  starting transfers between devices: 15.4 us -> 20.2 us
    all_to_all x1, blocking collectives: 90.2 us -> 72.3 us  [shards(): lax.all_to_all(jnp.stack([pack_rows(tokens), pack_rows(out_grad)]), 'expe...]
    all_gather x1, waiting for transfers between devices: 2.63 us -> 18.5 us  [gather_weights(): own = lax.all_gather(own, CHIPS, axis=1, tiled=True)]
    ppermute x5, starting transfers between devices: 7.16 us -> 11.7 us  [swap_cores(): return lax.ppermute(value, 'core', perm=[(0, 1), (1, 0)])]
    dot_general x3 -> x1, matrix products: 6.27 us -> 10.7 us  [contract_first(): lax.dot_general(matrix_a, matrix_b, (((0,), (0,)), ((), ())), preferred_e...]
    another operation x3 -> x2, other arithmetic: 3.91 us -> 0.61 us  [the longest x1 3.31 us: scatter_grads(): stacked = jnp.stack(parts).astype(jnp.bfloat16)]
    all_to_all x1, waiting for transfers between devices: 23.6 us -> 26.8 us  [shards(): lax.all_to_all(expert_out, 'expert', split_axis=0, concat_axis=0, tiled=T...]
    concatenate x0 -> x1, other arithmetic: none -> 3.16 us  [shards(): pair_rows = jnp.concatenate([both_rows, swap_cores(both_rows)], axis=1)]
    reduce_scatter x1, waiting for transfers between devices: 2.93 us -> 0.01 us  [scatter_grads(): lax.psum_scatter(parts.astype(jnp.bfloat16), CHIPS, scatter_dimension=0,...]
  transfers between devices with their start and end apart: 9 -> 9, of which waited for: 6 -> 5; matrix products, arithmetic and copies ran while one was open for 16% -> 18% of each run, Pallas kernels for 0% -> 0%
where the time goes in v11:
time: 290 us
  waiting for transfers between devices  103 us (36%)
  blocking collectives  72.3 us (25%)
  matrix products  28.9 us (10%)
  other arithmetic  26.8 us (9%)
  local copies, waits for them, and re-layouts  24.1 us (8%)
  starting transfers between devices  20.2 us (7%)
  between operations  14.3 us (5%)
    all_to_all x1, blocking collectives, shards(): lax.all_to_all(jnp.stack([pack_rows(tokens), pack_rows(out_grad)]), 'expe...  72.3 us
    all_to_all x1, waiting for transfers between devices, shards(): lax.all_to_all(token_grad.reshape(experts, capacity, model_width), 'exper...  51.6 us
    all_to_all x1, waiting for transfers between devices, shards(): lax.all_to_all(expert_out, 'expert', split_axis=0, concat_axis=0, tiled=T...  26.8 us
    all_gather x1, waiting for transfers between devices, gather_weights(): own = lax.all_gather(own, CHIPS, axis=1, tiled=True)  18.5 us
    ppermute x5, starting transfers between devices, swap_cores(): return lax.ppermute(value, 'core', perm=[(0, 1), (1, 0)])  11.7 us
    dot_general x1, matrix products, contract_first(): lax.dot_general(matrix_a, matrix_b, (((0,), (0,)), ((), ())), preferred_e...  10.7 us
    dot_general x3, matrix products, contract_last(): lax.dot_general(matrix_a, matrix_b, (((1,), (1,)), ((), ())), preferred_e...  10.1 us
    gather x2, local copies, waits for them, and re-layouts, pack_rows(): jnp.take(values, source_row, axis=0) * filled  6.35 us
  transfers between devices with their start and end apart: 9, of which 5 were waited for; matrix products, arithmetic and copies ran while one was open for 18% of the time, Pallas kernels for 0%

profile of v11, /device:TPU:1, one launch (start us, length us, event | category | flops | bytes accessed | tf_op | source)
XLA Modules:
  0.0 289.5 jit_solution(1780936461019658532)
XLA Ops:
  10.0 3.3 %collective-permute-start.1 = (bf16[3,80,384]{2,1,0:T(8,128)(2,1)S(1)}, bf16[3,80,384]{2,1,0:T(8,128)(2,1)S(1)}, u32[]{:S(2)}, u32[]{:S(2)}) collective-permute-start(bf16[3,80,384]{2,1,0:T(8,128)(2,1)S(1)} %pad_maximum_fusion.2), channel_id=1, source_target_pairs={{0,8},{8,0},{1,9},{9,1},{2,10},{10,2},{3,11},{11,3},{4,12},{12,4},... | collective-permute-start | bytes 552968 | tf_op jit(solution)/shard_map/ppermute | solution.py:25
  17.0 1.4 scatter_custom_fusion
  18.4 1.6 multiply_convert_fusion.1
  20.0 3.2 %gather_fusion.1 = bf16[320,2560]{1,0:T(8,128)(2,1)} fusion(bf16[256,2560]{1,0:T(8,128)(2,1)S(1)} %multiply_convert_fusion.1, s32[1024]{0:T(1024)S(1)} %pad_clamp_fusion.1), kind=kCustom, calls=%fused_computation.2.clone | custom fusion | bytes 3278080 | tf_op jit(solution)/shard_map/jit(_take)/gather | solution.py:89
  23.2 3.2 %gather_fusion = bf16[320,2560]{1,0:T(8,128)(2,1)} fusion(bf16[256,2560]{1,0:T(8,128)(2,1)S(1)} %copy-done, s32[1024]{0:T(1024)S(1)} %pad_clamp_fusion.1), kind=kCustom, calls=%fused_computation.clone | custom fusion | bytes 3278080 | tf_op jit(solution)/shard_map/jit(_take)/gather | solution.py:89
  26.4 2.2 scatter_custom_fusion.1
  29.5 1.8 select_multiply_fusion.1
  31.7 72.3 %all_to_all.15 = bf16[2,8,40,2560]{3,2,0,1:T(8,128)(2,1)S(1)} all-to-all(bf16[2,8,40,2560]{3,2,0,1:T(8,128)(2,1)S(1)} %pad_maximum_fusion.1), channel_id=1, replica_groups=mesh['x'=4,'zh'=4,'core'=2,'expert'=8] {'expert'}, dimensions={1} | all-to-all | bytes 6553600 | tf_op jit(solution)/shard_map/all_to_all | solution.py:95
  104.2 3.5 %collective-permute-start = (bf16[2,320,2560]{2,1,0:T(8,128)(2,1)S(1)}, bf16[2,320,2560]{2,1,0:T(8,128)(2,1)S(1)}, u32[]{:S(2)}, u32[]{:S(2)}) collective-permute-start(bf16[2,320,2560]{2,1,0:T(8,128)(2,1)S(1)} %bitcast.81), channel_id=1, source_target_pairs={{0,8},{8,0},{1,9},{9,1},{2,10},{10,2},{3,11},{11,3},{4,12},{12,4},... | collective-permute-start | bytes 9830408 | tf_op jit(solution)/shard_map/ppermute | solution.py:25
  107.7 5.5 %collective-permute-done = bf16[2,320,2560]{2,1,0:T(8,128)(2,1)S(1)} collective-permute-done((bf16[2,320,2560]{2,1,0:T(8,128)(2,1)S(1)}, bf16[2,320,2560]{2,1,0:T(8,128)(2,1)S(1)}, u32[]{:S(2)}, u32[]{:S(2)}) %collective-permute-start) | collective-permute-done | bytes 3276832 | tf_op jit(solution)/shard_map/ppermute | solution.py:25
  113.2 1.8 copy-done.5
  115.0 3.2 %pad_maximum_fusion = bf16[2,640,2560]{2,1,0:T(8,128)(2,1)} fusion(bf16[2,320,2560]{2,1,0:T(8,128)(2,1)S(1)} %collective-permute-done, bf16[2,320,2560]{2,1,0:T(8,128)(2,1)S(1)} %bitcast.82), kind=kLoop, calls=%fused_computation.9 | loop fusion | flops 13107200 | bytes 13107200 | tf_op jit(solution)/shard_map/concatenate | solution.py:102
  118.1 18.5 %all-gather.2.cloned.1.call-done = bf16[3,2560,384]{2,1,0:T(8,128)(2,1)} async-done(((bf16[3,160,384]{2,1,0:T(8,128)(2,1)}), bf16[3,2560,384]{2,1,0:T(8,128)(2,1)}) %all-gather.2.cloned.1.call-update) | async-done | bytes 5898256 | tf_op jit(solution)/shard_map/all_gather | solution.py:37
  136.7 4.0 %fusion.20 = f32[640,384]{1,0:T(8,128)S(1)} fusion(bf16[3,2560,384]{2,1,0:T(8,128)(2,1)} %all-gather.2.cloned.1.call-done, bf16[2,320,2560]{2,1,0:T(8,128)(2,1)S(1)} %bitcast.83, bf16[2,320,2560]{2,1,0:T(8,128)(2,1)} %copy-done.5), kind=kOutput, calls=%fused_computation.40 | convolution fusion | flops 1264844800 | bytes 9502720 | tf_op jit(solution)/shard_map/dot_general | solution.py:106
  141.4 1.8 fusion.19
  143.3 2.2 multiply_convert_fusion.2
  146.6 10.7 %convolution_convert_fusion = bf16[2560,1152]{1,0:T(8,128)(2,1)} fusion(bf16[1280,2560]{1,0:T(8,128)(2,1)S(1)} %bitcast.88, bf16[640,384]{1,0:T(8,128)(2,1)S(1)} %get-tuple-element.11, bf16[640,384]{1,0:T(8,128)(2,1)S(1)} %broadcast_in_dim.40, bf16[640,384]{1,0:T(8,128)(2,1)S(1)} %get-tuple-element.9, bf16[640,384]{1,0:T(8,128)(2,1)S(1)} %get-tuple-element.10), kind=kOutput, calls=%fused_computation.6 | convolution fusion | flops 7567441920 | bytes 14417920 | tf_op jit(solution)/shard_map/dot_general | solution.py:19
  158.3 3.6 %fusion.18 = f32[640,2560]{1,0:T(8,128)S(1)} fusion(bf16[640,384]{1,0:T(8,128)(2,1)S(1)} %copy-done.10, bf16[3,2560,384]{2,1,0:T(8,128)(2,1)} %all-gather.2.cloned.1.call-done), kind=kOutput, calls=%fused_computation.38 | convolution fusion | flops 1258291200 | bytes 9011200 | tf_op jit(solution)/shard_map/dot_general | solution.py:13
  161.9 1.9 convolution_add_fusion
  164.9 4.6 %fusion.21 = f32[640,2560]{1,0:T(8,128)} fusion(bf16[640,384]{1,0:T(8,128)(2,1)S(1)} %copy-done.8, bf16[3,2560,384]{2,1,0:T(8,128)(2,1)S(1)} %bitcast.93), kind=kOutput, calls=%fused_computation.41 | convolution fusion | flops 1258291200 | bytes 9011200 | tf_op jit(solution)/shard_map/dot_general | solution.py:13
  169.5 3.8 %slice.137 = f32[320,2560]{1,0:T(8,128)} slice(f32[640,2560]{1,0:T(8,128)} %fusion.21), slice={[320:640], [0:2560]} | slice | bytes 6553600 | tf_op jit(solution)/shard_map/slice | solution.py:61
  173.8 1.6 fusion.7
  175.4 4.2 %all-to-all-start.2 = ((bf16[8,40,2560]{2,1,0:T(8,128)(2,1)}), bf16[8,40,2560]{2,1,0:T(8,128)(2,1)S(1)}, u32[]{:S(2)}, u32[]{:S(2)}) async-start(bf16[8,40,2560]{2,1,0:T(8,128)(2,1)} %bitcast.28), calls=%async_computation.2 | async-start | bytes 3276800 | tf_op jit(solution)/shard_map/all_to_all | solution.py:137
  179.6 4.5 %fusion.8 = bf16[320,2560]{1,0:T(8,128)(2,1)} fusion(f32[320,2560]{1,0:T(8,128)} %collective-permute-done.2, f32[640,2560]{1,0:T(8,128)} %fusion.21), kind=kLoop, calls=%fused_computation.23 | loop fusion | flops 1638400 | bytes 8192000 | tf_op jit(solution)/shard_map/convert_element_type | solution.py:62
  184.2 51.6 %all-to-all-done.2 = bf16[8,40,2560]{2,1,0:T(8,128)(2,1)S(1)} async-done(((bf16[8,40,2560]{2,1,0:T(8,128)(2,1)}), bf16[8,40,2560]{2,1,0:T(8,128)(2,1)S(1)}, u32[]{:S(2)}, u32[]{:S(2)}) %all-to-all-start.2) | async-done | bytes 1638432 | tf_op jit(solution)/shard_map/all_to_all | solution.py:137
  235.8 4.2 %all-to-all-start.1 = ((bf16[8,40,2560]{2,1,0:T(8,128)(2,1)}), bf16[8,40,2560]{2,1,0:T(8,128)(2,1)S(1)}, u32[]{:S(2)}, u32[]{:S(2)}) async-start(bf16[8,40,2560]{2,1,0:T(8,128)(2,1)} %bitcast.91), calls=%async_computation.1 | async-start | bytes 3276800 | tf_op jit(solution)/shard_map/all_to_all | solution.py:128
  240.0 2.5 gather_fusion.3
  242.5 26.8 %all-to-all-done.1 = bf16[8,40,2560]{2,1,0:T(8,128)(2,1)S(1)} async-done(((bf16[8,40,2560]{2,1,0:T(8,128)(2,1)}), bf16[8,40,2560]{2,1,0:T(8,128)(2,1)S(1)}, u32[]{:S(2)}, u32[]{:S(2)}) %all-to-all-start.1) | async-done | bytes 1638432 | tf_op jit(solution)/shard_map/all_to_all | solution.py:128
  269.3 2.5 gather_fusion.2
  271.8 2.7 broadcast_select_fusion
  274.5 1.4 multiply_convert_fusion
  276.0 3.6 %collective-permute-start.4 = (bf16[160,1152]{1,0:T(8,128)(2,1)}, bf16[160,1152]{1,0:T(8,128)(2,1)S(1)}, u32[]{:S(2)}, u32[]{:S(2)}) collective-permute-start(bf16[160,1152]{1,0:T(8,128)(2,1)} %reduce-scatter.2.cloned.1.call-done), channel_id=1, source_target_pairs={{0,8},{8,0},{1,9},{9,1},{2,10},{10,2},{3,11},{11,3},{4,12},{12,4},... | collective-permute-start | bytes 1105928 | tf_op jit(solution)/shard_map/ppermute | solution.py:25
  (78 shorter events, 15.3 us)
Async XLA Ops:
  7.2 16.0 %copy-start = (bf16[256,2560]{1,0:T(8,128)(2,1)S(1)}, bf16[256,2560]{1,0:T(8,128)(2,1)}, u32[]{:S(2)}) copy-start(bf16[256,2560]{1,0:T(8,128)(2,1)} %param.11) | copy-start | bytes 3932164
  7.2 129.5 %all-gather.2.cloned.1.call-start = ((), (), s32[]{:S(2)}) async-start(), calls=%async_computation.4 | async-start | bytes 6266880 | tf_op jit(solution)/shard_map/all_gather | solution.py:37
  10.0 18.5 %collective-permute-start.1 = (bf16[3,80,384]{2,1,0:T(8,128)(2,1)S(1)}, bf16[3,80,384]{2,1,0:T(8,128)(2,1)S(1)}, u32[]{:S(2)}, u32[]{:S(2)}) collective-permute-start(bf16[3,80,384]{2,1,0:T(8,128)(2,1)S(1)} %pad_maximum_fusion.2), channel_id=1, source_target_pairs={{0,8},{8,0},{1,9},{9,1},{2,10},{10,2},{3,11},{11,3},{4,12},{12,4},... | collective-permute-start | bytes 552968 | tf_op jit(solution)/shard_map/ppermute | solution.py:25
  23.2 6.3 %copy-start.2 = (bf16[320,2560]{1,0:T(8,128)(2,1)S(1)}, bf16[320,2560]{1,0:T(8,128)(2,1)}, u32[]{:S(2)}) copy-start(bf16[320,2560]{1,0:T(8,128)(2,1)} %gather_fusion.1) | copy-start | bytes 4915204
  29.4 246.5 %reduce-scatter.2.cloned.1.call-start = ((), (), s32[]{:S(2)}) async-start(), calls=%async_computation.5 | async-start | bytes 6266880 | tf_op jit(solution)/shard_map/reduce_scatter | solution.py:42
  104.2 9.0 %collective-permute-start = (bf16[2,320,2560]{2,1,0:T(8,128)(2,1)S(1)}, bf16[2,320,2560]{2,1,0:T(8,128)(2,1)S(1)}, u32[]{:S(2)}, u32[]{:S(2)}) collective-permute-start(bf16[2,320,2560]{2,1,0:T(8,128)(2,1)S(1)} %bitcast.81), channel_id=1, source_target_pairs={{0,8},{8,0},{1,9},{9,1},{2,10},{10,2},{3,11},{11,3},{4,12},{12,4},... | collective-permute-start | bytes 9830408 | tf_op jit(solution)/shard_map/ppermute | solution.py:25
  113.2 1.8 copy-start.5
  136.7 4.0 %copy-start.3 = (bf16[3,2560,384]{2,1,0:T(8,128)(2,1)S(1)}, bf16[3,2560,384]{2,1,0:T(8,128)(2,1)}, u32[]{:S(2)}) copy-start(bf16[3,2560,384]{2,1,0:T(8,128)(2,1)} %all-gather.2.cloned.1.call-done) | copy-start | bytes 17694724
  136.7 4.7 %copy-start.6 = (bf16[2,320,2560]{2,1,0:T(8,128)(2,1)S(1)}, bf16[2,320,2560]{2,1,0:T(8,128)(2,1)}, u32[]{:S(2)}) copy-start(bf16[2,320,2560]{2,1,0:T(8,128)(2,1)} %copy-done.5) | copy-start | bytes 9830404
  141.4 5.2 %slice-start = ((s8[6553600]{0:T(1024)(128)(4,1)}), s8[4194304]{0:T(1024)(128)(4,1)S(1)}, s32[]{:S(2)}) async-start(s8[6553600]{0:T(1024)(128)(4,1)} %bitcast.86), calls=%async_computation.6 | async-start | bytes 8388608
  143.3 3.3 %slice-start.1 = ((s8[6553600]{0:T(1024)(128)(4,1)}), s8[2359296]{0:T(1024)(128)(4,1)S(1)}, s32[]{:S(2)}) async-start(s8[6553600]{0:T(1024)(128)(4,1)} %bitcast.86), calls=%async_computation.7 | async-start | bytes 4718592
  145.5 0.8 copy-start.7
  145.5 0.9 copy-start.9
  145.5 1.1 copy-start.11
  157.3 1.0 copy-start.10
  157.3 4.6 %slice-start.2 = ((s8[5898240]{0:T(1024)(128)(4,1)}), s8[1703936]{0:T(1024)(128)(4,1)S(1)}, s32[]{:S(2)}) async-start(s8[5898240]{0:T(1024)(128)(4,1)} %bitcast.92), calls=%async_computation.8 | async-start | bytes 3407872
  158.3 3.6 %slice-start.3 = ((s8[5898240]{0:T(1024)(128)(4,1)}), s8[4194304]{0:T(1024)(128)(4,1)S(1)}, s32[]{:S(2)}) async-start(s8[5898240]{0:T(1024)(128)(4,1)} %bitcast.92), calls=%async_computation.9 | async-start | bytes 8388608
  158.3 3.6 %copy-start.12 = (bf16[640,384]{1,0:T(8,128)(2,1)S(1)}, bf16[640,384]{1,0:T(8,128)(2,1)}, u32[]{:S(2)}) copy-start(bf16[640,384]{1,0:T(8,128)(2,1)} %copy-done.11) | copy-start | bytes 1474564
  163.9 1.0 copy-start.8
  164.1 9.7 %collective-permute-start.3 = (f32[320,2560]{1,0:T(8,128)S(1)}, f32[320,2560]{1,0:T(8,128)S(1)}, u32[]{:S(2)}, u32[]{:S(2)}) collective-permute-start(f32[320,2560]{1,0:T(8,128)S(1)} %slice.141), channel_id=1, source_target_pairs={{0,8},{8,0},{1,9},{9,1},{2,10},{10,2},{3,11},{11,3},{4,12},{12,4},... | collective-permute-start | bytes 9830408 | tf_op jit(solution)/shard_map/ppermute | solution.py:25
  173.4 6.3 %collective-permute-start.2 = (f32[320,2560]{1,0:T(8,128)}, f32[320,2560]{1,0:T(8,128)}, u32[]{:S(2)}, u32[]{:S(2)}) collective-permute-start(f32[320,2560]{1,0:T(8,128)} %slice.137), channel_id=1, source_target_pairs={{0,8},{8,0},{1,9},{9,1},{2,10},{10,2},{3,11},{11,3},{4,12},{12,4},... | collective-permute-start | bytes 9830408 | tf_op jit(solution)/shard_map/ppermute | solution.py:25
  175.4 60.4 %all-to-all-start.2 = ((bf16[8,40,2560]{2,1,0:T(8,128)(2,1)}), bf16[8,40,2560]{2,1,0:T(8,128)(2,1)S(1)}, u32[]{:S(2)}, u32[]{:S(2)}) async-start(bf16[8,40,2560]{2,1,0:T(8,128)(2,1)} %bitcast.28), calls=%async_computation.2 | async-start | bytes 3276800 | tf_op jit(solution)/shard_map/all_to_all | solution.py:137
  184.2 55.8 %copy-start.13 = (s32[256,1]{0,1:T(1,128)S(1)}, s32[256,1]{0,1:T(1,128)}, u32[]{:S(2)}) copy-start(s32[256,1]{0,1:T(1,128)} %param.12) | copy-start | bytes 3076
  235.8 33.5 %all-to-all-start.1 = ((bf16[8,40,2560]{2,1,0:T(8,128)(2,1)}), bf16[8,40,2560]{2,1,0:T(8,128)(2,1)S(1)}, u32[]{:S(2)}, u32[]{:S(2)}) async-start(bf16[8,40,2560]{2,1,0:T(8,128)(2,1)} %bitcast.91), calls=%async_computation.1 | async-start | bytes 3276800 | tf_op jit(solution)/shard_map/all_to_all | solution.py:128
  271.8 2.7 copy-start.4
  271.8 10.9 %copy-start.1 = (bf16[256,2560]{1,0:T(8,128)(2,1)S(1)}, bf16[256,2560]{1,0:T(8,128)(2,1)}, u32[]{:S(2)}) copy-start(bf16[256,2560]{1,0:T(8,128)(2,1)} %param.11) | copy-start | bytes 3932164
  276.0 5.1 %collective-permute-start.4 = (bf16[160,1152]{1,0:T(8,128)(2,1)}, bf16[160,1152]{1,0:T(8,128)(2,1)S(1)}, u32[]{:S(2)}, u32[]{:S(2)}) collective-permute-start(bf16[160,1152]{1,0:T(8,128)(2,1)} %reduce-scatter.2.cloned.1.call-done), channel_id=1, source_target_pairs={{0,8},{8,0},{1,9},{9,1},{2,10},{10,2},{3,11},{11,3},{4,12},{12,4},... | collective-permute-start | bytes 1105928 | tf_op jit(solution)/shard_map/ppermute | solution.py:25
Sparse Core Ops, SparseCore 0:
  29.6 107.0 all-gather.1
  157.4 115.8 reduce-scatter.1

commit v12 on v9

--- a/solution.py
+++ b/solution.py
@@ -26,16 +26,10 @@
 
 
 def gather_weights(*weights):
-    half = weights[0].shape[1] // 2
+    full = lax.all_gather(jnp.stack(weights), DP, axis=1, tiled=True)
+    half = full.shape[2] // 2
     first = lax.axis_index("core") == 0
-    kept = jnp.stack([jnp.where(first, w[:, :half], w[:, half:]) for w in weights])
-    sent = jnp.stack([jnp.where(first, w[:, half:], w[:, :half]) for w in weights])
-    came = swap_cores(sent)
-    own = jnp.where(
-        first, jnp.concatenate([kept, came], axis=1), jnp.concatenate([came, kept], axis=1)
-    )
-    own = lax.all_gather(own, CHIPS, axis=1, tiled=True)
-    return [own[i] for i in range(len(weights))]
+    return [jnp.where(first, full[i, :, :half], full[i, :, half:]) for i in range(len(weights))]
 
 
 def scatter_grads(*parts):

time: 281 us -> 291 us (1.036)
  matrix products: 22.2 us -> 33.8 us
  blocking collectives: 90.2 us -> 93.6 us
    all_to_all x1, waiting for transfers between devices: 23.6 us -> 28.9 us  [shards(): lax.all_to_all(expert_out, 'expert', split_axis=0, concat_axis=0, tiled=T...]
    dot_general x3, matrix products: 7.39 us -> 12.2 us  [contract_last(): lax.dot_general(matrix_a, matrix_b, (((1,), (1,)), ((), ())), preferred_e...]
    all_to_all x1, blocking collectives: 90.2 us -> 93.6 us  [shards(): lax.all_to_all(jnp.stack([pack_rows(tokens), pack_rows(out_grad)]), 'expe...]
    reduce_scatter x1, waiting for transfers between devices: 2.93 us -> 0.01 us  [scatter_grads(): chip_sum = lax.psum_scatter(stacked, CHIPS, scatter_dimension=1, tiled=True)]
    ppermute x5 -> x4, starting transfers between devices: 7.16 us -> 4.26 us  [swap_cores(): return lax.ppermute(value, 'core', perm=[(0, 1), (1, 0)])]
    unnamed x36 -> x26, local copies, waits for them, and re-layouts: 6.51 us -> 4.2 us
    ppermute x5 -> x4, waiting for transfers between devices: 5.73 us -> 6.67 us  [swap_cores(): return lax.ppermute(value, 'core', perm=[(0, 1), (1, 0)])]
  transfers between devices with their start and end apart: 9 -> 8, of which waited for: 6 -> 3; matrix products, arithmetic and copies ran while one was open for 16% -> 18% of each run, Pallas kernels for 0% -> 0%
where the time goes in v12:
time: 291 us; the launch traced here: 290 us
  blocking collectives  93.6 us (32%)
  waiting for transfers between devices  86.4 us (30%)
  matrix products  33.8 us (12%)
  other arithmetic  26.8 us (9%)
  local copies, waits for them, and re-layouts  22.6 us (8%)
  between operations  14.3 us (5%)
  starting transfers between devices  12.9 us (4%)
    all_to_all x1, blocking collectives, shards(): lax.all_to_all(jnp.stack([pack_rows(tokens), pack_rows(out_grad)]), 'expe...  93.6 us
    all_to_all x1, waiting for transfers between devices, shards(): lax.all_to_all(token_grad.reshape(experts, capacity, model_width), 'exper...  50.8 us
    all_to_all x1, waiting for transfers between devices, shards(): lax.all_to_all(expert_out, 'expert', split_axis=0, concat_axis=0, tiled=T...  28.9 us
    dot_general x3, matrix products, contract_last(): lax.dot_general(matrix_a, matrix_b, (((1,), (1,)), ((), ())), preferred_e...  12.2 us
    dot_general x3, matrix products, contract_first(): lax.dot_general(matrix_a, matrix_b, (((0,), (0,)), ((), ())), preferred_e...  7.7 us
    ppermute x4, waiting for transfers between devices, swap_cores(): return lax.ppermute(value, 'core', perm=[(0, 1), (1, 0)])  6.67 us
    gather x2, local copies, waits for them, and re-layouts, pack_rows(): jnp.take(values, source_row, axis=0) * filled  6.33 us
    convert_element_type x2, other arithmetic, pair_total(): return (partial[:slots] + arrived).astype(jnp.bfloat16)  6.2 us
  transfers between devices with their start and end apart: 8, of which 3 were waited for; matrix products, arithmetic and copies ran while one was open for 18% of the time, Pallas kernels for 0%

profile of v12, /device:TPU:1, one launch (start us, length us, event | category | flops | bytes accessed | tf_op | source)
XLA Modules:
  0.0 290.4 jit_solution(3883968914655255935)
XLA Ops:
  7.2 1.9 pad_maximum_fusion.3
  14.3 1.6 multiply_convert_fusion.1
  15.9 3.2 %gather_fusion.1 = bf16[320,2560]{1,0:T(8,128)(2,1)} fusion(bf16[256,2560]{1,0:T(8,128)(2,1)S(1)} %multiply_convert_fusion.1, s32[1024]{0:T(1024)S(1)} %pad_clamp_fusion.1), kind=kCustom, calls=%fused_computation.2.clone | custom fusion | bytes 3278080 | tf_op jit(solution)/shard_map/jit(_take)/gather | solution.py:81
  19.1 3.2 %gather_fusion = bf16[320,2560]{1,0:T(8,128)(2,1)} fusion(bf16[256,2560]{1,0:T(8,128)(2,1)S(1)} %copy-done, s32[1024]{0:T(1024)S(1)} %pad_clamp_fusion.1), kind=kCustom, calls=%fused_computation.clone | custom fusion | bytes 3278080 | tf_op jit(solution)/shard_map/jit(_take)/gather | solution.py:81
  22.2 2.2 scatter_custom_fusion.1
  24.4 1.9 select_multiply_fusion.1
  26.6 93.6 %all_to_all.15 = bf16[2,8,40,2560]{3,2,0,1:T(8,128)(2,1)S(1)} all-to-all(bf16[2,8,40,2560]{3,2,0,1:T(8,128)(2,1)S(1)} %pad_maximum_fusion.2), channel_id=1, replica_groups=mesh['x'=4,'zh'=4,'core'=2,'expert'=8] {'expert'}, dimensions={1} | all-to-all | bytes 6553600 | tf_op jit(solution)/shard_map/all_to_all | solution.py:87
  120.4 1.9 collective-permute-start
  122.3 6.7 %collective-permute-done = bf16[2,320,2560]{2,1,0:T(8,128)(2,1)} collective-permute-done((bf16[2,320,2560]{2,1,0:T(8,128)(2,1)S(1)}, bf16[2,320,2560]{2,1,0:T(8,128)(2,1)}, u32[]{:S(2)}, u32[]{:S(2)}) %collective-permute-start) | collective-permute-done | bytes 3276832 | tf_op jit(solution)/shard_map/ppermute | solution.py:25
  129.0 3.0 %fusion.4 = bf16[640,2560]{1,0:T(8,128)(2,1)} fusion(bf16[2,320,2560]{2,1,0:T(8,128)(2,1)S(1)} %bitcast.67, bf16[2,320,2560]{2,1,0:T(8,128)(2,1)} %collective-permute-done), kind=kLoop, calls=%fused_computation.17 | loop fusion | flops 6553600 | bytes 9830400 | tf_op jit(solution)/shard_map/squeeze | solution.py:95
  132.0 5.1 %fusion.20 = f32[640,384]{1,0:T(8,128)S(1)} fusion(bf16[640,2560]{1,0:T(8,128)(2,1)} %fusion.4, bf16[3,2560,768]{2,1,0:T(8,128)(2,1)} %all-gather.2.cloned.1.call-done, pred[]{:T(512)S(6)} %eq.37), kind=kOutput, calls=%fused_computation.46 | convolution fusion | flops 1259274240 | bytes 8192001 | tf_op jit(solution)/shard_map/dot_general | solution.py:98
  137.1 4.0 %fusion.17 = f32[640,384]{1,0:T(8,128)S(1)} fusion(bf16[640,2560]{1,0:T(8,128)(2,1)S(1)} %copy-done.5, bf16[3,2560,768]{2,1,0:T(8,128)(2,1)} %all-gather.2.cloned.1.call-done, pred[]{:T(512)S(6)} %eq.37), kind=kOutput, calls=%fused_computation.45 | convolution fusion | flops 1259274240 | bytes 8192001 | tf_op jit(solution)/shard_map/dot_general | solution.py:97
  141.1 4.8 %multiply_convert_fusion.2 = (bf16[640,384]{1,0:T(8,128)(2,1)S(1)}, bf16[640,384]{1,0:T(8,128)(2,1)S(1)}, bf16[640,384]{1,0:T(8,128)(2,1)S(1)}) fusion(f32[640,384]{1,0:T(8,128)S(1)} %fusion.17, f32[640,384]{1,0:T(8,128)S(1)} %fusion.20, bf16[3,2560,768]{2,1,0:T(8,128)(2,1)} %all-gather.2.cloned.1.call-done, pred[]{:T(512)S(6)} %eq.37, ...), kind=kOutput, calls=%fused_computation.36 | convolution fusion | flops 1269514240 | bytes 13926401 | tf_op jit(solution)/shard_map/dot_general | solution.py:102
  146.0 2.1 fusion.1
  148.1 2.1 fusion
  150.2 3.5 %fusion.2 = bf16[1,2560,384]{2,1,0:T(8,128)(2,1)S(1)} fusion(bf16[640,384]{1,0:T(8,128)(2,1)S(1)} %get-tuple-element.11, bf16[2,320,2560]{2,1,0:T(8,128)(2,1)} %collective-permute-done, bf16[2,320,2560]{2,1,0:T(8,128)(2,1)S(1)} %bitcast.69), kind=kOutput, calls=%fused_computation.15 | convolution fusion | flops 1265827840 | bytes 9011200 | tf_op jit(solution)/shard_map/dot_general | solution.py:19
  153.7 3.2 %pad_maximum_fusion = bf16[3,2560,384]{2,1,0:T(8,128)(2,1)} fusion(bf16[1,2560,384]{2,1,0:T(8,128)(2,1)S(1)} %fusion.2, bf16[1,2560,384]{2,1,0:T(8,128)(2,1)S(1)} %fusion.1, bf16[1,2560,384]{2,1,0:T(8,128)(2,1)S(1)} %fusion), kind=kLoop, calls=%fused_computation.8 | loop fusion | flops 5898240 | bytes 11796480 | tf_op jit(solution)/shard_map/stack | solution.py:36
  158.0 4.1 %fusion.15 = f32[640,2560]{1,0:T(8,128)S(1)} fusion(bf16[640,384]{1,0:T(8,128)(2,1)S(1)} %copy-done.11, bf16[3,2560,768]{2,1,0:T(8,128)(2,1)} %all-gather.2.cloned.1.call-done, pred[]{:T(512)S(6)} %eq.37), kind=kOutput, calls=%fused_computation.44 | convolution fusion | flops 1259274240 | bytes 10977281 | tf_op jit(solution)/shard_map/dot_general | solution.py:13
  162.1 4.1 %convolution_add_fusion = f32[640,2560]{1,0:T(8,128)S(1)} fusion(f32[640,2560]{1,0:T(8,128)S(1)} %fusion.15, bf16[640,384]{1,0:T(8,128)(2,1)S(1)} %copy-done.7, bf16[3,2560,768]{2,1,0:T(8,128)(2,1)} %all-gather.2.cloned.1.call-done, pred[]{:T(512)S(6)} %eq.37), kind=kOutput, calls=%fused_computation.9 | convolution fusion | flops 1260912640 | bytes 17530880 | tf_op jit(solution)/shard_map/dot_general | solution.py:13
  167.3 4.1 %fusion.23 = f32[640,2560]{1,0:T(8,128)S(1)} fusion(bf16[640,384]{1,0:T(8,128)(2,1)S(1)} %copy-done.9, bf16[3,2560,768]{2,1,0:T(8,128)(2,1)} %all-gather.2.cloned.1.call-done, pred[]{:T(512)S(6)} %eq.37), kind=kOutput, calls=%fused_computation.47 | convolution fusion | flops 1259274240 | bytes 10977281 | tf_op jit(solution)/shard_map/dot_general | solution.py:13
  171.4 2.7 copy-done.2
  174.1 2.0 slice.104
  176.4 1.6 fusion.5
  178.0 4.6 %all-to-all-start.2 = ((bf16[8,40,2560]{2,1,0:T(8,128)(2,1)}), bf16[8,40,2560]{2,1,0:T(8,128)(2,1)S(1)}, u32[]{:S(2)}, u32[]{:S(2)}) async-start(bf16[8,40,2560]{2,1,0:T(8,128)(2,1)} %bitcast.19), calls=%async_computation.2 | async-start | bytes 3276800 | tf_op jit(solution)/shard_map/all_to_all | solution.py:124
  182.6 4.6 %fusion.7 = bf16[320,2560]{1,0:T(8,128)(2,1)} fusion(f32[320,2560]{1,0:T(8,128)} %collective-permute-done.1, f32[640,2560]{1,0:T(8,128)} %copy-done.2), kind=kLoop, calls=%fused_computation.23 | loop fusion | flops 1638400 | bytes 8192000 | tf_op jit(solution)/shard_map/convert_element_type | solution.py:54
  187.2 50.8 %all-to-all-done.2 = bf16[8,40,2560]{2,1,0:T(8,128)(2,1)S(1)} async-done(((bf16[8,40,2560]{2,1,0:T(8,128)(2,1)}), bf16[8,40,2560]{2,1,0:T(8,128)(2,1)S(1)}, u32[]{:S(2)}, u32[]{:S(2)}) %all-to-all-start.2) | async-done | bytes 1638432 | tf_op jit(solution)/shard_map/all_to_all | solution.py:124
  238.0 3.9 %all-to-all-start.1 = ((bf16[8,40,2560]{2,1,0:T(8,128)(2,1)}), bf16[8,40,2560]{2,1,0:T(8,128)(2,1)S(1)}, u32[]{:S(2)}, u32[]{:S(2)}) async-start(bf16[8,40,2560]{2,1,0:T(8,128)(2,1)} %bitcast.72), calls=%async_computation.1 | async-start | bytes 3276800 | tf_op jit(solution)/shard_map/all_to_all | solution.py:115
  241.9 2.5 gather_fusion.3
  244.5 28.9 %all-to-all-done.1 = bf16[8,40,2560]{2,1,0:T(8,128)(2,1)S(1)} async-done(((bf16[8,40,2560]{2,1,0:T(8,128)(2,1)}), bf16[8,40,2560]{2,1,0:T(8,128)(2,1)S(1)}, u32[]{:S(2)}, u32[]{:S(2)}) %all-to-all-start.1) | async-done | bytes 1638432 | tf_op jit(solution)/shard_map/all_to_all | solution.py:115
  273.4 2.5 gather_fusion.2
  275.9 2.9 multiply_convert_fusion
  278.8 1.5 collective-permute-start.3
  (60 shorter events, 11.5 us)
Async XLA Ops:
  7.2 11.9 %copy-start = (bf16[256,2560]{1,0:T(8,128)(2,1)S(1)}, bf16[256,2560]{1,0:T(8,128)(2,1)}, u32[]{:S(2)}) copy-start(bf16[256,2560]{1,0:T(8,128)(2,1)} %param.11) | copy-start | bytes 3932164
  7.2 124.8 %all-gather.2.cloned.1.call-start = ((), (), s32[]{:S(2)}) async-start(), calls=%async_computation.4 | async-start | bytes 12165120 | tf_op jit(solution)/shard_map/all_gather | solution.py:29
  9.1 269.6 %reduce-scatter.2.cloned.1.call-start = ((), (), s32[]{:S(2)}) async-start(), calls=%async_computation.5 | async-start | bytes 6266880 | tf_op jit(solution)/shard_map/reduce_scatter | solution.py:37
  19.0 5.4 %copy-start.3 = (bf16[320,2560]{1,0:T(8,128)(2,1)S(1)}, bf16[320,2560]{1,0:T(8,128)(2,1)}, u32[]{:S(2)}) copy-start(bf16[320,2560]{1,0:T(8,128)(2,1)} %gather_fusion.1) | copy-start | bytes 4915204
  120.4 8.6 %collective-permute-start = (bf16[2,320,2560]{2,1,0:T(8,128)(2,1)S(1)}, bf16[2,320,2560]{2,1,0:T(8,128)(2,1)}, u32[]{:S(2)}, u32[]{:S(2)}) collective-permute-start(bf16[2,320,2560]{2,1,0:T(8,128)(2,1)S(1)} %bitcast.66), channel_id=1, source_target_pairs={{0,8},{8,0},{1,9},{9,1},{2,10},{10,2},{3,11},{11,3},{4,12},{12,4},... | collective-permute-start | bytes 9830408 | tf_op jit(solution)/shard_map/ppermute | solution.py:25
  132.0 5.1 %copy-start.5 = (bf16[640,2560]{1,0:T(8,128)(2,1)S(1)}, bf16[640,2560]{1,0:T(8,128)(2,1)}, u32[]{:S(2)}) copy-start(bf16[640,2560]{1,0:T(8,128)(2,1)} %fusion.4) | copy-start | bytes 9830404
  145.9 2.1 copy-start.6
  146.0 2.1 copy-start.10
  146.0 4.2 %copy-start.8 = (bf16[640,384]{1,0:T(8,128)(2,1)}, bf16[640,384]{1,0:T(8,128)(2,1)S(1)}, u32[]{:S(2)}) copy-start(bf16[640,384]{1,0:T(8,128)(2,1)S(1)} %get-tuple-element.11) | copy-start | bytes 1474564
  157.0 1.0 copy-start.11
  158.0 4.1 %copy-start.7 = (bf16[640,384]{1,0:T(8,128)(2,1)S(1)}, bf16[640,384]{1,0:T(8,128)(2,1)}, u32[]{:S(2)}) copy-start(bf16[640,384]{1,0:T(8,128)(2,1)} %copy-done.6) | copy-start | bytes 1474564
  166.2 1.2 copy-start.9
  166.4 10.0 %collective-permute-start.2 = (f32[320,2560]{1,0:T(8,128)S(1)}, f32[320,2560]{1,0:T(8,128)S(1)}, u32[]{:S(2)}, u32[]{:S(2)}) collective-permute-start(f32[320,2560]{1,0:T(8,128)S(1)} %slice.106), channel_id=1, source_target_pairs={{0,8},{8,0},{1,9},{9,1},{2,10},{10,2},{3,11},{11,3},{4,12},{12,4},... | collective-permute-start | bytes 9830408 | tf_op jit(solution)/shard_map/ppermute | solution.py:25
  171.4 2.7 copy-start.2
  176.1 6.6 %collective-permute-start.1 = (f32[320,2560]{1,0:T(8,128)}, f32[320,2560]{1,0:T(8,128)}, u32[]{:S(2)}, u32[]{:S(2)}) collective-permute-start(f32[320,2560]{1,0:T(8,128)} %slice.104), channel_id=1, source_target_pairs={{0,8},{8,0},{1,9},{9,1},{2,10},{10,2},{3,11},{11,3},{4,12},{12,4},... | collective-permute-start | bytes 9830408 | tf_op jit(solution)/shard_map/ppermute | solution.py:25
  178.0 60.0 %all-to-all-start.2 = ((bf16[8,40,2560]{2,1,0:T(8,128)(2,1)}), bf16[8,40,2560]{2,1,0:T(8,128)(2,1)S(1)}, u32[]{:S(2)}, u32[]{:S(2)}) async-start(bf16[8,40,2560]{2,1,0:T(8,128)(2,1)} %bitcast.19), calls=%async_computation.2 | async-start | bytes 3276800 | tf_op jit(solution)/shard_map/all_to_all | solution.py:124
  187.2 54.7 %copy-start.12 = (s32[256,1]{0,1:T(1,128)S(1)}, s32[256,1]{0,1:T(1,128)}, u32[]{:S(2)}) copy-start(s32[256,1]{0,1:T(1,128)} %param.12) | copy-start | bytes 3076
  238.0 35.3 %all-to-all-start.1 = ((bf16[8,40,2560]{2,1,0:T(8,128)(2,1)}), bf16[8,40,2560]{2,1,0:T(8,128)(2,1)S(1)}, u32[]{:S(2)}, u32[]{:S(2)}) async-start(bf16[8,40,2560]{2,1,0:T(8,128)(2,1)} %bitcast.72), calls=%async_computation.1 | async-start | bytes 3276800 | tf_op jit(solution)/shard_map/all_to_all | solution.py:115
  275.9 4.4 %copy-start.4 = (bf16[256,2560]{1,0:T(8,128)(2,1)S(1)}, bf16[256,2560]{1,0:T(8,128)(2,1)}, u32[]{:S(2)}) copy-start(bf16[256,2560]{1,0:T(8,128)(2,1)} %gather_fusion.3) | copy-start | bytes 3932164
  275.9 7.7 %copy-start.1 = (bf16[256,2560]{1,0:T(8,128)(2,1)S(1)}, bf16[256,2560]{1,0:T(8,128)(2,1)}, u32[]{:S(2)}) copy-start(bf16[256,2560]{1,0:T(8,128)(2,1)} %param.11) | copy-start | bytes 3932164
  278.8 3.8 %collective-permute-start.3 = (bf16[3,160,384]{2,1,0:T(8,128)(2,1)}, bf16[3,160,384]{2,1,0:T(8,128)(2,1)S(1)}, u32[]{:S(2)}, u32[]{:S(2)}) collective-permute-start(bf16[3,160,384]{2,1,0:T(8,128)(2,1)} %reduce-scatter.2.cloned.1.call-done), channel_id=1, source_target_pairs={{0,8},{8,0},{1,9},{9,1},{2,10},{10,2},{3,11},{11,3},{4,12},{12,4},... | collective-permute-start | bytes 1105928 | tf_op jit(solution)/shard_map/ppermute | solution.py:25
Sparse Core Ops, SparseCore 0:
  11.2 119.3 all-gather.1
  157.1 116.5 reduce-scatter.1

commit v13 on v12

--- a/solution.py
+++ b/solution.py
@@ -28,8 +28,8 @@
 def gather_weights(*weights):
     full = lax.all_gather(jnp.stack(weights), DP, axis=1, tiled=True)
     half = full.shape[2] // 2
-    first = lax.axis_index("core") == 0
-    return [jnp.where(first, full[i, :, :half], full[i, :, half:]) for i in range(len(weights))]
+    start = lax.axis_index("core") * half
+    return [lax.dynamic_slice_in_dim(full[i], start, half, axis=1) for i in range(len(weights))]
 
 
 def scatter_grads(*parts):

time: 291 us -> 288 us (0.990)
  matrix products: 33.8 us -> 25.2 us
  local copies, waits for them, and re-layouts: 22.6 us -> 28.2 us
    slice x1 -> x2, local copies, waits for them, and re-layouts: 0.21 us -> 5.19 us  [the longest x1 4.97 us: gather_weights(): full[i]]
    dot_general x1, matrix products: 5.12 us -> 1.86 us  [shards(): act_up = jnp.dot(received, up_own, preferred_element_type=jnp.float32)]
  transfers between devices with their start and end apart: 8 -> 8, of which waited for: 3 -> 4; matrix products, arithmetic and copies ran while one was open for 18% -> 18% of each run, Pallas kernels for 0% -> 0%
where the time goes in v13:
time: 288 us
  blocking collectives  93.6 us (32%)
  waiting for transfers between devices  84.2 us (29%)
  local copies, waits for them, and re-layouts  28.2 us (10%)
  other arithmetic  27 us (9%)
  matrix products  25.2 us (9%)
  starting transfers between devices  15.1 us (5%)
  between operations  14.4 us (5%)
    all_to_all x1, blocking collectives, shards(): lax.all_to_all(jnp.stack([pack_rows(tokens), pack_rows(out_grad)]), 'expe...  93.6 us
    all_to_all x1, waiting for transfers between devices, shards(): lax.all_to_all(token_grad.reshape(experts, capacity, model_width), 'exper...  48.6 us
    all_to_all x1, waiting for transfers between devices, shards(): lax.all_to_all(expert_out, 'expert', split_axis=0, concat_axis=0, tiled=T...  28.3 us
    dot_general x3, matrix products, contract_last(): lax.dot_general(matrix_a, matrix_b, (((1,), (1,)), ((), ())), preferred_e...  10.1 us
    dot_general x3, matrix products, contract_first(): lax.dot_general(matrix_a, matrix_b, (((0,), (0,)), ((), ())), preferred_e...  7.78 us
    ppermute x4, waiting for transfers between devices, swap_cores(): return lax.ppermute(value, 'core', perm=[(0, 1), (1, 0)])  7.3 us
    convert_element_type x2, other arithmetic, pair_total(): return (partial[:slots] + arrived).astype(jnp.bfloat16)  6.37 us
    gather x2, local copies, waits for them, and re-layouts, pack_rows(): jnp.take(values, source_row, axis=0) * filled  6.32 us
  transfers between devices with their start and end apart: 8, of which 4 were waited for; matrix products, arithmetic and copies ran while one was open for 18% of the time, Pallas kernels for 0%

profile of v13, /device:TPU:1, one launch (start us, length us, event | category | flops | bytes accessed | tf_op | source)
XLA Modules:
  0.0 287.8 jit_solution(17447754134198401573)
XLA Ops:
  7.2 1.9 pad_maximum_fusion.3
  14.3 1.6 multiply_convert_fusion.1
  15.9 3.2 %gather_fusion.1 = bf16[320,2560]{1,0:T(8,128)(2,1)} fusion(bf16[256,2560]{1,0:T(8,128)(2,1)S(1)} %multiply_convert_fusion.1, s32[1024]{0:T(1024)S(1)} %pad_clamp_fusion.1), kind=kCustom, calls=%fused_computation.2.clone | custom fusion | bytes 3278080 | tf_op jit(solution)/shard_map/jit(_take)/gather | solution.py:81
  19.1 3.2 %gather_fusion = bf16[320,2560]{1,0:T(8,128)(2,1)} fusion(bf16[256,2560]{1,0:T(8,128)(2,1)S(1)} %copy-done, s32[1024]{0:T(1024)S(1)} %pad_clamp_fusion.1), kind=kCustom, calls=%fused_computation.clone | custom fusion | bytes 3278080 | tf_op jit(solution)/shard_map/jit(_take)/gather | solution.py:81
  22.2 2.2 scatter_custom_fusion.1
  24.4 1.9 select_multiply_fusion.1
  26.6 93.6 %all_to_all.15 = bf16[2,8,40,2560]{3,2,0,1:T(8,128)(2,1)S(1)} all-to-all(bf16[2,8,40,2560]{3,2,0,1:T(8,128)(2,1)S(1)} %pad_maximum_fusion.2), channel_id=1, replica_groups=mesh['x'=4,'zh'=4,'core'=2,'expert'=8] {'expert'}, dimensions={1} | all-to-all | bytes 6553600 | tf_op jit(solution)/shard_map/all_to_all | solution.py:87
  120.4 1.9 collective-permute-start
  122.3 7.2 %collective-permute-done = bf16[2,320,2560]{2,1,0:T(8,128)(2,1)} collective-permute-done((bf16[2,320,2560]{2,1,0:T(8,128)(2,1)S(1)}, bf16[2,320,2560]{2,1,0:T(8,128)(2,1)}, u32[]{:S(2)}, u32[]{:S(2)}) %collective-permute-start) | collective-permute-done | bytes 3276832 | tf_op jit(solution)/shard_map/ppermute | solution.py:25
  129.5 3.0 %fusion.4 = bf16[640,2560]{1,0:T(8,128)(2,1)} fusion(bf16[2,320,2560]{2,1,0:T(8,128)(2,1)S(1)} %bitcast.70, bf16[2,320,2560]{2,1,0:T(8,128)(2,1)} %collective-permute-done), kind=kLoop, calls=%fused_computation.17 | loop fusion | flops 6553600 | bytes 9830400 | tf_op jit(solution)/shard_map/squeeze | solution.py:95
  132.5 5.0 %fusion.45 = (bf16[1,2560,768]{2,1,0:T(8,128)(2,1)S(1)}, bf16[1,2560,768]{2,1,0:T(8,128)(2,1)S(1)}, bf16[1,2560,768]{2,1,0:T(8,128)(2,1)S(1)}) fusion(bf16[3,2560,768]{2,1,0:T(8,128)(2,1)} %all-gather.2.cloned.1.call-done), kind=kLoop, calls=%fused_computation.85 | loop fusion | bytes 23592960 | tf_op jit(solution)/shard_map/slice | solution.py:32
  137.8 1.9 fusion.13
  139.7 1.9 fusion.17
  141.6 3.6 %multiply_convert_fusion.2 = (bf16[640,384]{1,0:T(8,128)(2,1)S(1)}, bf16[640,384]{1,0:T(8,128)(2,1)S(1)}, bf16[640,384]{1,0:T(8,128)(2,1)S(1)}) fusion(f32[640,384]{1,0:T(8,128)S(1)} %fusion.17, f32[640,384]{1,0:T(8,128)S(1)} %fusion.13, bf16[1,2560,768]{2,1,0:T(8,128)(2,1)S(1)} %get-tuple-element.9, s32[]{:T(128)S(6)} %select_n.45, ...), kind=kOutput, calls=%fused_computation.47 | convolution fusion | flops 1268531200 | bytes 11960324 | tf_op jit(solution)/shard_map/dot_general | solution.py:102
  145.3 2.1 fusion.1
  147.4 2.1 fusion
  149.6 3.5 %fusion.2 = bf16[1,2560,384]{2,1,0:T(8,128)(2,1)S(1)} fusion(bf16[640,384]{1,0:T(8,128)(2,1)S(1)} %get-tuple-element.14, bf16[2,320,2560]{2,1,0:T(8,128)(2,1)} %collective-permute-done, bf16[2,320,2560]{2,1,0:T(8,128)(2,1)S(1)} %bitcast.72), kind=kOutput, calls=%fused_computation.15 | convolution fusion | flops 1265827840 | bytes 9011200 | tf_op jit(solution)/shard_map/dot_general | solution.py:19
  153.1 3.3 %pad_maximum_fusion = bf16[3,2560,384]{2,1,0:T(8,128)(2,1)} fusion(bf16[1,2560,384]{2,1,0:T(8,128)(2,1)S(1)} %fusion.2, bf16[1,2560,384]{2,1,0:T(8,128)(2,1)S(1)} %fusion.1, bf16[1,2560,384]{2,1,0:T(8,128)(2,1)S(1)} %fusion), kind=kLoop, calls=%fused_computation.8 | loop fusion | flops 5898240 | bytes 11796480 | tf_op jit(solution)/shard_map/stack | solution.py:36
  157.4 3.6 %fusion.15 = f32[640,2560]{1,0:T(8,128)S(1)} fusion(bf16[640,384]{1,0:T(8,128)(2,1)S(1)} %copy-done.13, bf16[1,2560,768]{2,1,0:T(8,128)(2,1)} %copy-done.4, s32[]{:T(128)S(6)} %select_n.45), kind=kOutput, calls=%fused_computation.34 | convolution fusion | flops 1258291200 | bytes 9011204 | tf_op jit(solution)/shard_map/dot_general | solution.py:13
  161.0 1.9 convolution_add_fusion
  165.1 4.6 %fusion.10 = f32[640,2560]{1,0:T(8,128)} fusion(bf16[640,384]{1,0:T(8,128)(2,1)S(1)} %copy-done.11, bf16[1,2560,768]{2,1,0:T(8,128)(2,1)S(1)} %copy-done.3, s32[]{:T(128)S(6)} %select_n.45), kind=kOutput, calls=%fused_computation.29 | convolution fusion | flops 1258291200 | bytes 9011204 | tf_op jit(solution)/shard_map/dot_general | solution.py:13
  169.8 3.9 %slice.89 = f32[320,2560]{1,0:T(8,128)} slice(f32[640,2560]{1,0:T(8,128)} %fusion.10), slice={[320:640], [0:2560]} | slice | bytes 6553600 | tf_op jit(solution)/shard_map/slice | solution.py:53
  174.0 1.6 fusion.5
  175.6 4.1 %all-to-all-start.2 = ((bf16[8,40,2560]{2,1,0:T(8,128)(2,1)}), bf16[8,40,2560]{2,1,0:T(8,128)(2,1)S(1)}, u32[]{:S(2)}, u32[]{:S(2)}) async-start(bf16[8,40,2560]{2,1,0:T(8,128)(2,1)} %bitcast.19), calls=%async_computation.2 | async-start | bytes 3276800 | tf_op jit(solution)/shard_map/all_to_all | solution.py:124
  179.8 4.8 %fusion.7 = bf16[320,2560]{1,0:T(8,128)(2,1)} fusion(f32[320,2560]{1,0:T(8,128)} %collective-permute-done.1, f32[640,2560]{1,0:T(8,128)} %fusion.10), kind=kLoop, calls=%fused_computation.23 | loop fusion | flops 1638400 | bytes 8192000 | tf_op jit(solution)/shard_map/convert_element_type | solution.py:54
  184.6 48.6 %all-to-all-done.2 = bf16[8,40,2560]{2,1,0:T(8,128)(2,1)S(1)} async-done(((bf16[8,40,2560]{2,1,0:T(8,128)(2,1)}), bf16[8,40,2560]{2,1,0:T(8,128)(2,1)S(1)}, u32[]{:S(2)}, u32[]{:S(2)}) %all-to-all-start.2) | async-done | bytes 1638432 | tf_op jit(solution)/shard_map/all_to_all | solution.py:124
  233.2 6.1 %all-to-all-start.1 = ((bf16[8,40,2560]{2,1,0:T(8,128)(2,1)}), bf16[8,40,2560]{2,1,0:T(8,128)(2,1)S(1)}, u32[]{:S(2)}, u32[]{:S(2)}) async-start(bf16[8,40,2560]{2,1,0:T(8,128)(2,1)} %bitcast.75), calls=%async_computation.1 | async-start | bytes 3276800 | tf_op jit(solution)/shard_map/all_to_all | solution.py:115
  239.3 2.5 gather_fusion.3
  241.8 28.3 %all-to-all-done.1 = bf16[8,40,2560]{2,1,0:T(8,128)(2,1)S(1)} async-done(((bf16[8,40,2560]{2,1,0:T(8,128)(2,1)}), bf16[8,40,2560]{2,1,0:T(8,128)(2,1)S(1)}, u32[]{:S(2)}, u32[]{:S(2)}) %all-to-all-start.1) | async-done | bytes 1638432 | tf_op jit(solution)/shard_map/all_to_all | solution.py:115
  270.1 2.5 gather_fusion.2
  272.6 2.9 %multiply_convert_fusion = bf16[256,2560]{1,0:T(8,128)(2,1)} fusion(bf16[256,2560]{1,0:T(8,128)(2,1)} %gather_fusion.2, f32[256]{0:T(256)S(1)} %bitcast.80, pred[256]{0:T(512)(128)(4,1)S(1)} %get-tuple-element.7), kind=kLoop, calls=%fused_computation.25 | loop fusion | flops 2621440 | bytes 2622720 | tf_op jit(solution)/shard_map/convert_element_type | solution.py:118
  275.5 2.1 collective-permute-start.3
  (69 shorter events, 13.0 us)
Async XLA Ops:
  7.2 11.9 %copy-start = (bf16[256,2560]{1,0:T(8,128)(2,1)S(1)}, bf16[256,2560]{1,0:T(8,128)(2,1)}, u32[]{:S(2)}) copy-start(bf16[256,2560]{1,0:T(8,128)(2,1)} %param.11) | copy-start | bytes 3932164
  7.2 125.3 %all-gather.2.cloned.1.call-start = ((), (), s32[]{:S(2)}) async-start(), calls=%async_computation.4 | async-start | bytes 12165120 | tf_op jit(solution)/shard_map/all_gather | solution.py:29
  9.1 266.4 %reduce-scatter.2.cloned.1.call-start = ((), (), s32[]{:S(2)}) async-start(), calls=%async_computation.5 | async-start | bytes 6266880 | tf_op jit(solution)/shard_map/reduce_scatter | solution.py:37
  19.0 5.3 %copy-start.7 = (bf16[320,2560]{1,0:T(8,128)(2,1)S(1)}, bf16[320,2560]{1,0:T(8,128)(2,1)}, u32[]{:S(2)}) copy-start(bf16[320,2560]{1,0:T(8,128)(2,1)} %gather_fusion.1) | copy-start | bytes 4915204
  120.4 9.1 %collective-permute-start = (bf16[2,320,2560]{2,1,0:T(8,128)(2,1)S(1)}, bf16[2,320,2560]{2,1,0:T(8,128)(2,1)}, u32[]{:S(2)}, u32[]{:S(2)}) collective-permute-start(bf16[2,320,2560]{2,1,0:T(8,128)(2,1)S(1)} %bitcast.69), channel_id=1, source_target_pairs={{0,8},{8,0},{1,9},{9,1},{2,10},{10,2},{3,11},{11,3},{4,12},{12,4},... | collective-permute-start | bytes 9830408 | tf_op jit(solution)/shard_map/ppermute | solution.py:25
  132.5 5.4 %copy-start.9 = (bf16[640,2560]{1,0:T(8,128)(2,1)S(1)}, bf16[640,2560]{1,0:T(8,128)(2,1)}, u32[]{:S(2)}) copy-start(bf16[640,2560]{1,0:T(8,128)(2,1)} %fusion.4) | copy-start | bytes 9830404
  137.5 4.1 %copy-start.2 = (bf16[1,2560,768]{2,1,0:T(8,128)(2,1)}, bf16[1,2560,768]{2,1,0:T(8,128)(2,1)S(1)}, u32[]{:S(2)}) copy-start(bf16[1,2560,768]{2,1,0:T(8,128)(2,1)S(1)} %get-tuple-element.9) | copy-start | bytes 11796484
  137.5 7.7 %copy-start.4 = (bf16[1,2560,768]{2,1,0:T(8,128)(2,1)}, bf16[1,2560,768]{2,1,0:T(8,128)(2,1)S(1)}, u32[]{:S(2)}) copy-start(bf16[1,2560,768]{2,1,0:T(8,128)(2,1)S(1)} %get-tuple-element.11) | copy-start | bytes 11796484
  137.5 7.7 %copy-start.5 = (bf16[1,2560,768]{2,1,0:T(8,128)(2,1)}, bf16[1,2560,768]{2,1,0:T(8,128)(2,1)S(1)}, u32[]{:S(2)}) copy-start(bf16[1,2560,768]{2,1,0:T(8,128)(2,1)S(1)} %get-tuple-element.10) | copy-start | bytes 11796484
  145.2 2.2 copy-start.14
  145.2 2.2 copy-start.12
  145.3 4.3 %copy-start.10 = (bf16[640,384]{1,0:T(8,128)(2,1)}, bf16[640,384]{1,0:T(8,128)(2,1)S(1)}, u32[]{:S(2)}) copy-start(bf16[640,384]{1,0:T(8,128)(2,1)S(1)} %get-tuple-element.14) | copy-start | bytes 1474564
  156.4 1.0 copy-start.13
  157.4 3.6 %copy-start.6 = (bf16[1,2560,768]{2,1,0:T(8,128)(2,1)S(1)}, bf16[1,2560,768]{2,1,0:T(8,128)(2,1)}, u32[]{:S(2)}) copy-start(bf16[1,2560,768]{2,1,0:T(8,128)(2,1)} %copy-done.5) | copy-start | bytes 11796484
  157.4 3.6 %copy-start.15 = (bf16[640,384]{1,0:T(8,128)(2,1)S(1)}, bf16[640,384]{1,0:T(8,128)(2,1)}, u32[]{:S(2)}) copy-start(bf16[640,384]{1,0:T(8,128)(2,1)} %copy-done.14) | copy-start | bytes 1474564
  162.9 2.1 copy-start.3
  162.9 2.2 copy-start.11
  163.2 10.8 %collective-permute-start.2 = (f32[320,2560]{1,0:T(8,128)S(1)}, f32[320,2560]{1,0:T(8,128)S(1)}, u32[]{:S(2)}, u32[]{:S(2)}) collective-permute-start(f32[320,2560]{1,0:T(8,128)S(1)} %slice.91), channel_id=1, source_target_pairs={{0,8},{8,0},{1,9},{9,1},{2,10},{10,2},{3,11},{11,3},{4,12},{12,4},... | collective-permute-start | bytes 9830408 | tf_op jit(solution)/shard_map/ppermute | solution.py:25
  173.6 6.2 %collective-permute-start.1 = (f32[320,2560]{1,0:T(8,128)}, f32[320,2560]{1,0:T(8,128)}, u32[]{:S(2)}, u32[]{:S(2)}) collective-permute-start(f32[320,2560]{1,0:T(8,128)} %slice.89), channel_id=1, source_target_pairs={{0,8},{8,0},{1,9},{9,1},{2,10},{10,2},{3,11},{11,3},{4,12},{12,4},... | collective-permute-start | bytes 9830408 | tf_op jit(solution)/shard_map/ppermute | solution.py:25
  175.6 57.6 %all-to-all-start.2 = ((bf16[8,40,2560]{2,1,0:T(8,128)(2,1)}), bf16[8,40,2560]{2,1,0:T(8,128)(2,1)S(1)}, u32[]{:S(2)}, u32[]{:S(2)}) async-start(bf16[8,40,2560]{2,1,0:T(8,128)(2,1)} %bitcast.19), calls=%async_computation.2 | async-start | bytes 3276800 | tf_op jit(solution)/shard_map/all_to_all | solution.py:124
  184.6 54.7 %copy-start.16 = (s32[256,1]{0,1:T(1,128)S(1)}, s32[256,1]{0,1:T(1,128)}, u32[]{:S(2)}) copy-start(s32[256,1]{0,1:T(1,128)} %param.12) | copy-start | bytes 3076
  233.2 36.9 %all-to-all-start.1 = ((bf16[8,40,2560]{2,1,0:T(8,128)(2,1)}), bf16[8,40,2560]{2,1,0:T(8,128)(2,1)S(1)}, u32[]{:S(2)}, u32[]{:S(2)}) async-start(bf16[8,40,2560]{2,1,0:T(8,128)(2,1)} %bitcast.75), calls=%async_computation.1 | async-start | bytes 3276800 | tf_op jit(solution)/shard_map/all_to_all | solution.py:115
  272.6 5.1 %copy-start.8 = (bf16[256,2560]{1,0:T(8,128)(2,1)S(1)}, bf16[256,2560]{1,0:T(8,128)(2,1)}, u32[]{:S(2)}) copy-start(bf16[256,2560]{1,0:T(8,128)(2,1)} %gather_fusion.3) | copy-start | bytes 3932164
  272.6 8.3 %copy-start.1 = (bf16[256,2560]{1,0:T(8,128)(2,1)S(1)}, bf16[256,2560]{1,0:T(8,128)(2,1)}, u32[]{:S(2)}) copy-start(bf16[256,2560]{1,0:T(8,128)(2,1)} %param.11) | copy-start | bytes 3932164
  275.5 4.4 %collective-permute-start.3 = (bf16[3,160,384]{2,1,0:T(8,128)(2,1)}, bf16[3,160,384]{2,1,0:T(8,128)(2,1)S(1)}, u32[]{:S(2)}, u32[]{:S(2)}) collective-permute-start(bf16[3,160,384]{2,1,0:T(8,128)(2,1)} %reduce-scatter.2.cloned.1.call-done), channel_id=1, source_target_pairs={{0,8},{8,0},{1,9},{9,1},{2,10},{10,2},{3,11},{11,3},{4,12},{12,4},... | collective-permute-start | bytes 1105928 | tf_op jit(solution)/shard_map/ppermute | solution.py:25
Sparse Core Ops, SparseCore 0:
  11.2 119.3 all-gather.1
  156.5 115.5 reduce-scatter.1

commit v14 on v9

--- a/solution.py
+++ b/solution.py
@@ -56,8 +56,8 @@
 
 
 def pair_total(partial, slots):
-    arrived = swap_cores(partial[slots:])
-    return (partial[:slots] + arrived).astype(jnp.bfloat16)
+    arrived = swap_cores(partial[slots:].astype(jnp.bfloat16))
+    return (partial[:slots] + arrived.astype(jnp.float32)).astype(jnp.bfloat16)
 
 
 def shards(tokens, routes, gate_levels, w_gate, w_up, w_down, grad_out):

time: 281 us -> 281 us (level)
  local copies, waits for them, and re-layouts: 24.9 us -> 20.1 us
  waiting for transfers between devices: 86.3 us -> 90.3 us
  matrix products: 22.2 us -> 25.2 us
    ppermute x5, waiting for transfers between devices: 5.73 us -> 11.7 us  [swap_cores(): return lax.ppermute(value, 'core', perm=[(0, 1), (1, 0)])]
    all_to_all x1, waiting for transfers between devices: 51.4 us -> 46.2 us  [shards(): lax.all_to_all(token_grad.reshape(experts, capacity, model_width), 'exper...]
    reduce_scatter x1, waiting for transfers between devices: 2.93 us -> 6.43 us  [scatter_grads(): chip_sum = lax.psum_scatter(stacked, CHIPS, scatter_dimension=1, tiled=True)]
    dot_general x3, matrix products: 7.39 us -> 10.4 us  [contract_last(): lax.dot_general(matrix_a, matrix_b, (((1,), (1,)), ((), ())), preferred_e...]
    unnamed x36 -> x30, local copies, waits for them, and re-layouts: 6.51 us -> 3.54 us
  transfers between devices with their start and end apart: 9 -> 9, of which waited for: 6 -> 7; matrix products, arithmetic and copies ran while one was open for 16% -> 16% of each run, Pallas kernels for 0% -> 0%
where the time goes in v14:
time: 281 us; the launch traced here: 280 us
  waiting for transfers between devices  90.3 us (32%)
  blocking collectives  90.2 us (32%)
  matrix products  25.2 us (9%)
  other arithmetic  23.9 us (9%)
  local copies, waits for them, and re-layouts  20.1 us (7%)
  starting transfers between devices  15.6 us (6%)
  between operations  14.3 us (5%)
    all_to_all x1, blocking collectives, shards(): lax.all_to_all(jnp.stack([pack_rows(tokens), pack_rows(out_grad)]), 'expe...  90.2 us
    all_to_all x1, waiting for transfers between devices, shards(): lax.all_to_all(token_grad.reshape(experts, capacity, model_width), 'exper...  46.2 us
    all_to_all x1, waiting for transfers between devices, shards(): lax.all_to_all(expert_out, 'expert', split_axis=0, concat_axis=0, tiled=T...  23.2 us
    ppermute x5, waiting for transfers between devices, swap_cores(): return lax.ppermute(value, 'core', perm=[(0, 1), (1, 0)])  11.7 us
    dot_general x3, matrix products, contract_last(): lax.dot_general(matrix_a, matrix_b, (((1,), (1,)), ((), ())), preferred_e...  10.4 us
    ppermute x5, starting transfers between devices, swap_cores(): return lax.ppermute(value, 'core', perm=[(0, 1), (1, 0)])  7.32 us
    reduce_scatter x1, waiting for transfers between devices, scatter_grads(): chip_sum = lax.psum_scatter(stacked, CHIPS, scatter_dimension=1, tiled=True)  6.43 us
    gather x2, local copies, waits for them, and re-layouts, pack_rows(): jnp.take(values, source_row, axis=0) * filled  6.33 us
  transfers between devices with their start and end apart: 9, of which 7 were waited for; matrix products, arithmetic and copies ran while one was open for 16% of the time, Pallas kernels for 0%

profile of v14, /device:TPU:1, one launch (start us, length us, event | category | flops | bytes accessed | tf_op | source)
XLA Modules:
  0.0 279.7 jit_solution(7870147629803167941)
XLA Ops:
  9.2 3.3 %collective-permute-start.1 = (bf16[3,80,384]{2,1,0:T(8,128)(2,1)S(1)}, bf16[3,80,384]{2,1,0:T(8,128)(2,1)S(1)}, u32[]{:S(2)}, u32[]{:S(2)}) collective-permute-start(bf16[3,80,384]{2,1,0:T(8,128)(2,1)S(1)} %pad_maximum_fusion.3), channel_id=1, source_target_pairs={{0,8},{8,0},{1,9},{9,1},{2,10},{10,2},{3,11},{11,3},{4,12},{12,4},... | collective-permute-start | bytes 552968 | tf_op jit(solution)/shard_map/ppermute | solution.py:25
  17.6 1.6 multiply_convert_fusion.1
  20.2 3.2 %gather_fusion.1 = bf16[320,2560]{1,0:T(8,128)(2,1)} fusion(bf16[256,2560]{1,0:T(8,128)(2,1)S(1)} %multiply_convert_fusion.1, s32[1024]{0:T(1024)S(1)} %pad_clamp_fusion.1), kind=kCustom, calls=%fused_computation.2.clone | custom fusion | bytes 3278080 | tf_op jit(solution)/shard_map/jit(_take)/gather | solution.py:87
  23.3 3.2 %gather_fusion = bf16[320,2560]{1,0:T(8,128)(2,1)} fusion(bf16[256,2560]{1,0:T(8,128)(2,1)S(1)} %copy-done, s32[1024]{0:T(1024)S(1)} %pad_clamp_fusion.1), kind=kCustom, calls=%fused_computation.clone | custom fusion | bytes 3278080 | tf_op jit(solution)/shard_map/jit(_take)/gather | solution.py:87
  26.5 2.2 scatter_custom_fusion.1
  28.7 1.8 select_multiply_fusion.1
  30.9 90.2 %all_to_all.15 = bf16[2,8,40,2560]{3,2,0,1:T(8,128)(2,1)S(1)} all-to-all(bf16[2,8,40,2560]{3,2,0,1:T(8,128)(2,1)S(1)} %pad_maximum_fusion.2), channel_id=1, replica_groups=mesh['x'=4,'zh'=4,'core'=2,'expert'=8] {'expert'}, dimensions={1} | all-to-all | bytes 6553600 | tf_op jit(solution)/shard_map/all_to_all | solution.py:93
  122.5 5.5 %collective-permute-done = bf16[2,320,2560]{2,1,0:T(8,128)(2,1)S(1)} collective-permute-done((bf16[2,320,2560]{2,1,0:T(8,128)(2,1)S(1)}, bf16[2,320,2560]{2,1,0:T(8,128)(2,1)S(1)}, u32[]{:S(2)}, u32[]{:S(2)}) %collective-permute-start) | collective-permute-done | bytes 3276832 | tf_op jit(solution)/shard_map/ppermute | solution.py:25
  128.0 1.7 copy-done.5
  129.7 1.8 fusion.4
  131.5 2.7 all-gather.2.cloned.1.call-done
  134.2 4.5 %fusion.10 = f32[640,384]{1,0:T(8,128)S(1)} fusion(bf16[640,2560]{1,0:T(8,128)(2,1)} %fusion.4, bf16[3,2560,384]{2,1,0:T(8,128)(2,1)} %all-gather.2.cloned.1.call-done), kind=kOutput, calls=%fused_computation.34 | convolution fusion | flops 1258291200 | bytes 6225920 | tf_op jit(solution)/shard_map/dot_general | solution.py:104
  139.4 1.9 fusion.9
  141.4 2.2 multiply_convert_fusion.2
  143.6 2.1 fusion
  145.7 2.1 fusion.1
  147.8 2.1 fusion.2
  149.9 3.4 %pad_maximum_fusion = bf16[3,2560,384]{2,1,0:T(8,128)(2,1)} fusion(bf16[1,2560,384]{2,1,0:T(8,128)(2,1)S(1)} %fusion.2, bf16[1,2560,384]{2,1,0:T(8,128)(2,1)S(1)} %fusion.1, bf16[1,2560,384]{2,1,0:T(8,128)(2,1)S(1)} %fusion), kind=kLoop, calls=%fused_computation.8 | loop fusion | flops 5898240 | bytes 11796480 | tf_op jit(solution)/shard_map/stack | solution.py:42
  154.3 3.5 %fusion.8 = f32[640,2560]{1,0:T(8,128)S(1)} fusion(bf16[640,384]{1,0:T(8,128)(2,1)S(1)} %copy-done.11, bf16[3,2560,384]{2,1,0:T(8,128)(2,1)} %all-gather.2.cloned.1.call-done), kind=kOutput, calls=%fused_computation.32 | convolution fusion | flops 1258291200 | bytes 9011200 | tf_op jit(solution)/shard_map/dot_general | solution.py:13
  157.8 3.5 %convolution_add_fusion = f32[640,2560]{1,0:T(8,128)S(1)} fusion(f32[640,2560]{1,0:T(8,128)S(1)} %fusion.8, bf16[640,384]{1,0:T(8,128)(2,1)S(1)} %copy-done.13, bf16[3,2560,384]{2,1,0:T(8,128)(2,1)} %all-gather.2.cloned.1.call-done), kind=kOutput, calls=%fused_computation.9 | convolution fusion | flops 1259929600 | bytes 15564800 | tf_op jit(solution)/shard_map/dot_general | solution.py:13
  162.0 3.1 %collective-permute-done.3 = bf16[320,2560]{1,0:T(8,128)(2,1)S(1)} collective-permute-done((bf16[320,2560]{1,0:T(8,128)(2,1)S(1)}, bf16[320,2560]{1,0:T(8,128)(2,1)S(1)}, u32[]{:S(2)}, u32[]{:S(2)}) %collective-permute-start.3) | collective-permute-done | bytes 1638432 | tf_op jit(solution)/shard_map/ppermute | solution.py:25
  165.2 1.8 fusion.5
  166.9 4.1 %all-to-all-start.2 = ((bf16[8,40,2560]{2,1,0:T(8,128)(2,1)}), bf16[8,40,2560]{2,1,0:T(8,128)(2,1)S(1)}, u32[]{:S(2)}, u32[]{:S(2)}) async-start(bf16[8,40,2560]{2,1,0:T(8,128)(2,1)} %bitcast.28), calls=%async_computation.2 | async-start | bytes 3276800 | tf_op jit(solution)/shard_map/all_to_all | solution.py:130
  171.1 3.5 %fusion.12 = f32[640,2560]{1,0:T(8,128)S(1)} fusion(bf16[640,384]{1,0:T(8,128)(2,1)S(1)} %copy-done.9, bf16[3,2560,384]{2,1,0:T(8,128)(2,1)} %all-gather.2.cloned.1.call-done), kind=kOutput, calls=%fused_computation.36 | convolution fusion | flops 1258291200 | bytes 9011200 | tf_op jit(solution)/shard_map/dot_general | solution.py:13
  175.4 3.1 %collective-permute-done.2 = bf16[320,2560]{1,0:T(8,128)(2,1)S(1)} collective-permute-done((bf16[320,2560]{1,0:T(8,128)(2,1)S(1)}, bf16[320,2560]{1,0:T(8,128)(2,1)S(1)}, u32[]{:S(2)}, u32[]{:S(2)}) %collective-permute-start.2) | collective-permute-done | bytes 1638432 | tf_op jit(solution)/shard_map/ppermute | solution.py:25
  180.2 46.2 %all-to-all-done.2 = bf16[8,40,2560]{2,1,0:T(8,128)(2,1)S(1)} async-done(((bf16[8,40,2560]{2,1,0:T(8,128)(2,1)}), bf16[8,40,2560]{2,1,0:T(8,128)(2,1)S(1)}, u32[]{:S(2)}, u32[]{:S(2)}) %all-to-all-start.2) | async-done | bytes 1638432 | tf_op jit(solution)/shard_map/all_to_all | solution.py:130
  226.4 4.1 %all-to-all-start.1 = ((bf16[8,40,2560]{2,1,0:T(8,128)(2,1)}), bf16[8,40,2560]{2,1,0:T(8,128)(2,1)S(1)}, u32[]{:S(2)}, u32[]{:S(2)}) async-start(bf16[8,40,2560]{2,1,0:T(8,128)(2,1)} %bitcast.83), calls=%async_computation.1 | async-start | bytes 3276800 | tf_op jit(solution)/shard_map/all_to_all | solution.py:121
  230.5 2.5 gather_fusion.3
  233.0 23.2 %all-to-all-done.1 = bf16[8,40,2560]{2,1,0:T(8,128)(2,1)S(1)} async-done(((bf16[8,40,2560]{2,1,0:T(8,128)(2,1)}), bf16[8,40,2560]{2,1,0:T(8,128)(2,1)S(1)}, u32[]{:S(2)}, u32[]{:S(2)}) %all-to-all-start.1) | async-done | bytes 1638432 | tf_op jit(solution)/shard_map/all_to_all | solution.py:121
  256.2 2.5 gather_fusion.2
  258.7 2.9 %multiply_convert_fusion = bf16[256,2560]{1,0:T(8,128)(2,1)} fusion(bf16[256,2560]{1,0:T(8,128)(2,1)} %gather_fusion.2, f32[256]{0:T(256)S(1)} %bitcast.93, pred[256]{0:T(512)(128)(4,1)S(1)} %get-tuple-element.7), kind=kLoop, calls=%fused_computation.27 | loop fusion | flops 2621440 | bytes 2622720 | tf_op jit(solution)/shard_map/convert_element_type | solution.py:124
  261.6 6.4 %reduce-scatter.2.cloned.1.call-done = bf16[3,160,384]{2,1,0:T(8,128)(2,1)} async-done(((bf16[3,2560,384]{2,1,0:T(8,128)(2,1)}), bf16[3,160,384]{2,1,0:T(8,128)(2,1)}) %reduce-scatter.2.cloned.1.call-update) | async-done | bytes 368656 | tf_op jit(solution)/shard_map/reduce_scatter | solution.py:43
  (69 shorter events, 19.5 us)
Async XLA Ops:
  7.2 16.2 %copy-start = (bf16[256,2560]{1,0:T(8,128)(2,1)S(1)}, bf16[256,2560]{1,0:T(8,128)(2,1)}, u32[]{:S(2)}) copy-start(bf16[256,2560]{1,0:T(8,128)(2,1)} %param.11) | copy-start | bytes 3932164
  7.2 127.0 %all-gather.2.cloned.1.call-start = ((), (), s32[]{:S(2)}) async-start(), calls=%async_computation.4 | async-start | bytes 6266880 | tf_op jit(solution)/shard_map/all_gather | solution.py:37
  9.2 10.0 %collective-permute-start.1 = (bf16[3,80,384]{2,1,0:T(8,128)(2,1)S(1)}, bf16[3,80,384]{2,1,0:T(8,128)(2,1)S(1)}, u32[]{:S(2)}, u32[]{:S(2)}) collective-permute-start(bf16[3,80,384]{2,1,0:T(8,128)(2,1)S(1)} %pad_maximum_fusion.3), channel_id=1, source_target_pairs={{0,8},{8,0},{1,9},{9,1},{2,10},{10,2},{3,11},{11,3},{4,12},{12,4},... | collective-permute-start | bytes 552968 | tf_op jit(solution)/shard_map/ppermute | solution.py:25
  20.1 248.0 %reduce-scatter.2.cloned.1.call-start = ((), (), s32[]{:S(2)}) async-start(), calls=%async_computation.5 | async-start | bytes 6266880 | tf_op jit(solution)/shard_map/reduce_scatter | solution.py:43
  23.3 5.3 %copy-start.2 = (bf16[320,2560]{1,0:T(8,128)(2,1)S(1)}, bf16[320,2560]{1,0:T(8,128)(2,1)}, u32[]{:S(2)}) copy-start(bf16[320,2560]{1,0:T(8,128)(2,1)} %gather_fusion.1) | copy-start | bytes 4915204
  121.3 6.7 %collective-permute-start = (bf16[2,320,2560]{2,1,0:T(8,128)(2,1)S(1)}, bf16[2,320,2560]{2,1,0:T(8,128)(2,1)S(1)}, u32[]{:S(2)}, u32[]{:S(2)}) collective-permute-start(bf16[2,320,2560]{2,1,0:T(8,128)(2,1)S(1)} %bitcast.79), channel_id=1, source_target_pairs={{0,8},{8,0},{1,9},{9,1},{2,10},{10,2},{3,11},{11,3},{4,12},{12,4},... | collective-permute-start | bytes 9830408 | tf_op jit(solution)/shard_map/ppermute | solution.py:25
  128.0 1.7 copy-start.5
  134.2 4.5 %copy-start.3 = (bf16[3,2560,384]{2,1,0:T(8,128)(2,1)S(1)}, bf16[3,2560,384]{2,1,0:T(8,128)(2,1)}, u32[]{:S(2)}) copy-start(bf16[3,2560,384]{2,1,0:T(8,128)(2,1)} %all-gather.2.cloned.1.call-done) | copy-start | bytes 17694724
  134.2 5.2 %copy-start.7 = (bf16[640,2560]{1,0:T(8,128)(2,1)S(1)}, bf16[640,2560]{1,0:T(8,128)(2,1)}, u32[]{:S(2)}) copy-start(bf16[640,2560]{1,0:T(8,128)(2,1)} %fusion.4) | copy-start | bytes 9830404
  139.4 1.9 copy-start.6
  143.5 2.1 copy-start.10
  143.5 2.1 copy-start.12
  143.5 4.2 %copy-start.8 = (bf16[640,384]{1,0:T(8,128)(2,1)}, bf16[640,384]{1,0:T(8,128)(2,1)S(1)}, u32[]{:S(2)}) copy-start(bf16[640,384]{1,0:T(8,128)(2,1)S(1)} %get-tuple-element.11) | copy-start | bytes 1474564
  153.3 1.0 copy-start.11
  154.3 3.5 %copy-start.13 = (bf16[640,384]{1,0:T(8,128)(2,1)S(1)}, bf16[640,384]{1,0:T(8,128)(2,1)}, u32[]{:S(2)}) copy-start(bf16[640,384]{1,0:T(8,128)(2,1)} %copy-done.12) | copy-start | bytes 1474564
  161.5 3.7 %collective-permute-start.3 = (bf16[320,2560]{1,0:T(8,128)(2,1)S(1)}, bf16[320,2560]{1,0:T(8,128)(2,1)S(1)}, u32[]{:S(2)}, u32[]{:S(2)}) collective-permute-start(bf16[320,2560]{1,0:T(8,128)(2,1)S(1)} %slice.183), channel_id=1, source_target_pairs={{0,8},{8,0},{1,9},{9,1},{2,10},{10,2},{3,11},{11,3},{4,12},{12,4},... | collective-permute-start | bytes 4915208 | tf_op jit(solution)/shard_map/ppermute | solution.py:25
  166.9 4.2 %copy-start.9 = (bf16[640,384]{1,0:T(8,128)(2,1)S(1)}, bf16[640,384]{1,0:T(8,128)(2,1)}, u32[]{:S(2)}) copy-start(bf16[640,384]{1,0:T(8,128)(2,1)} %copy-done.8) | copy-start | bytes 1474564
  166.9 59.5 %all-to-all-start.2 = ((bf16[8,40,2560]{2,1,0:T(8,128)(2,1)}), bf16[8,40,2560]{2,1,0:T(8,128)(2,1)S(1)}, u32[]{:S(2)}, u32[]{:S(2)}) async-start(bf16[8,40,2560]{2,1,0:T(8,128)(2,1)} %bitcast.28), calls=%async_computation.2 | async-start | bytes 3276800 | tf_op jit(solution)/shard_map/all_to_all | solution.py:130
  174.7 3.9 %collective-permute-start.2 = (bf16[320,2560]{1,0:T(8,128)(2,1)S(1)}, bf16[320,2560]{1,0:T(8,128)(2,1)S(1)}, u32[]{:S(2)}, u32[]{:S(2)}) collective-permute-start(bf16[320,2560]{1,0:T(8,128)(2,1)S(1)} %slice.184), channel_id=1, source_target_pairs={{0,8},{8,0},{1,9},{9,1},{2,10},{10,2},{3,11},{11,3},{4,12},{12,4},... | collective-permute-start | bytes 4915208 | tf_op jit(solution)/shard_map/ppermute | solution.py:25
  180.2 50.3 %copy-start.14 = (s32[256,1]{0,1:T(1,128)S(1)}, s32[256,1]{0,1:T(1,128)}, u32[]{:S(2)}) copy-start(s32[256,1]{0,1:T(1,128)} %param.12) | copy-start | bytes 3076
  226.4 29.8 %all-to-all-start.1 = ((bf16[8,40,2560]{2,1,0:T(8,128)(2,1)}), bf16[8,40,2560]{2,1,0:T(8,128)(2,1)S(1)}, u32[]{:S(2)}, u32[]{:S(2)}) async-start(bf16[8,40,2560]{2,1,0:T(8,128)(2,1)} %bitcast.83), calls=%async_computation.1 | async-start | bytes 3276800 | tf_op jit(solution)/shard_map/all_to_all | solution.py:121
  258.7 10.8 %copy-start.4 = (bf16[256,2560]{1,0:T(8,128)(2,1)S(1)}, bf16[256,2560]{1,0:T(8,128)(2,1)}, u32[]{:S(2)}) copy-start(bf16[256,2560]{1,0:T(8,128)(2,1)} %gather_fusion.3) | copy-start | bytes 3932164
  258.7 14.1 %copy-start.1 = (bf16[256,2560]{1,0:T(8,128)(2,1)S(1)}, bf16[256,2560]{1,0:T(8,128)(2,1)}, u32[]{:S(2)}) copy-start(bf16[256,2560]{1,0:T(8,128)(2,1)} %param.11) | copy-start | bytes 3932164
  268.1 3.8 %collective-permute-start.4 = (bf16[3,160,384]{2,1,0:T(8,128)(2,1)}, bf16[3,160,384]{2,1,0:T(8,128)(2,1)S(1)}, u32[]{:S(2)}, u32[]{:S(2)}) collective-permute-start(bf16[3,160,384]{2,1,0:T(8,128)(2,1)} %reduce-scatter.2.cloned.1.call-done), channel_id=1, source_target_pairs={{0,8},{8,0},{1,9},{9,1},{2,10},{10,2},{3,11},{11,3},{4,12},{12,4},... | collective-permute-start | bytes 1105928 | tf_op jit(solution)/shard_map/ppermute | solution.py:25
Sparse Core Ops, SparseCore 0:
  20.2 113.9 all-gather.1
  153.5 114.5 reduce-scatter.1

commit v15 on v14

--- a/solution.py
+++ b/solution.py
@@ -48,7 +48,8 @@
         return jnp.where(first, value[:, :rows], value[:, rows:]).astype(jnp.float32)
 
     mine = my_rows(chip_sum)
-    theirs = my_rows(swap_cores(chip_sum))
+    sent = jnp.where(first, chip_sum[:, rows:], chip_sum[:, :rows])
+    theirs = swap_cores(sent).astype(jnp.float32)
     block = jnp.where(
         first, jnp.concatenate([mine, theirs], axis=2), jnp.concatenate([theirs, mine], axis=2)
     )

time: 281 us -> 280 us (level)
  transfers between devices with their start and end apart: 9 -> 9, of which waited for: 7 -> 7; matrix products, arithmetic and copies ran while one was open for 16% -> 14% of each run, Pallas kernels for 0% -> 0%
where the time goes in v15:
time: 280 us
  waiting for transfers between devices  92.7 us (33%)
  blocking collectives  90.2 us (32%)
  matrix products  25.2 us (9%)
  other arithmetic  22.4 us (8%)
  local copies, waits for them, and re-layouts  19.1 us (7%)
  starting transfers between devices  16.4 us (6%)
  between operations  14.4 us (5%)
    all_to_all x1, blocking collectives, shards(): lax.all_to_all(jnp.stack([pack_rows(tokens), pack_rows(out_grad)]), 'expe...  90.2 us
    all_to_all x1, waiting for transfers between devices, shards(): lax.all_to_all(token_grad.reshape(experts, capacity, model_width), 'exper...  46.3 us
    all_to_all x1, waiting for transfers between devices, shards(): lax.all_to_all(expert_out, 'expert', split_axis=0, concat_axis=0, tiled=T...  23.9 us
    ppermute x5, waiting for transfers between devices, swap_cores(): return lax.ppermute(value, 'core', perm=[(0, 1), (1, 0)])  11.7 us
    dot_general x3, matrix products, contract_last(): lax.dot_general(matrix_a, matrix_b, (((1,), (1,)), ((), ())), preferred_e...  10.4 us
    ppermute x5, starting transfers between devices, swap_cores(): return lax.ppermute(value, 'core', perm=[(0, 1), (1, 0)])  8.25 us
    reduce_scatter x1, waiting for transfers between devices, scatter_grads(): chip_sum = lax.psum_scatter(stacked, CHIPS, scatter_dimension=1, tiled=True)  8.08 us
    gather x2, local copies, waits for them, and re-layouts, pack_rows(): jnp.take(values, source_row, axis=0) * filled  6.36 us
  transfers between devices with their start and end apart: 9, of which 7 were waited for; matrix products, arithmetic and copies ran while one was open for 14% of the time, Pallas kernels for 0%

profile of v15, /device:TPU:1, one launch (start us, length us, event | category | flops | bytes accessed | tf_op | source)
XLA Modules:
  0.0 280.4 jit_solution(13304889179467214032)
XLA Ops:
  9.2 3.3 %collective-permute-start.1 = (bf16[3,80,384]{2,1,0:T(8,128)(2,1)S(1)}, bf16[3,80,384]{2,1,0:T(8,128)(2,1)S(1)}, u32[]{:S(2)}, u32[]{:S(2)}) collective-permute-start(bf16[3,80,384]{2,1,0:T(8,128)(2,1)S(1)} %pad_maximum_fusion.3), channel_id=1, source_target_pairs={{0,8},{8,0},{1,9},{9,1},{2,10},{10,2},{3,11},{11,3},{4,12},{12,4},... | collective-permute-start | bytes 552968 | tf_op jit(solution)/shard_map/ppermute | solution.py:25
  17.6 1.6 multiply_convert_fusion.1
  20.2 3.2 %gather_fusion.1 = bf16[320,2560]{1,0:T(8,128)(2,1)} fusion(bf16[256,2560]{1,0:T(8,128)(2,1)S(1)} %multiply_convert_fusion.1, s32[1024]{0:T(1024)S(1)} %pad_clamp_fusion.1), kind=kCustom, calls=%fused_computation.2.clone | custom fusion | bytes 3278080 | tf_op jit(solution)/shard_map/jit(_take)/gather | solution.py:88
  23.4 3.2 %gather_fusion = bf16[320,2560]{1,0:T(8,128)(2,1)} fusion(bf16[256,2560]{1,0:T(8,128)(2,1)S(1)} %copy-done, s32[1024]{0:T(1024)S(1)} %pad_clamp_fusion.1), kind=kCustom, calls=%fused_computation.clone | custom fusion | bytes 3278080 | tf_op jit(solution)/shard_map/jit(_take)/gather | solution.py:88
  26.5 2.2 scatter_custom_fusion.1
  28.7 1.8 select_multiply_fusion.1
  30.9 90.2 %all_to_all.15 = bf16[2,8,40,2560]{3,2,0,1:T(8,128)(2,1)S(1)} all-to-all(bf16[2,8,40,2560]{3,2,0,1:T(8,128)(2,1)S(1)} %pad_maximum_fusion.2), channel_id=1, replica_groups=mesh['x'=4,'zh'=4,'core'=2,'expert'=8] {'expert'}, dimensions={1} | all-to-all | bytes 6553600 | tf_op jit(solution)/shard_map/all_to_all | solution.py:94
  122.6 5.5 %collective-permute-done = bf16[2,320,2560]{2,1,0:T(8,128)(2,1)S(1)} collective-permute-done((bf16[2,320,2560]{2,1,0:T(8,128)(2,1)S(1)}, bf16[2,320,2560]{2,1,0:T(8,128)(2,1)S(1)}, u32[]{:S(2)}, u32[]{:S(2)}) %collective-permute-start) | collective-permute-done | bytes 3276832 | tf_op jit(solution)/shard_map/ppermute | solution.py:25
  128.0 1.7 copy-done.5
  129.8 1.8 fusion.4
  131.6 2.6 all-gather.2.cloned.1.call-done
  134.2 4.5 %fusion.10 = f32[640,384]{1,0:T(8,128)S(1)} fusion(bf16[640,2560]{1,0:T(8,128)(2,1)} %fusion.4, bf16[3,2560,384]{2,1,0:T(8,128)(2,1)} %all-gather.2.cloned.1.call-done), kind=kOutput, calls=%fused_computation.34 | convolution fusion | flops 1258291200 | bytes 6225920 | tf_op jit(solution)/shard_map/dot_general | solution.py:105
  139.4 1.9 fusion.9
  141.4 2.2 multiply_convert_fusion.2
  143.6 2.1 fusion
  145.7 2.1 fusion.1
  147.8 2.1 fusion.2
  149.9 3.3 %pad_maximum_fusion = bf16[3,2560,384]{2,1,0:T(8,128)(2,1)} fusion(bf16[1,2560,384]{2,1,0:T(8,128)(2,1)S(1)} %fusion.2, bf16[1,2560,384]{2,1,0:T(8,128)(2,1)S(1)} %fusion.1, bf16[1,2560,384]{2,1,0:T(8,128)(2,1)S(1)} %fusion), kind=kLoop, calls=%fused_computation.8 | loop fusion | flops 5898240 | bytes 11796480 | tf_op jit(solution)/shard_map/stack | solution.py:42
  154.2 3.5 %fusion.8 = f32[640,2560]{1,0:T(8,128)S(1)} fusion(bf16[640,384]{1,0:T(8,128)(2,1)S(1)} %copy-done.11, bf16[3,2560,384]{2,1,0:T(8,128)(2,1)} %all-gather.2.cloned.1.call-done), kind=kOutput, calls=%fused_computation.32 | convolution fusion | flops 1258291200 | bytes 9011200 | tf_op jit(solution)/shard_map/dot_general | solution.py:13
  157.7 3.5 %convolution_add_fusion = f32[640,2560]{1,0:T(8,128)S(1)} fusion(f32[640,2560]{1,0:T(8,128)S(1)} %fusion.8, bf16[640,384]{1,0:T(8,128)(2,1)S(1)} %copy-done.13, bf16[3,2560,384]{2,1,0:T(8,128)(2,1)} %all-gather.2.cloned.1.call-done), kind=kOutput, calls=%fused_computation.9 | convolution fusion | flops 1259929600 | bytes 15564800 | tf_op jit(solution)/shard_map/dot_general | solution.py:13
  161.9 3.1 %collective-permute-done.3 = bf16[320,2560]{1,0:T(8,128)(2,1)S(1)} collective-permute-done((bf16[320,2560]{1,0:T(8,128)(2,1)S(1)}, bf16[320,2560]{1,0:T(8,128)(2,1)S(1)}, u32[]{:S(2)}, u32[]{:S(2)}) %collective-permute-start.3) | collective-permute-done | bytes 1638432 | tf_op jit(solution)/shard_map/ppermute | solution.py:25
  165.1 1.8 fusion.5
  166.8 4.1 %all-to-all-start.2 = ((bf16[8,40,2560]{2,1,0:T(8,128)(2,1)}), bf16[8,40,2560]{2,1,0:T(8,128)(2,1)S(1)}, u32[]{:S(2)}, u32[]{:S(2)}) async-start(bf16[8,40,2560]{2,1,0:T(8,128)(2,1)} %bitcast.28), calls=%async_computation.2 | async-start | bytes 3276800 | tf_op jit(solution)/shard_map/all_to_all | solution.py:131
  171.0 3.5 %fusion.12 = f32[640,2560]{1,0:T(8,128)S(1)} fusion(bf16[640,384]{1,0:T(8,128)(2,1)S(1)} %copy-done.9, bf16[3,2560,384]{2,1,0:T(8,128)(2,1)} %all-gather.2.cloned.1.call-done), kind=kOutput, calls=%fused_computation.36 | convolution fusion | flops 1258291200 | bytes 9011200 | tf_op jit(solution)/shard_map/dot_general | solution.py:13
  175.3 3.1 %collective-permute-done.2 = bf16[320,2560]{1,0:T(8,128)(2,1)S(1)} collective-permute-done((bf16[320,2560]{1,0:T(8,128)(2,1)S(1)}, bf16[320,2560]{1,0:T(8,128)(2,1)S(1)}, u32[]{:S(2)}, u32[]{:S(2)}) %collective-permute-start.2) | collective-permute-done | bytes 1638432 | tf_op jit(solution)/shard_map/ppermute | solution.py:25
  178.5 1.6 fusion.7
  180.1 46.3 %all-to-all-done.2 = bf16[8,40,2560]{2,1,0:T(8,128)(2,1)S(1)} async-done(((bf16[8,40,2560]{2,1,0:T(8,128)(2,1)}), bf16[8,40,2560]{2,1,0:T(8,128)(2,1)S(1)}, u32[]{:S(2)}, u32[]{:S(2)}) %all-to-all-start.2) | async-done | bytes 1638432 | tf_op jit(solution)/shard_map/all_to_all | solution.py:131
  226.4 3.9 %all-to-all-start.1 = ((bf16[8,40,2560]{2,1,0:T(8,128)(2,1)}), bf16[8,40,2560]{2,1,0:T(8,128)(2,1)S(1)}, u32[]{:S(2)}, u32[]{:S(2)}) async-start(bf16[8,40,2560]{2,1,0:T(8,128)(2,1)} %bitcast.83), calls=%async_computation.1 | async-start | bytes 3276800 | tf_op jit(solution)/shard_map/all_to_all | solution.py:122
  230.4 2.5 gather_fusion.3
  232.9 23.9 %all-to-all-done.1 = bf16[8,40,2560]{2,1,0:T(8,128)(2,1)S(1)} async-done(((bf16[8,40,2560]{2,1,0:T(8,128)(2,1)}), bf16[8,40,2560]{2,1,0:T(8,128)(2,1)S(1)}, u32[]{:S(2)}, u32[]{:S(2)}) %all-to-all-start.1) | async-done | bytes 1638432 | tf_op jit(solution)/shard_map/all_to_all | solution.py:122
  259.6 8.1 %reduce-scatter.2.cloned.1.call-done = bf16[3,160,384]{2,1,0:T(8,128)(2,1)} async-done(((bf16[3,2560,384]{2,1,0:T(8,128)(2,1)}), bf16[3,160,384]{2,1,0:T(8,128)(2,1)}) %reduce-scatter.2.cloned.1.call-update) | async-done | bytes 368656 | tf_op jit(solution)/shard_map/reduce_scatter | solution.py:43
  268.9 2.4 collective-permute-start.4
  (69 shorter events, 19.4 us)
Async XLA Ops:
  7.2 16.2 %copy-start = (bf16[256,2560]{1,0:T(8,128)(2,1)S(1)}, bf16[256,2560]{1,0:T(8,128)(2,1)}, u32[]{:S(2)}) copy-start(bf16[256,2560]{1,0:T(8,128)(2,1)} %param.11) | copy-start | bytes 3932164
  7.2 127.0 %all-gather.2.cloned.1.call-start = ((), (), s32[]{:S(2)}) async-start(), calls=%async_computation.4 | async-start | bytes 6266880 | tf_op jit(solution)/shard_map/all_gather | solution.py:37
  9.2 10.0 %collective-permute-start.1 = (bf16[3,80,384]{2,1,0:T(8,128)(2,1)S(1)}, bf16[3,80,384]{2,1,0:T(8,128)(2,1)S(1)}, u32[]{:S(2)}, u32[]{:S(2)}) collective-permute-start(bf16[3,80,384]{2,1,0:T(8,128)(2,1)S(1)} %pad_maximum_fusion.3), channel_id=1, source_target_pairs={{0,8},{8,0},{1,9},{9,1},{2,10},{10,2},{3,11},{11,3},{4,12},{12,4},... | collective-permute-start | bytes 552968 | tf_op jit(solution)/shard_map/ppermute | solution.py:25
  20.1 247.6 %reduce-scatter.2.cloned.1.call-start = ((), (), s32[]{:S(2)}) async-start(), calls=%async_computation.5 | async-start | bytes 6266880 | tf_op jit(solution)/shard_map/reduce_scatter | solution.py:43
  23.4 5.4 %copy-start.2 = (bf16[320,2560]{1,0:T(8,128)(2,1)S(1)}, bf16[320,2560]{1,0:T(8,128)(2,1)}, u32[]{:S(2)}) copy-start(bf16[320,2560]{1,0:T(8,128)(2,1)} %gather_fusion.1) | copy-start | bytes 4915204
  121.3 6.7 %collective-permute-start = (bf16[2,320,2560]{2,1,0:T(8,128)(2,1)S(1)}, bf16[2,320,2560]{2,1,0:T(8,128)(2,1)S(1)}, u32[]{:S(2)}, u32[]{:S(2)}) collective-permute-start(bf16[2,320,2560]{2,1,0:T(8,128)(2,1)S(1)} %bitcast.79), channel_id=1, source_target_pairs={{0,8},{8,0},{1,9},{9,1},{2,10},{10,2},{3,11},{11,3},{4,12},{12,4},... | collective-permute-start | bytes 9830408 | tf_op jit(solution)/shard_map/ppermute | solution.py:25
  128.0 1.7 copy-start.5
  134.2 4.5 %copy-start.3 = (bf16[3,2560,384]{2,1,0:T(8,128)(2,1)S(1)}, bf16[3,2560,384]{2,1,0:T(8,128)(2,1)}, u32[]{:S(2)}) copy-start(bf16[3,2560,384]{2,1,0:T(8,128)(2,1)} %all-gather.2.cloned.1.call-done) | copy-start | bytes 17694724
  134.2 5.2 %copy-start.7 = (bf16[640,2560]{1,0:T(8,128)(2,1)S(1)}, bf16[640,2560]{1,0:T(8,128)(2,1)}, u32[]{:S(2)}) copy-start(bf16[640,2560]{1,0:T(8,128)(2,1)} %fusion.4) | copy-start | bytes 9830404
  139.4 1.9 copy-start.6
  143.5 2.1 copy-start.10
  143.5 2.1 copy-start.12
  143.6 4.2 %copy-start.8 = (bf16[640,384]{1,0:T(8,128)(2,1)}, bf16[640,384]{1,0:T(8,128)(2,1)S(1)}, u32[]{:S(2)}) copy-start(bf16[640,384]{1,0:T(8,128)(2,1)S(1)} %get-tuple-element.11) | copy-start | bytes 1474564
  153.2 1.0 copy-start.11
  154.2 3.5 %copy-start.13 = (bf16[640,384]{1,0:T(8,128)(2,1)S(1)}, bf16[640,384]{1,0:T(8,128)(2,1)}, u32[]{:S(2)}) copy-start(bf16[640,384]{1,0:T(8,128)(2,1)} %copy-done.12) | copy-start | bytes 1474564
  161.4 3.7 %collective-permute-start.3 = (bf16[320,2560]{1,0:T(8,128)(2,1)S(1)}, bf16[320,2560]{1,0:T(8,128)(2,1)S(1)}, u32[]{:S(2)}, u32[]{:S(2)}) collective-permute-start(bf16[320,2560]{1,0:T(8,128)(2,1)S(1)} %slice.171), channel_id=1, source_target_pairs={{0,8},{8,0},{1,9},{9,1},{2,10},{10,2},{3,11},{11,3},{4,12},{12,4},... | collective-permute-start | bytes 4915208 | tf_op jit(solution)/shard_map/ppermute | solution.py:25
  166.8 4.1 %copy-start.9 = (bf16[640,384]{1,0:T(8,128)(2,1)S(1)}, bf16[640,384]{1,0:T(8,128)(2,1)}, u32[]{:S(2)}) copy-start(bf16[640,384]{1,0:T(8,128)(2,1)} %copy-done.8) | copy-start | bytes 1474564
  166.8 59.6 %all-to-all-start.2 = ((bf16[8,40,2560]{2,1,0:T(8,128)(2,1)}), bf16[8,40,2560]{2,1,0:T(8,128)(2,1)S(1)}, u32[]{:S(2)}, u32[]{:S(2)}) async-start(bf16[8,40,2560]{2,1,0:T(8,128)(2,1)} %bitcast.28), calls=%async_computation.2 | async-start | bytes 3276800 | tf_op jit(solution)/shard_map/all_to_all | solution.py:131
  174.6 3.9 %collective-permute-start.2 = (bf16[320,2560]{1,0:T(8,128)(2,1)S(1)}, bf16[320,2560]{1,0:T(8,128)(2,1)S(1)}, u32[]{:S(2)}, u32[]{:S(2)}) collective-permute-start(bf16[320,2560]{1,0:T(8,128)(2,1)S(1)} %slice.172), channel_id=1, source_target_pairs={{0,8},{8,0},{1,9},{9,1},{2,10},{10,2},{3,11},{11,3},{4,12},{12,4},... | collective-permute-start | bytes 4915208 | tf_op jit(solution)/shard_map/ppermute | solution.py:25
  180.1 50.3 %copy-start.14 = (s32[256,1]{0,1:T(1,128)S(1)}, s32[256,1]{0,1:T(1,128)}, u32[]{:S(2)}) copy-start(s32[256,1]{0,1:T(1,128)} %param.12) | copy-start | bytes 3076
  226.4 30.3 %all-to-all-start.1 = ((bf16[8,40,2560]{2,1,0:T(8,128)(2,1)}), bf16[8,40,2560]{2,1,0:T(8,128)(2,1)S(1)}, u32[]{:S(2)}, u32[]{:S(2)}) async-start(bf16[8,40,2560]{2,1,0:T(8,128)(2,1)} %bitcast.83), calls=%async_computation.1 | async-start | bytes 3276800 | tf_op jit(solution)/shard_map/all_to_all | solution.py:122
  258.2 13.1 %copy-start.4 = (bf16[256,2560]{1,0:T(8,128)(2,1)S(1)}, bf16[256,2560]{1,0:T(8,128)(2,1)}, u32[]{:S(2)}) copy-start(bf16[256,2560]{1,0:T(8,128)(2,1)} %gather_fusion.3) | copy-start | bytes 3932164
  267.7 5.8 %copy-start.1 = (bf16[256,2560]{1,0:T(8,128)(2,1)S(1)}, bf16[256,2560]{1,0:T(8,128)(2,1)}, u32[]{:S(2)}) copy-start(bf16[256,2560]{1,0:T(8,128)(2,1)} %param.11) | copy-start | bytes 3932164
  268.9 3.7 %collective-permute-start.4 = (bf16[3,80,384]{2,1,0:T(8,128)(2,1)S(1)}, bf16[3,80,384]{2,1,0:T(8,128)(2,1)S(1)}, u32[]{:S(2)}, u32[]{:S(2)}) collective-permute-start(bf16[3,80,384]{2,1,0:T(8,128)(2,1)S(1)} %get-tuple-element.16), channel_id=1, source_target_pairs={{0,8},{8,0},{1,9},{9,1},{2,10},{10,2},{3,11},{11,3},{4,12},{12,4},... | collective-permute-start | bytes 552968 | tf_op jit(solution)/shard_map/ppermute | solution.py:25
Sparse Core Ops, SparseCore 0:
  20.2 113.9 all-gather.1
  153.3 114.3 reduce-scatter.1
